TPU v7x, 256 devices: a whole 4x4x8 slice. The times are simulated.
256 devices in a mesh: sample: 16 (over y, x_hi, core), filter: 16 (over x_lo, z).
Axes of the slice: x: 4 (x_hi: 2, x_lo: 2; x = x_hi * 2 + x_lo), y: 4, z: 8, core: 2. Of those that a mesh axis runs over, the one named last changes fastest.
Arguments:
- activations: bfloat16 [16, 2, 128, 2048], P('sample', None, None, 'filter'), may hold values from -18 to 18
- cotangent: bfloat16 [16, 2, 128, 2048], P('sample', None, None, 'filter'), may hold values from -2.5 to 2.5
- master_first: float32 [9, 2048, 2048], P(None, 'sample', 'filter'), may hold values from -0.046875 to 0.046875
- moment_first: float32 [9, 2048, 2048], P(None, 'sample', 'filter'), may hold values from -6 to 6
- second_first: float32 [9, 2048, 2048], P(None, 'sample', 'filter'), may hold values from 0.05 to 1
- master_second: float32 [9, 2048, 2048], P(None, 'sample', 'filter'), may hold values from -0.046875 to 0.046875
- moment_second: float32 [9, 2048, 2048], P(None, 'sample', 'filter'), may hold values from -6 to 6
- second_second: float32 [9, 2048, 2048], P(None, 'sample', 'filter'), may hold values from 0.05 to 1
Outputs:
- level_out: bfloat16 [16, 2, 128, 2048], P('sample', None, None, 'filter')
- input_grad: bfloat16 [16, 2, 128, 2048], P('sample', None, None, 'filter')
- new_master_first: float32 [9, 2048, 2048], P(None, 'sample', 'filter')
- new_moment_first: float32 [9, 2048, 2048], P(None, 'sample', 'filter')
- new_second_first: float32 [9, 2048, 2048], P(None, 'sample', 'filter')
- new_master_second: float32 [9, 2048, 2048], P(None, 'sample', 'filter')
- new_moment_second: float32 [9, 2048, 2048], P(None, 'sample', 'filter')
- new_second_second: float32 [9, 2048, 2048], P(None, 'sample', 'filter')
All inputs are finite; a program needn't handle non-finite values.
Results may differ from a plain program's by a relative error of at most 0.017.
Values may be sent and summed in bfloat16 or wider, within the bound.
No kernel may reach another device: no remote copies, remote signals or barrier semaphores. Data moves between devices by JAX's collectives and lax.ppermute only.
A program may use at most 128 MiB of HBM per device.

v0:
```python
import jax
import jax.numpy as jnp
from jax import lax
from jax.sharding import PartitionSpec as P

GROUP = 64


NORM_EPS = 1e-05
LEARN_RATE = 0.001
BETA_ONE = 0.9
BETA_TWO = 0.999
ADAM_EPS = 1e-08
CORRECT_ONE = 1.0 - 0.9**10
CORRECT_TWO = 1.0 - 0.999**10


def pad_slab(field):
    return jnp.pad(field, ((0, 0), (1, 1), (1, 1), (0, 0)))


def window(padded, row_start, column_start, height, breadth):
    return padded[:, row_start : row_start + height, column_start : column_start + breadth, :]


def conv_forward(source, weight):
    samples, height, breadth, depth_in = source.shape
    padded = pad_slab(source)
    summed = jnp.zeros((samples * height * breadth, weight.shape[2]), jnp.float32)
    for kernel_tap in range(9):
        shifted = window(padded, kernel_tap // 3, kernel_tap % 3, height, breadth)
        summed = summed + jnp.dot(
            shifted.reshape(samples * height * breadth, depth_in),
            weight[kernel_tap],
            preferred_element_type=jnp.float32,
        )
    return summed.reshape(samples, height, breadth, weight.shape[2])


def group_silu(pre_act):
    samples, height, breadth, depth_all = pre_act.shape
    grouped = pre_act.reshape(samples, height, breadth, depth_all // GROUP, GROUP)
    center = jnp.mean(grouped, axis=(1, 2, 4), keepdims=True)
    deviation = grouped - center
    spread = jnp.mean(deviation * deviation, axis=(1, 2, 4), keepdims=True)
    return jax.nn.silu(deviation * lax.rsqrt(spread + NORM_EPS)).reshape(pre_act.shape)


def tap_grads(source, upstream):
    samples, height, breadth, depth_in = source.shape
    padded = pad_slab(source)
    flat_up = upstream.reshape(samples, height * breadth, upstream.shape[3])
    results = []
    for kernel_tap in range(9):
        shifted = window(padded, kernel_tap // 3, kernel_tap % 3, height, breadth).reshape(
            samples, height * breadth, depth_in
        )
        results.append(
            lax.dot_general(
                shifted, flat_up, (((1,), (1,)), ((0,), (0,))), preferred_element_type=jnp.float32
            ).astype(jnp.bfloat16)
        )
    return jnp.stack(results, axis=1)


def adam_update(master, moment, second, gradient):
    moment_new = BETA_ONE * moment + (1.0 - BETA_ONE) * gradient
    second_new = BETA_TWO * second + (1.0 - BETA_TWO) * gradient * gradient
    step_size = moment_new / CORRECT_ONE / (jnp.sqrt(second_new / CORRECT_TWO) + ADAM_EPS)
    return (master - LEARN_RATE * step_size, moment_new, second_new)


def full_weight(master):
    return lax.all_gather(master.astype(jnp.bfloat16), "sample", axis=1, tiled=True)


def keep_panels(source):
    return lax.all_gather(source, "filter", axis=3, tiled=True)


def data_grad(upstream, weight):
    samples, height, breadth, depth_out = upstream.shape
    cell_count = samples * height * breadth
    padded = pad_slab(upstream)
    shifted_all = [
        window(padded, 2 - kernel_tap // 3, 2 - kernel_tap % 3, height, breadth).reshape(
            cell_count, depth_out
        )
        for kernel_tap in range(9)
    ]
    local_rows = weight.shape[1] // lax.axis_size("filter")
    summed = jnp.zeros((local_rows * lax.axis_size("filter"), cell_count), jnp.float32)
    for kernel_tap in range(9):
        summed = summed + lax.dot_general(
            weight[kernel_tap],
            shifted_all[kernel_tap],
            (((1,), (1,)), ((), ())),
            preferred_element_type=jnp.float32,
        )
    own_rows = lax.psum_scatter(
        summed.astype(jnp.bfloat16), "filter", scatter_dimension=0, tiled=True
    ).astype(jnp.float32)
    return own_rows.T.reshape(samples, height, breadth, local_rows)


def filter_grad(whole, upstream):
    partial_sum = tap_grads(whole, upstream)[0].astype(jnp.float32)
    return lax.psum_scatter(
        partial_sum.astype(jnp.bfloat16), "sample", scatter_dimension=1, tiled=True
    ).astype(jnp.float32)


def per_device(
    activations,
    cotangent,
    master_first,
    moment_first,
    second_first,
    master_second,
    moment_second,
    second_second,
):
    weight_first = full_weight(master_first)
    weight_second = full_weight(master_second)
    whole_input = keep_panels(activations)
    pre_first = conv_forward(whole_input, weight_first)
    hidden = group_silu(pre_first).astype(jnp.bfloat16)
    whole_hidden = keep_panels(hidden)
    pre_second = conv_forward(whole_hidden, weight_second)
    level_out = (activations.astype(jnp.float32) + pre_second).astype(jnp.bfloat16)
    hidden_grad = data_grad(cotangent, weight_second)
    _, pullback = jax.vjp(group_silu, pre_first)
    pre_grad = pullback(hidden_grad)[0].astype(jnp.bfloat16)
    input_grad = (cotangent.astype(jnp.float32) + data_grad(pre_grad, weight_first)).astype(
        jnp.bfloat16
    )
    grad_second = filter_grad(whole_hidden, cotangent)
    grad_first = filter_grad(whole_input, pre_grad)
    new_master_first, new_moment_first, new_second_first = adam_update(
        master_first, moment_first, second_first, grad_first
    )
    new_master_second, new_moment_second, new_second_second = adam_update(
        master_second, moment_second, second_second, grad_second
    )
    return (
        level_out,
        input_grad,
        new_master_first,
        new_moment_first,
        new_second_first,
        new_master_second,
        new_moment_second,
        new_second_second,
    )


def solution(mesh):
    placed = (
        P("sample", None, None, "filter"),
        P("sample", None, None, "filter"),
        P(None, "sample", "filter"),
        P(None, "sample", "filter"),
        P(None, "sample", "filter"),
        P(None, "sample", "filter"),
        P(None, "sample", "filter"),
        P(None, "sample", "filter"),
    )
    return jax.shard_map(
        per_device,
        mesh=mesh,
        in_specs=placed,
        out_specs=(
            P("sample", None, None, "filter"),
            P("sample", None, None, "filter"),
            P(None, "sample", "filter"),
            P(None, "sample", "filter"),
            P(None, "sample", "filter"),
            P(None, "sample", "filter"),
            P(None, "sample", "filter"),
            P(None, "sample", "filter"),
        ),
        check_vma=False,
    )
```

profile of v0, /device:TPU:6, one launch (start us, length us, event | category | flops | bytes accessed | tf_op | source)
XLA Modules:
  0.0 661.5 jit_solution(3601517996749550026)
XLA Ops:
  7.9 1.8 convert_element_type.155
  9.8 67.2 %all-gather.5.cloned.1.call-done = bf16[1,2,128,2048]{3,2,1,0:T(8,128)(2,1)} async-done(((bf16[1,2,128,128]{3,2,1,0:T(8,128)(2,1)}), bf16[1,2,128,2048]{3,2,1,0:T(8,128)(2,1)}) %all-gather.5.cloned.1.call-update) | async-done | bytes 1048592 | tf_op jit(solution)/shard_map/all_gather | solution.py:78
  77.1 5.0 pad_slice_fusion.8
  82.1 58.6 %all-gather.7.cloned.1.call-done = bf16[9,2048,128]{2,1,0:T(8,128)(2,1)} async-done(((bf16[9,128,128]{2,1,0:T(8,128)(2,1)}), bf16[9,2048,128]{2,1,0:T(8,128)(2,1)}) %all-gather.7.cloned.1.call-update) | async-done | bytes 4718608 | tf_op jit(solution)/shard_map/all_gather | solution.py:74
  140.7 1.9 fusion.67
  142.6 2.3 convolution_add_fusion.27
  145.0 1.8 convolution_add_fusion.26
  146.8 1.7 convolution_add_fusion.25
  152.4 68.0 %all-gather.9.cloned.1.call-done = bf16[1,2,128,2048]{2,3,1,0:T(8,128)(2,1)} async-done(((bf16[1,2,128,128]{2,3,1,0:T(8,128)(2,1)}), bf16[1,2,128,2048]{2,3,1,0:T(8,128)(2,1)}) %all-gather.9.cloned.1.call-update) | async-done | bytes 1048592 | tf_op jit(solution)/shard_map/all_gather | solution.py:78
  220.4 1.6 fusion.52
  222.0 1.6 fusion.50
  223.6 1.6 fusion.48
  228.8 2.1 copy-done.9
  231.0 87.3 %reduce-scatter.11.cloned.1.call-done = bf16[9,128,128]{2,1,0:T(8,128)(2,1)} async-done(((bf16[9,2048,128]{2,1,0:T(8,128)(2,1)}), bf16[9,128,128]{2,1,0:T(8,128)(2,1)}) %reduce-scatter.11.cloned.1.call-update) | async-done | bytes 294928 | tf_op jit(solution)/shard_map/reduce_scatter | solution.py:108
  318.3 3.3 multiply_subtract_fusion
  322.6 59.8 %all-gather.11.cloned.1.call-done = bf16[9,2048,128]{2,1,0:T(8,128)(2,1)} async-done(((bf16[9,128,128]{2,1,0:T(8,128)(2,1)}), bf16[9,2048,128]{2,1,0:T(8,128)(2,1)}) %all-gather.11.cloned.1.call-update) | async-done | bytes 4718608 | tf_op jit(solution)/shard_map/all_gather | solution.py:74
  382.4 1.7 fusion.68
  384.0 1.5 convolution_bitcast_fusion.1
  388.3 1.6 fusion.6
  389.9 2.3 copy.67
  392.3 71.3 %reduce-scatter.13.cloned.1.call-done = bf16[128,256]{1,0:T(8,128)(2,1)} async-done(((bf16[2048,256]{1,0:T(8,128)(2,1)}), bf16[128,256]{1,0:T(8,128)(2,1)}) %reduce-scatter.13.cloned.1.call-update) | async-done | bytes 65552
  463.6 0.9 copy.68
  468.4 2.5 fusion.18
  470.9 1.7 copy.54
  472.5 1.1 fusion.76
  474.4 1.6 copy.56
  476.0 1.6 copy.57
  477.6 1.6 copy.58
  480.1 1.0 copy.62
  481.1 1.0 copy.63
  482.1 1.7 fusion.66
  483.8 1.6 convolution_add_fusion.7
  485.4 1.5 convolution_add_fusion.6
  489.1 1.4 fusion.7
  490.5 2.3 copy.69
  493.1 2.7 fusion.20
  495.8 2.5 fusion.22
  498.4 2.5 fusion.24
  500.9 1.3 fusion.26
  502.2 1.3 fusion.28
  503.5 1.3 fusion.30
  504.9 1.3 fusion.32
  506.1 1.3 fusion.34
  507.5 3.6 pad_slice_fusion
  511.1 2.3 copy.44
  513.4 2.3 copy.45
  515.6 2.3 copy.46
  517.9 2.3 copy.47
  520.2 2.3 copy.49
  522.5 2.3 copy.50
  524.8 1.4 copy.51
  526.7 1.3 copy.48
  528.0 1.9 fusion.69
  529.9 1.9 convolution_add_fusion.19
  531.8 1.9 convolution_add_fusion.18
  533.7 1.5 convolution_add_fusion.17
  535.2 1.5 convolution_add_fusion.16
  536.7 1.5 convolution_add_fusion.15
  538.2 1.5 convolution_add_fusion.14
  539.7 1.5 convolution_add_fusion.13
  541.2 1.5 convolution_add_fusion.12
  542.6 18.8 %reduce-scatter.15.cloned.1.call-done = bf16[128,256]{1,0:T(8,128)(2,1)} async-done(((bf16[2048,256]{1,0:T(8,128)(2,1)}), bf16[128,256]{1,0:T(8,128)(2,1)}) %reduce-scatter.15.cloned.1.call-update) | async-done | bytes 65552
  563.1 88.6 %reduce-scatter.9.cloned.1.call-done = bf16[9,128,128]{2,1,0:T(8,128)(2,1)} async-done(((bf16[9,2048,128]{2,1,0:T(8,128)(2,1)}), bf16[9,128,128]{2,1,0:T(8,128)(2,1)}) %reduce-scatter.9.cloned.1.call-update) | async-done | bytes 294928 | tf_op jit(solution)/shard_map/reduce_scatter | solution.py:108
  651.7 3.0 multiply_subtract_fusion.1
  (128 shorter events, 22.4 us)
Async XLA Ops:
  7.2 69.9 %all-gather.5.cloned.1.call-start = ((), (), s32[]{:S(2)}) async-start(), calls=%async_computation.4 | async-start | bytes 1114112 | tf_op jit(solution)/shard_map/all_gather | solution.py:78
  7.9 132.8 %all-gather.7.cloned.1.call-start = ((), (), s32[]{:S(2)}) async-start(), calls=%async_computation.5 | async-start | bytes 5013504 | tf_op jit(solution)/shard_map/all_gather | solution.py:74
  9.8 210.6 %all-gather.9.cloned.1.call-start = ((), (), s32[]{:S(2)}) async-start(), calls=%async_computation.6 | async-start | bytes 1114112 | tf_op jit(solution)/shard_map/all_gather | solution.py:78
  140.7 6.1 copy-start.1
  140.7 7.8 %copy-start.2 = (bf16[1,2,128,2048]{3,2,1,0:T(8,128)(2,1)S(1)}, bf16[1,2,128,2048]{3,2,1,0:T(8,128)(2,1)}, u32[]{:S(2)}) copy-start(bf16[1,2,128,2048]{3,2,1,0:T(8,128)(2,1)} %all-gather.5.cloned.1.call-done) | copy-start | bytes 3145732
  140.7 8.2 %copy-start.5 = (bf16[1,2,128,2048]{3,2,1,0:T(8,128)(2,1)S(1)}, bf16[1,2,128,2048]{3,2,1,0:T(8,128)(2,1)}, u32[]{:S(2)}) copy-start(bf16[1,2,128,2048]{3,2,1,0:T(8,128)(2,1)} %get-tuple-element.28) | copy-start | bytes 3145732
  142.6 6.7 %copy-start.3 = (bf16[1,2,128,2048]{3,2,1,0:T(8,128)(2,1)S(1)}, bf16[1,2,128,2048]{3,2,1,0:T(8,128)(2,1)}, u32[]{:S(2)}) copy-start(bf16[1,2,128,2048]{3,2,1,0:T(8,128)(2,1)} %get-tuple-element.29) | copy-start | bytes 3145732
  148.5 71.9 %copy-start.15 = (bf16[1,2,128,128]{3,2,1,0:T(8,128)(2,1)S(1)}, bf16[1,2,128,128]{3,2,1,0:T(8,128)(2,1)}, u32[]{:S(2)}) copy-start(bf16[1,2,128,128]{3,2,1,0:T(8,128)(2,1)} %param.9) | copy-start | bytes 196612
  151.3 75.1 %copy-start.24 = (f32[2]{0:T(128)}, f32[2]{0:T(128)S(1)}, u32[]{:S(2)}) copy-start(f32[2]{0:T(128)S(1)} %reduce_sum.85) | copy-start | bytes 28
  152.4 165.9 %reduce-scatter.11.cloned.1.call-start = ((), (), s32[]{:S(2)}) async-start(), calls=%async_computation.9 | async-start | bytes 5013504 | tf_op jit(solution)/shard_map/reduce_scatter | solution.py:108
  220.4 4.8 copy-start.7
  228.8 2.1 copy-start.9
  231.0 151.4 %all-gather.11.cloned.1.call-start = ((), (), s32[]{:S(2)}) async-start(), calls=%async_computation.7 | async-start | bytes 5013504 | tf_op jit(solution)/shard_map/all_gather | solution.py:74
  321.6 142.0 %reduce-scatter.13.cloned.1.call-start = ((), (), s32[]{:S(2)}) async-start(), calls=%async_computation.10 | async-start | bytes 1114112
  382.4 3.2 copy-start
  382.4 3.2 copy-start.23
  382.4 3.7 copy-start.22
  382.4 4.1 copy-start.18
  385.6 1.4 copy-start.17
  386.5 0.9 copy-start.16
  392.2 169.2 %reduce-scatter.15.cloned.1.call-start = ((), (), s32[]{:S(2)}) async-start(), calls=%async_computation.11 | async-start | bytes 1114112
  482.1 3.3 copy-start.20
  482.1 4.8 slice-start
  483.7 3.1 slice-start.1
  483.7 3.1 copy-start.19
  492.8 158.9 %reduce-scatter.9.cloned.1.call-start = ((), (), s32[]{:S(2)}) async-start(), calls=%async_computation.8 | async-start | bytes 5013504 | tf_op jit(solution)/shard_map/reduce_scatter | solution.py:108
  493.1 9.1 %copy-start.6 = (bf16[1,2,128,2048]{3,2,1,0:T(8,128)(2,1)S(1)}, bf16[1,2,128,2048]{3,2,1,0:T(8,128)(2,1)}, u32[]{:S(2)}) copy-start(bf16[1,2,128,2048]{3,2,1,0:T(8,128)(2,1)} %get-tuple-element.28) | copy-start | bytes 3145732
  493.1 10.4 %copy-start.4 = (bf16[1,2,128,2048]{3,2,1,0:T(8,128)(2,1)S(1)}, bf16[1,2,128,2048]{3,2,1,0:T(8,128)(2,1)}, u32[]{:S(2)}) copy-start(bf16[1,2,128,2048]{3,2,1,0:T(8,128)(2,1)} %get-tuple-element.29) | copy-start | bytes 3145732
  503.5 3.9 copy-start.8
  528.0 5.7 copy-start.13
  528.0 7.2 %copy-start.14 = (bf16[1,2,128,2048]{3,2,1,0:T(8,128)(2,1)S(1)}, bf16[1,2,128,2048]{3,2,1,0:T(8,128)(2,1)}, u32[]{:S(2)}) copy-start(bf16[1,2,128,2048]{3,2,1,0:T(8,128)(2,1)} %copy.48) | copy-start | bytes 3145732
  528.0 8.7 %copy-start.12 = (bf16[1,2,128,2048]{3,2,1,0:T(8,128)(2,1)S(1)}, bf16[1,2,128,2048]{3,2,1,0:T(8,128)(2,1)}, u32[]{:S(2)}) copy-start(bf16[1,2,128,2048]{3,2,1,0:T(8,128)(2,1)} %copy.49) | copy-start | bytes 3145732
  529.9 8.3 %copy-start.11 = (bf16[1,2,128,2048]{3,2,1,0:T(8,128)(2,1)S(1)}, bf16[1,2,128,2048]{3,2,1,0:T(8,128)(2,1)}, u32[]{:S(2)}) copy-start(bf16[1,2,128,2048]{3,2,1,0:T(8,128)(2,1)} %copy.50) | copy-start | bytes 3145732
  531.8 7.9 %copy-start.10 = (bf16[1,2,128,2048]{3,2,1,0:T(8,128)(2,1)S(1)}, bf16[1,2,128,2048]{3,2,1,0:T(8,128)(2,1)}, u32[]{:S(2)}) copy-start(bf16[1,2,128,2048]{3,2,1,0:T(8,128)(2,1)} %copy.51) | copy-start | bytes 3145732
  535.2 27.2 %copy-start.21 = (bf16[1,2,128,128]{3,2,1,0:T(8,128)(2,1)S(1)}, bf16[1,2,128,128]{3,2,1,0:T(8,128)(2,1)}, u32[]{:S(2)}) copy-start(bf16[1,2,128,128]{3,2,1,0:T(8,128)(2,1)} %param.8) | copy-start | bytes 196612
Sparse Core Ops, SparseCore 0:
  9.7 67.3 all-gather.4
  80.4 60.2 all-gather.6
  152.5 67.8 all-gather.8
  231.1 87.1 reduce-scatter.10
  321.7 60.6 all-gather.10
  392.3 71.1 reduce-scatter.12
  493.0 68.4 reduce-scatter.14
  565.8 85.8 reduce-scatter.8
where the time goes:
time: 664 us; the launch traced here: 662 us
  waiting for transfers between devices  520 us (78%)
  matrix products  65.3 us (10%)
  local copies, waits for them, and re-layouts  46.1 us (7%)
  between operations  14.8 us (2%)
  other arithmetic  14.2 us (2%)
    reduce_scatter x2, waiting for transfers between devices, filter_grad(): lax.psum_scatter(partial_sum.astype(jnp.bfloat16), 'sample', scatter_dime...  176 us
    all_gather x2, waiting for transfers between devices, keep_panels(): return lax.all_gather(source, 'filter', axis=3, tiled=True)  135 us
    all_gather x2, waiting for transfers between devices, full_weight(): lax.all_gather(master.astype(jnp.bfloat16), 'sample', axis=1, tiled=True)  118 us
    unnamed x10, waiting for transfers between devices  90.9 us
    slice x20, local copies, waits for them, and re-layouts, window(): padded[:, row_start:row_start + height, column_start:column_start + bread...  33.4 us
    dot_general x18, matrix products, tap_grads(): lax.dot_general(shifted, flat_up, (((1,), (1,)), ((0,), (0,))), preferred...  25.2 us
    dot_general x18, matrix products, conv_forward(): jnp.dot(shifted.reshape(samples * height * breadth, depth_in), weight[ker...  24.4 us
    dot_general x18, matrix products, data_grad(): lax.dot_general(weight[kernel_tap], shifted_all[kernel_tap], (((1,), (1,)...  15.7 us
  transfers between devices with their start and end apart: 8, of which 8 were waited for; matrix products, arithmetic and copies ran while one was open for 9% of the time, Pallas kernels for 0%

commit v1 on v0

v1 whole, which is shorter than its diff:
```python
import jax
import jax.numpy as jnp
from jax import lax
from jax.sharding import PartitionSpec as P

GROUP = 64

NORM_EPS = 1e-05
LEARN_RATE = 0.001
BETA_ONE = 0.9
BETA_TWO = 0.999
ADAM_EPS = 1e-08
CORRECT_ONE = 1.0 - 0.9**10
CORRECT_TWO = 1.0 - 0.999**10


def pad_slab(field):
    return jnp.pad(field, ((0, 0), (1, 1), (1, 1), (0, 0)))


def window(padded, row_start, column_start, height, breadth):
    return padded[:, row_start : row_start + height, column_start : column_start + breadth, :]


def conv_forward(source, weight):
    samples, height, breadth, depth_in = source.shape
    padded = pad_slab(source)
    summed = jnp.zeros((samples * height * breadth, weight.shape[2]), jnp.float32)
    for kernel_tap in range(9):
        shifted = window(padded, kernel_tap // 3, kernel_tap % 3, height, breadth)
        summed = summed + jnp.dot(
            shifted.reshape(samples * height * breadth, depth_in),
            weight[kernel_tap],
            preferred_element_type=jnp.float32,
        )
    return summed.reshape(samples, height, breadth, weight.shape[2])


def adjoint_block(upstream, weight):
    samples, height, breadth, depth_out = upstream.shape
    padded = pad_slab(upstream)
    summed = jnp.zeros((samples * height * breadth, weight.shape[1]), jnp.float32)
    for kernel_tap in range(9):
        shifted = window(padded, 2 - kernel_tap // 3, 2 - kernel_tap % 3, height, breadth)
        summed = summed + lax.dot_general(
            shifted.reshape(samples * height * breadth, depth_out),
            weight[kernel_tap],
            (((1,), (1,)), ((), ())),
            preferred_element_type=jnp.float32,
        )
    return summed.reshape(samples, height, breadth, weight.shape[1])


def group_silu(pre_act):
    samples, height, breadth, depth_all = pre_act.shape
    grouped = pre_act.reshape(samples, height, breadth, depth_all // GROUP, GROUP)
    center = jnp.mean(grouped, axis=(1, 2, 4), keepdims=True)
    deviation = grouped - center
    spread = jnp.mean(deviation * deviation, axis=(1, 2, 4), keepdims=True)
    return jax.nn.silu(deviation * lax.rsqrt(spread + NORM_EPS)).reshape(pre_act.shape)


def tap_grad_sum(source, upstream):
    samples, height, breadth, depth_in = source.shape
    padded = pad_slab(source)
    flat_up = upstream.reshape(samples, height * breadth, upstream.shape[3])
    results = []
    for kernel_tap in range(9):
        shifted = window(padded, kernel_tap // 3, kernel_tap % 3, height, breadth).reshape(
            samples, height * breadth, depth_in
        )
        per_sample = lax.dot_general(
            shifted, flat_up, (((1,), (1,)), ((0,), (0,))), preferred_element_type=jnp.float32
        )
        results.append(jnp.sum(per_sample.astype(jnp.bfloat16).astype(jnp.float32), axis=0))
    return jnp.stack(results, axis=0)


def adam_update(master, moment, second, gradient):
    moment_new = BETA_ONE * moment + (1.0 - BETA_ONE) * gradient
    second_new = BETA_TWO * second + (1.0 - BETA_TWO) * gradient * gradient
    step_size = moment_new / CORRECT_ONE / (jnp.sqrt(second_new / CORRECT_TWO) + ADAM_EPS)
    return (master - LEARN_RATE * step_size, moment_new, second_new)


def transpose_mesh(block):
    count = lax.axis_size("sample")
    pairs = [(row * count + col, col * count + row) for row in range(count) for col in range(count)]
    return lax.ppermute(block, ("sample", "filter"), pairs)


def gather_along(block, axis):
    count = lax.axis_size(axis)
    return lax.all_to_all(jnp.tile(block, (count, 1, 1, 1)), axis, 0, 0, tiled=True)


def sum_scatter_along(blocks, axis):
    count = lax.axis_size(axis)
    pieces = lax.all_to_all(blocks, axis, 0, 0, tiled=True)
    return jnp.sum(pieces.astype(jnp.float32).reshape((count,) + blocks.shape[1:]), axis=0, keepdims=True)


def forward_conv(field, weight):
    whole = gather_along(transpose_mesh(field), "filter")
    partial = conv_forward(whole, weight)
    return whole, sum_scatter_along(partial, "sample")


def adjoint_conv(upstream_whole, weight):
    terms = adjoint_block(upstream_whole, weight).astype(jnp.bfloat16)
    return transpose_mesh(sum_scatter_along(terms, "filter"))


def per_device(
    activations,
    cotangent,
    master_first,
    moment_first,
    second_first,
    master_second,
    moment_second,
    second_second,
):
    weight_first = master_first.astype(jnp.bfloat16)
    weight_second = master_second.astype(jnp.bfloat16)
    whole_cotangent = gather_along(cotangent, "sample")
    whole_input, pre_first = forward_conv(activations, weight_first)
    hidden = group_silu(pre_first).astype(jnp.bfloat16)
    whole_hidden, pre_second = forward_conv(hidden, weight_second)
    level_out = (activations.astype(jnp.float32) + pre_second).astype(jnp.bfloat16)
    hidden_grad = adjoint_conv(whole_cotangent, weight_second)
    _, pullback = jax.vjp(group_silu, pre_first)
    pre_grad = pullback(hidden_grad)[0].astype(jnp.bfloat16)
    whole_pre_grad = gather_along(pre_grad, "sample")
    input_grad = (cotangent.astype(jnp.float32) + adjoint_conv(whole_pre_grad, weight_first)).astype(
        jnp.bfloat16
    )
    grad_second = tap_grad_sum(whole_hidden, whole_cotangent)
    grad_first = tap_grad_sum(whole_input, whole_pre_grad)
    new_master_first, new_moment_first, new_second_first = adam_update(
        master_first, moment_first, second_first, grad_first
    )
    new_master_second, new_moment_second, new_second_second = adam_update(
        master_second, moment_second, second_second, grad_second
    )
    return (
        level_out,
        input_grad,
        new_master_first,
        new_moment_first,
        new_second_first,
        new_master_second,
        new_moment_second,
        new_second_second,
    )


def solution(mesh):
    field = P("sample", None, None, "filter")
    taps = P(None, "sample", "filter")
    return jax.shard_map(
        per_device,
        mesh=mesh,
        in_specs=(field, field, taps, taps, taps, taps, taps, taps),
        out_specs=(field, field, taps, taps, taps, taps, taps, taps),
        check_vma=False,
    )
```

time: 664 us -> 337 us (0.51)
  waiting for transfers between devices: 520 us -> 154 us
  starting transfers between devices: 0.73 us -> 72.5 us
  blocking collectives: 0 us -> 33.2 us
  matrix products: 65.3 us -> 33 us
  local copies, waits for them, and re-layouts: 46.1 us -> 29.6 us
  between operations: 14.8 us -> 1.66 us
    all_gather x4 -> x0, waiting for transfers between devices: 254 us -> none  [the longest x2 135 us: keep_panels(): return lax.all_gather(source, 'filter', axis=3, tiled=True)]
    reduce_scatter x2 -> x0, waiting for transfers between devices: 176 us -> none  [filter_grad(): lax.psum_scatter(partial_sum.astype(jnp.bfloat16), 'sample', scatter_dime...]
    all_to_all x0 -> x7, waiting for transfers between devices: none -> 112 us  [the longest x4 72.3 us: gather_along(): lax.all_to_all(jnp.tile(block, (count, 1, 1, 1)), axis, 0, 0, tiled=True)]
    unnamed x10 -> x0, waiting for transfers between devices: 90.9 us -> none
    all_to_all x0 -> x7, starting transfers between devices: none -> 49.8 us  [the longest x4 30.1 us: gather_along(): lax.all_to_all(jnp.tile(block, (count, 1, 1, 1)), axis, 0, 0, tiled=True)]
    ppermute x0 -> x4, waiting for transfers between devices: none -> 42.1 us  [transpose_mesh(): return lax.ppermute(block, ('sample', 'filter'), pairs)]
    all_to_all x0 -> x1, blocking collectives: none -> 33.2 us  [sum_scatter_along(): pieces = lax.all_to_all(blocks, axis, 0, 0, tiled=True)]
    ppermute x0 -> x4, starting transfers between devices: none -> 22.7 us  [transpose_mesh(): return lax.ppermute(block, ('sample', 'filter'), pairs)]
  transfers between devices with their start and end apart: 8 -> 11, of which waited for: 8 -> 11; matrix products, arithmetic and copies ran while one was open for 9% -> 8% of each run, Pallas kernels for 0% -> 0%
where the time goes in v1:
time: 337 us; the launch traced here: 335 us
  waiting for transfers between devices  154 us (46%)
  starting transfers between devices  72.5 us (22%)
  blocking collectives  33.2 us (10%)
  matrix products  33 us (10%)
  local copies, waits for them, and re-layouts  29.6 us (9%)
  other arithmetic  11.7 us (3%)
    all_to_all x4, waiting for transfers between devices, gather_along(): lax.all_to_all(jnp.tile(block, (count, 1, 1, 1)), axis, 0, 0, tiled=True)  72.3 us
    ppermute x4, waiting for transfers between devices, transpose_mesh(): return lax.ppermute(block, ('sample', 'filter'), pairs)  42.1 us
    all_to_all x3, waiting for transfers between devices, sum_scatter_along(): pieces = lax.all_to_all(blocks, axis, 0, 0, tiled=True)  39.4 us
    all_to_all x1, blocking collectives, sum_scatter_along(): pieces = lax.all_to_all(blocks, axis, 0, 0, tiled=True)  33.2 us
    all_to_all x4, starting transfers between devices, gather_along(): lax.all_to_all(jnp.tile(block, (count, 1, 1, 1)), axis, 0, 0, tiled=True)  30.1 us
    ppermute x4, starting transfers between devices, transpose_mesh(): return lax.ppermute(block, ('sample', 'filter'), pairs)  22.7 us
    all_to_all x3, starting transfers between devices, sum_scatter_along(): pieces = lax.all_to_all(blocks, axis, 0, 0, tiled=True)  19.6 us
    unnamed x120, local copies, waits for them, and re-layouts  12.6 us
  transfers between devices with their start and end apart: 11, of which 11 were waited for; matrix products, arithmetic and copies ran while one was open for 8% of the time, Pallas kernels for 0%

profile of v1, /device:TPU:6, one launch (start us, length us, event | category | flops | bytes accessed | tf_op | source)
XLA Modules:
  0.0 335.5 jit_solution(5289877638386761376)
XLA Ops:
  0.6 7.9 %collective-permute-start = (bf16[1,2,128,128]{3,2,1,0:T(8,128)(2,1)}, bf16[1,2,128,128]{3,2,1,0:T(8,128)(2,1)S(1)}, u32[]{:S(2)}, u32[]{:S(2)}) collective-permute-start(bf16[1,2,128,128]{3,2,1,0:T(8,128)(2,1)} %param.8), channel_id=1, source_target_pairs={{0,0},{1,16},{2,32},{3,48},{4,64},{5,80},{6,96},{7,112},{8,128},{9... | collective-permute-start | bytes 196616 | tf_op jit(solution)/shard_map/ppermute | solution.py:89
  8.5 8.0 %collective-permute-done = bf16[1,2,128,128]{3,2,1,0:T(8,128)(2,1)S(1)} collective-permute-done((bf16[1,2,128,128]{3,2,1,0:T(8,128)(2,1)}, bf16[1,2,128,128]{3,2,1,0:T(8,128)(2,1)S(1)}, u32[]{:S(2)}, u32[]{:S(2)}) %collective-permute-start) | collective-permute-done | bytes 65568 | tf_op jit(solution)/shard_map/ppermute | solution.py:89
  16.5 1.2 tile.17
  17.7 9.0 %all-to-all-start = ((bf16[16,2,128,128]{3,2,1,0:T(8,128)(2,1)}), bf16[16,2,128,128]{3,2,1,0:T(8,128)(2,1)S(1)}, u32[]{:S(2)}, u32[]{:S(2)}) async-start(bf16[16,2,128,128]{3,2,1,0:T(8,128)(2,1)} %tile.17), calls=%async_computation | async-start | bytes 2097152 | tf_op jit(solution)/shard_map/all_to_all | solution.py:94
  26.8 27.3 %all-to-all-done = bf16[16,2,128,128]{3,2,1,0:T(8,128)(2,1)S(1)} async-done(((bf16[16,2,128,128]{3,2,1,0:T(8,128)(2,1)}), bf16[16,2,128,128]{3,2,1,0:T(8,128)(2,1)S(1)}, u32[]{:S(2)}, u32[]{:S(2)}) %all-to-all-start) | async-done | bytes 1048608 | tf_op jit(solution)/shard_map/all_to_all | solution.py:94
  54.1 2.4 pad_slice_fusion.24
  61.1 33.2 %all_to_all.40 = f32[16,2,128,128]{3,2,1,0:T(8,128)} all-to-all(f32[16,2,128,128]{3,2,1,0:T(8,128)S(1)} %bitcast.324), channel_id=1, replica_groups=mesh['sample'=16,'filter'=16] {'sample'}, dimensions={0} | all-to-all | bytes 4194304 | tf_op jit(solution)/shard_map/all_to_all | solution.py:99
  94.3 1.2 tile.41
  95.5 6.2 %all-to-all-start.4 = ((bf16[16,2,128,128]{3,2,1,0:T(8,128)(2,1)}), bf16[16,2,128,128]{3,2,1,0:T(8,128)(2,1)S(1)}, u32[]{:S(2)}, u32[]{:S(2)}) async-start(bf16[16,2,128,128]{3,2,1,0:T(8,128)(2,1)} %tile.41), calls=%async_computation.4 | async-start | bytes 2097152 | tf_op jit(solution)/shard_map/all_to_all | solution.py:94
  101.7 2.2 fusion.54
  104.7 5.0 %collective-permute-start.1 = (bf16[1,2,128,128]{3,2,1,0:T(8,128)(2,1)S(1)}, bf16[1,2,128,128]{3,2,1,0:T(8,128)(2,1)S(1)}, u32[]{:S(2)}, u32[]{:S(2)}) collective-permute-start(bf16[1,2,128,128]{3,2,1,0:T(8,128)(2,1)S(1)} %multiply_convert_fusion), channel_id=1, source_target_pairs={{0,0},{1,16},{2,32},{3,48},{4,64},{5,80},{6,96},{7,112},{8,128},{9... | collective-permute-start | bytes 196616 | tf_op jit(solution)/shard_map/ppermute | solution.py:89
  109.7 7.8 %all-to-all-done.4 = bf16[16,2,128,128]{3,2,1,0:T(8,128)(2,1)S(1)} async-done(((bf16[16,2,128,128]{3,2,1,0:T(8,128)(2,1)}), bf16[16,2,128,128]{3,2,1,0:T(8,128)(2,1)S(1)}, u32[]{:S(2)}, u32[]{:S(2)}) %all-to-all-start.4) | async-done | bytes 1048608 | tf_op jit(solution)/shard_map/all_to_all | solution.py:94
  117.5 3.9 %collective-permute-done.1 = bf16[1,2,128,128]{3,2,1,0:T(8,128)(2,1)S(1)} collective-permute-done((bf16[1,2,128,128]{3,2,1,0:T(8,128)(2,1)S(1)}, bf16[1,2,128,128]{3,2,1,0:T(8,128)(2,1)S(1)}, u32[]{:S(2)}, u32[]{:S(2)}) %collective-permute-start.1) | collective-permute-done | bytes 65568 | tf_op jit(solution)/shard_map/ppermute | solution.py:89
  121.4 1.2 tile.19
  122.7 3.9 %all-to-all-start.2 = ((bf16[16,2,128,128]{3,2,1,0:T(8,128)(2,1)}), bf16[16,2,128,128]{3,2,1,0:T(8,128)(2,1)S(1)}, u32[]{:S(2)}, u32[]{:S(2)}) async-start(bf16[16,2,128,128]{3,2,1,0:T(8,128)(2,1)} %tile.19), calls=%async_computation.2 | async-start | bytes 2097152 | tf_op jit(solution)/shard_map/all_to_all | solution.py:94
  126.6 3.5 %pad_slice_fusion.8 = (bf16[16,2,128,128]{3,2,1,0:T(8,128)(2,1)}, bf16[16,2,128,128]{3,2,1,0:T(8,128)(2,1)}, bf16[16,2,128,128]{3,2,1,0:T(8,128)(2,1)}, bf16[16,...) fusion(bf16[16,2,128,128]{3,2,1,0:T(8,128)(2,1)S(1)} %all-to-al, ...), kind=kLoop, calls=%fused_computation.42 | loop fusion | bytes 9437184 | tf_op jit(solution)/shard_map/slice | solution.py:22
  130.1 24.3 %all-to-all-done.2 = bf16[16,2,128,128]{3,2,1,0:T(8,128)(2,1)S(1)} async-done(((bf16[16,2,128,128]{3,2,1,0:T(8,128)(2,1)}), bf16[16,2,128,128]{3,2,1,0:T(8,128)(2,1)S(1)}, u32[]{:S(2)}, u32[]{:S(2)}) %all-to-all-start.2) | async-done | bytes 1048608 | tf_op jit(solution)/shard_map/all_to_all | solution.py:94
  154.4 2.4 pad_slice_fusion.16
  157.4 0.5 fusion.30
  157.9 0.5 fusion.31
  162.3 1.5 multiply_subtract_fusion
  163.8 1.8 fusion.52
  166.0 0.8 copy-done.34
  167.2 0.8 copy-done.33
  168.5 0.8 copy-done.32
  170.1 0.8 copy-done.31
  171.3 0.8 copy-done.30
  172.6 0.8 copy-done.29
  173.8 0.8 copy-done.36
  174.6 1.5 fusion
  176.0 5.7 %all-to-all-start.5 = ((bf16[16,2,128,128]{3,2,1,0:T(8,128)(2,1)}), bf16[16,2,128,128]{3,2,1,0:T(8,128)(2,1)}, u32[]{:S(2)}, u32[]{:S(2)}) async-start(bf16[16,2,128,128]{3,2,1,0:T(8,128)(2,1)} %bitcast.342), calls=%async_computation.5 | async-start | bytes 2097152 | tf_op jit(solution)/shard_map/all_to_all | solution.py:99
  181.7 2.1 convolution_add_fusion.23
  184.3 0.8 copy-done.23
  186.0 0.8 copy-done.21
  187.2 0.8 copy-done.19
  188.4 0.8 copy-done.17
  189.6 0.8 copy-done.15
  190.4 1.8 convolution_add_fusion.16
  192.2 15.6 %all-to-all-done.5 = bf16[16,2,128,128]{3,2,1,0:T(8,128)(2,1)} async-done(((bf16[16,2,128,128]{3,2,1,0:T(8,128)(2,1)}), bf16[16,2,128,128]{3,2,1,0:T(8,128)(2,1)}, u32[]{:S(2)}, u32[]{:S(2)}) %all-to-all-start.5) | async-done | bytes 1048608 | tf_op jit(solution)/shard_map/all_to_all | solution.py:99
  207.8 6.9 %all-to-all-start.3 = ((f32[16,2,128,128]{3,2,1,0:T(8,128)}), f32[16,2,128,128]{3,2,1,0:T(8,128)S(1)}, u32[]{:S(2)}, u32[]{:S(2)}) async-start(f32[16,2,128,128]{3,2,1,0:T(8,128)} %bitcast.323), calls=%async_computation.3 | async-start | bytes 4194304 | tf_op jit(solution)/shard_map/all_to_all | solution.py:99
  214.7 1.4 convert_reduce_fusion.1
  216.1 5.0 %collective-permute-start.2 = (f32[1,2,128,128]{3,2,1,0:T(8,128)S(1)}, f32[1,2,128,128]{3,2,1,0:T(8,128)S(1)}, u32[]{:S(2)}, u32[]{:S(2)}) collective-permute-start(f32[1,2,128,128]{3,2,1,0:T(8,128)S(1)} %bitcast.345), channel_id=1, source_target_pairs={{0,0},{1,16},{2,32},{3,48},{4,64},{5,80},{6,96},{7,112},{8,128},{9... | collective-permute-start | bytes 393224 | tf_op jit(solution)/shard_map/ppermute | solution.py:89
  221.1 18.3 %collective-permute-done.2 = f32[1,2,128,128]{3,2,1,0:T(8,128)S(1)} collective-permute-done((f32[1,2,128,128]{3,2,1,0:T(8,128)S(1)}, f32[1,2,128,128]{3,2,1,0:T(8,128)S(1)}, u32[]{:S(2)}, u32[]{:S(2)}) %collective-permute-start.2) | collective-permute-done | bytes 131104 | tf_op jit(solution)/shard_map/ppermute | solution.py:89
  240.4 6.1 %all-to-all-done.3 = f32[16,2,128,128]{3,2,1,0:T(8,128)S(1)} async-done(((f32[16,2,128,128]{3,2,1,0:T(8,128)}), f32[16,2,128,128]{3,2,1,0:T(8,128)S(1)}, u32[]{:S(2)}, u32[]{:S(2)}) %all-to-all-start.3) | async-done | bytes 2097184 | tf_op jit(solution)/shard_map/all_to_all | solution.py:99
  246.4 1.4 tile.43
  248.1 11.0 %all-to-all-start.6 = ((bf16[16,2,128,128]{3,2,1,0:T(8,128)(2,1)}), bf16[16,2,128,128]{3,2,1,0:T(8,128)(2,1)S(1)}, u32[]{:S(2)}, u32[]{:S(2)}) async-start(bf16[16,2,128,128]{3,2,1,0:T(8,128)(2,1)} %tile.43), calls=%async_computation.6 | async-start | bytes 2097152 | tf_op jit(solution)/shard_map/all_to_all | solution.py:94
  259.1 1.7 reduce_sum.290
  260.8 0.6 fusion.47
  261.5 13.0 %all-to-all-done.6 = bf16[16,2,128,128]{3,2,1,0:T(8,128)(2,1)S(1)} async-done(((bf16[16,2,128,128]{3,2,1,0:T(8,128)(2,1)}), bf16[16,2,128,128]{3,2,1,0:T(8,128)(2,1)S(1)}, u32[]{:S(2)}, u32[]{:S(2)}) %all-to-all-start.6) | async-done | bytes 1048608 | tf_op jit(solution)/shard_map/all_to_all | solution.py:94
  274.4 2.5 pad_slice_fusion
  280.4 1.5 fusion.1
  281.9 7.0 %all-to-all-start.7 = ((bf16[16,2,128,128]{3,2,1,0:T(8,128)(2,1)}), bf16[16,2,128,128]{3,2,1,0:T(8,128)(2,1)}, u32[]{:S(2)}, u32[]{:S(2)}) async-start(bf16[16,2,128,128]{3,2,1,0:T(8,128)(2,1)} %bitcast.341), calls=%async_computation.7 | async-start | bytes 2097152 | tf_op jit(solution)/shard_map/all_to_all | solution.py:99
  288.9 1.8 fusion.20
  290.7 0.6 bitcast_dynamic-update-slice_fusion.17
  291.9 0.5 fusion.22
  292.6 0.5 fusion.23
  293.7 1.8 fusion.25
  296.0 0.5 fusion.27
  297.4 17.7 %all-to-all-done.7 = bf16[16,2,128,128]{3,2,1,0:T(8,128)(2,1)} async-done(((bf16[16,2,128,128]{3,2,1,0:T(8,128)(2,1)}), bf16[16,2,128,128]{3,2,1,0:T(8,128)(2,1)}, u32[]{:S(2)}, u32[]{:S(2)}) %all-to-all-start.7) | async-done | bytes 1048608 | tf_op jit(solution)/shard_map/all_to_all | solution.py:99
  315.1 1.4 convert_reduce_fusion
  316.5 4.9 %collective-permute-start.3 = (f32[1,2,128,128]{3,2,1,0:T(8,128)S(1)}, f32[1,2,128,128]{3,2,1,0:T(8,128)S(1)}, u32[]{:S(2)}, u32[]{:S(2)}) collective-permute-start(f32[1,2,128,128]{3,2,1,0:T(8,128)S(1)} %bitcast.344), channel_id=1, source_target_pairs={{0,0},{1,16},{2,32},{3,48},{4,64},{5,80},{6,96},{7,112},{8,128},{9... | collective-permute-start | bytes 393224 | tf_op jit(solution)/shard_map/ppermute | solution.py:89
  321.4 1.4 multiply_subtract_fusion.1
  322.9 12.0 %collective-permute-done.3 = f32[1,2,128,128]{3,2,1,0:T(8,128)S(1)} collective-permute-done((f32[1,2,128,128]{3,2,1,0:T(8,128)S(1)}, f32[1,2,128,128]{3,2,1,0:T(8,128)S(1)}, u32[]{:S(2)}, u32[]{:S(2)}) %collective-permute-start.3) | collective-permute-done | bytes 131104 | tf_op jit(solution)/shard_map/ppermute | solution.py:89
  334.8 0.6 add_convert_fusion
  (178 shorter events, 22.8 us)
Async XLA Ops:
  0.6 26.1 %copy-start.41 = (f32[9,128,128]{2,1,0:T(8,128)S(1)}, f32[9,128,128]{2,1,0:T(8,128)}, u32[]{:S(2)}) copy-start(f32[9,128,128]{2,1,0:T(8,128)} %param.10) | copy-start | bytes 1769476
  0.6 15.8 %collective-permute-start = (bf16[1,2,128,128]{3,2,1,0:T(8,128)(2,1)}, bf16[1,2,128,128]{3,2,1,0:T(8,128)(2,1)S(1)}, u32[]{:S(2)}, u32[]{:S(2)}) collective-permute-start(bf16[1,2,128,128]{3,2,1,0:T(8,128)(2,1)} %param.8), channel_id=1, source_target_pairs={{0,0},{1,16},{2,32},{3,48},{4,64},{5,80},{6,96},{7,112},{8,128},{9... | collective-permute-start | bytes 196616 | tf_op jit(solution)/shard_map/ppermute | solution.py:89
  17.7 36.4 %all-to-all-start = ((bf16[16,2,128,128]{3,2,1,0:T(8,128)(2,1)}), bf16[16,2,128,128]{3,2,1,0:T(8,128)(2,1)S(1)}, u32[]{:S(2)}, u32[]{:S(2)}) async-start(bf16[16,2,128,128]{3,2,1,0:T(8,128)(2,1)} %tile.17), calls=%async_computation | async-start | bytes 2097152 | tf_op jit(solution)/shard_map/all_to_all | solution.py:94
  26.7 33.9 %copy-start.39 = (bf16[9,128,128]{2,1,0:T(8,128)(2,1)}, bf16[9,128,128]{2,1,0:T(8,128)(2,1)S(1)}, u32[]{:S(2)}) copy-start(bf16[9,128,128]{2,1,0:T(8,128)(2,1)S(1)} %convert_element_type.170) | copy-start | bytes 884740
  56.5 1.0 copy-start.11
  56.5 1.3 copy-start.13
  56.5 1.6 copy-start.9
  56.5 2.0 copy-start.7
  56.5 2.9 copy-start.6
  56.5 3.3 copy-start.4
  56.5 3.7 %copy-start.2 = (bf16[16,2,128,128]{3,2,1,0:T(8,128)(2,1)}, bf16[16,2,128,128]{3,2,1,0:T(8,128)(2,1)S(1)}, u32[]{:S(2)}) copy-start(bf16[16,2,128,128]{3,2,1,0:T(8,128)(2,1)S(1)} %get-tuple-element.56) | copy-start | bytes 3145732
  56.5 4.2 %copy-start = (bf16[16,2,128,128]{3,2,1,0:T(8,128)(2,1)}, bf16[16,2,128,128]{3,2,1,0:T(8,128)(2,1)S(1)}, u32[]{:S(2)}) copy-start(bf16[16,2,128,128]{3,2,1,0:T(8,128)(2,1)S(1)} %get-tuple-element.50) | copy-start | bytes 3145732
  61.1 33.2 %copy-start.49 = (bf16[1,2,128,128]{3,2,1,0:T(8,128)(2,1)S(1)}, bf16[1,2,128,128]{3,2,1,0:T(8,128)(2,1)}, u32[]{:S(2)}) copy-start(bf16[1,2,128,128]{3,2,1,0:T(8,128)(2,1)} %param.9) | copy-start | bytes 196612
  95.5 22.0 %all-to-all-start.4 = ((bf16[16,2,128,128]{3,2,1,0:T(8,128)(2,1)}), bf16[16,2,128,128]{3,2,1,0:T(8,128)(2,1)S(1)}, u32[]{:S(2)}, u32[]{:S(2)}) async-start(bf16[16,2,128,128]{3,2,1,0:T(8,128)(2,1)} %tile.41), calls=%async_computation.4 | async-start | bytes 2097152 | tf_op jit(solution)/shard_map/all_to_all | solution.py:94
  104.7 16.7 %collective-permute-start.1 = (bf16[1,2,128,128]{3,2,1,0:T(8,128)(2,1)S(1)}, bf16[1,2,128,128]{3,2,1,0:T(8,128)(2,1)S(1)}, u32[]{:S(2)}, u32[]{:S(2)}) collective-permute-start(bf16[1,2,128,128]{3,2,1,0:T(8,128)(2,1)S(1)} %multiply_convert_fusion), channel_id=1, source_target_pairs={{0,0},{1,16},{2,32},{3,48},{4,64},{5,80},{6,96},{7,112},{8,128},{9... | collective-permute-start | bytes 196616 | tf_op jit(solution)/shard_map/ppermute | solution.py:89
  122.7 31.7 %all-to-all-start.2 = ((bf16[16,2,128,128]{3,2,1,0:T(8,128)(2,1)}), bf16[16,2,128,128]{3,2,1,0:T(8,128)(2,1)S(1)}, u32[]{:S(2)}, u32[]{:S(2)}) async-start(bf16[16,2,128,128]{3,2,1,0:T(8,128)(2,1)} %tile.19), calls=%async_computation.2 | async-start | bytes 2097152 | tf_op jit(solution)/shard_map/all_to_all | solution.py:94
  156.8 1.6 copy-start.22
  156.8 2.5 copy-start.20
  156.9 3.0 copy-start.24
  156.9 3.0 copy-start.26
  156.9 3.0 copy-start.18
  156.9 3.5 %copy-start.16 = (bf16[16,2,128,128]{3,2,1,0:T(8,128)(2,1)}, bf16[16,2,128,128]{3,2,1,0:T(8,128)(2,1)S(1)}, u32[]{:S(2)}) copy-start(bf16[16,2,128,128]{3,2,1,0:T(8,128)(2,1)S(1)} %get-tuple-element.48) | copy-start | bytes 3145732
  156.9 4.0 %copy-start.14 = (bf16[16,2,128,128]{3,2,1,0:T(8,128)(2,1)}, bf16[16,2,128,128]{3,2,1,0:T(8,128)(2,1)S(1)}, u32[]{:S(2)}) copy-start(bf16[16,2,128,128]{3,2,1,0:T(8,128)(2,1)S(1)} %get-tuple-element.42) | copy-start | bytes 3145732
  160.9 1.1 copy-start.44
  160.9 1.2 copy-start.45
  160.9 1.4 copy-start.46
  163.8 10.0 %copy-start.37 = (bf16[9,128,128]{2,1,0:T(8,128)(2,1)}, bf16[9,128,128]{2,1,0:T(8,128)(2,1)S(1)}, u32[]{:S(2)}) copy-start(bf16[9,128,128]{2,1,0:T(8,128)(2,1)S(1)} %get-tuple-element.58) | copy-start | bytes 884740
  163.8 1.8 copy-start.35
  165.6 1.2 copy-start.34
  166.8 1.2 copy-start.33
  168.0 1.2 copy-start.32
  169.7 1.2 copy-start.31
  170.9 1.2 copy-start.30
  172.1 1.2 copy-start.29
  173.3 1.2 copy-start.36
  176.0 5.7 %copy-start.27 = (bf16[16,2,128,128]{3,2,1,0:T(8,128)(2,1)S(1)}, bf16[16,2,128,128]{3,2,1,0:T(8,128)(2,1)}, u32[]{:S(2)}) copy-start(bf16[16,2,128,128]{3,2,1,0:T(8,128)(2,1)} %copy-done.26) | copy-start | bytes 3145732
  176.0 31.7 %all-to-all-start.5 = ((bf16[16,2,128,128]{3,2,1,0:T(8,128)(2,1)}), bf16[16,2,128,128]{3,2,1,0:T(8,128)(2,1)}, u32[]{:S(2)}, u32[]{:S(2)}) async-start(bf16[16,2,128,128]{3,2,1,0:T(8,128)(2,1)} %bitcast.342), calls=%async_computation.5 | async-start | bytes 2097152 | tf_op jit(solution)/shard_map/all_to_all | solution.py:99
  181.7 2.2 copy-start.25
  181.7 2.2 copy-start.38
  183.9 1.2 copy-start.23
  185.5 1.2 copy-start.21
  186.8 1.2 copy-start.19
  188.0 1.2 copy-start.17
  189.2 1.2 copy-start.15
  207.8 38.6 %all-to-all-start.3 = ((f32[16,2,128,128]{3,2,1,0:T(8,128)}), f32[16,2,128,128]{3,2,1,0:T(8,128)S(1)}, u32[]{:S(2)}, u32[]{:S(2)}) async-start(f32[16,2,128,128]{3,2,1,0:T(8,128)} %bitcast.323), calls=%async_computation.3 | async-start | bytes 4194304 | tf_op jit(solution)/shard_map/all_to_all | solution.py:99
  216.1 23.3 %collective-permute-start.2 = (f32[1,2,128,128]{3,2,1,0:T(8,128)S(1)}, f32[1,2,128,128]{3,2,1,0:T(8,128)S(1)}, u32[]{:S(2)}, u32[]{:S(2)}) collective-permute-start(f32[1,2,128,128]{3,2,1,0:T(8,128)S(1)} %bitcast.345), channel_id=1, source_target_pairs={{0,0},{1,16},{2,32},{3,48},{4,64},{5,80},{6,96},{7,112},{8,128},{9... | collective-permute-start | bytes 393224 | tf_op jit(solution)/shard_map/ppermute | solution.py:89
  246.4 1.7 copy-start.28
  247.8 13.0 %copy-start.51 = (bf16[1,2,128,128]{3,2,1,0:T(8,128)(2,1)S(1)}, bf16[1,2,128,128]{3,2,1,0:T(8,128)(2,1)}, u32[]{:S(2)}) copy-start(bf16[1,2,128,128]{3,2,1,0:T(8,128)(2,1)} %param.8) | copy-start | bytes 196612
  248.1 26.3 %all-to-all-start.6 = ((bf16[16,2,128,128]{3,2,1,0:T(8,128)(2,1)}), bf16[16,2,128,128]{3,2,1,0:T(8,128)(2,1)S(1)}, u32[]{:S(2)}, u32[]{:S(2)}) async-start(bf16[16,2,128,128]{3,2,1,0:T(8,128)(2,1)} %tile.43), calls=%async_computation.6 | async-start | bytes 2097152 | tf_op jit(solution)/shard_map/all_to_all | solution.py:94
  261.5 15.4 %copy-start.40 = (bf16[9,128,128]{2,1,0:T(8,128)(2,1)S(1)}, bf16[9,128,128]{2,1,0:T(8,128)(2,1)}, u32[]{:S(2)}) copy-start(bf16[9,128,128]{2,1,0:T(8,128)(2,1)} %copy-done.39) | copy-start | bytes 884740
  281.9 9.5 %copy-start.12 = (bf16[16,2,128,128]{3,2,1,0:T(8,128)(2,1)S(1)}, bf16[16,2,128,128]{3,2,1,0:T(8,128)(2,1)}, u32[]{:S(2)}) copy-start(bf16[16,2,128,128]{3,2,1,0:T(8,128)(2,1)} %copy-done.11) | copy-start | bytes 3145732
  281.9 33.2 %all-to-all-start.7 = ((bf16[16,2,128,128]{3,2,1,0:T(8,128)(2,1)}), bf16[16,2,128,128]{3,2,1,0:T(8,128)(2,1)}, u32[]{:S(2)}, u32[]{:S(2)}) async-start(bf16[16,2,128,128]{3,2,1,0:T(8,128)(2,1)} %bitcast.341), calls=%async_computation.7 | async-start | bytes 2097152 | tf_op jit(solution)/shard_map/all_to_all | solution.py:99
  288.9 2.9 copy-start.10
  291.4 1.2 copy-start.8
  293.1 2.4 copy-start.5
  293.7 2.3 copy-start.3
  295.5 1.2 copy-start.1
  296.0 1.2 copy-start.43
  296.7 24.7 %copy-start.42 = (f32[9,128,128]{2,1,0:T(8,128)S(1)}, f32[9,128,128]{2,1,0:T(8,128)}, u32[]{:S(2)}) copy-start(f32[9,128,128]{2,1,0:T(8,128)} %param.10) | copy-start | bytes 1769476
  297.2 24.2 %copy-start.47 = (f32[9,128,128]{2,1,0:T(8,128)S(1)}, f32[9,128,128]{2,1,0:T(8,128)}, u32[]{:S(2)}) copy-start(f32[9,128,128]{2,1,0:T(8,128)} %param.11) | copy-start | bytes 1769476
  297.2 24.2 %copy-start.48 = (f32[9,128,128]{2,1,0:T(8,128)S(1)}, f32[9,128,128]{2,1,0:T(8,128)}, u32[]{:S(2)}) copy-start(f32[9,128,128]{2,1,0:T(8,128)} %param.12) | copy-start | bytes 1769476
  316.5 18.3 %copy-start.50 = (bf16[1,2,128,128]{3,2,1,0:T(8,128)(2,1)S(1)}, bf16[1,2,128,128]{3,2,1,0:T(8,128)(2,1)}, u32[]{:S(2)}) copy-start(bf16[1,2,128,128]{3,2,1,0:T(8,128)(2,1)} %param.9) | copy-start | bytes 196612
  316.5 18.3 %collective-permute-start.3 = (f32[1,2,128,128]{3,2,1,0:T(8,128)S(1)}, f32[1,2,128,128]{3,2,1,0:T(8,128)S(1)}, u32[]{:S(2)}, u32[]{:S(2)}) collective-permute-start(f32[1,2,128,128]{3,2,1,0:T(8,128)S(1)} %bitcast.344), channel_id=1, source_target_pairs={{0,0},{1,16},{2,32},{3,48},{4,64},{5,80},{6,96},{7,112},{8,128},{9... | collective-permute-start | bytes 393224 | tf_op jit(solution)/shard_map/ppermute | solution.py:89

commit v2 on v1

--- a/solution.py
+++ b/solution.py
@@ -89,26 +89,16 @@
     return lax.ppermute(block, ("sample", "filter"), pairs)
 
 
-def gather_along(block, axis):
-    count = lax.axis_size(axis)
-    return lax.all_to_all(jnp.tile(block, (count, 1, 1, 1)), axis, 0, 0, tiled=True)
+def exchange(payload, axis):
+    return lax.all_to_all(payload, axis, 0, 0, tiled=True)
 
 
-def sum_scatter_along(blocks, axis):
-    count = lax.axis_size(axis)
-    pieces = lax.all_to_all(blocks, axis, 0, 0, tiled=True)
-    return jnp.sum(pieces.astype(jnp.float32).reshape((count,) + blocks.shape[1:]), axis=0, keepdims=True)
+def tiled(block, axis):
+    return jnp.tile(block, (lax.axis_size(axis), 1, 1, 1))
 
 
-def forward_conv(field, weight):
-    whole = gather_along(transpose_mesh(field), "filter")
-    partial = conv_forward(whole, weight)
-    return whole, sum_scatter_along(partial, "sample")
-
-
-def adjoint_conv(upstream_whole, weight):
-    terms = adjoint_block(upstream_whole, weight).astype(jnp.bfloat16)
-    return transpose_mesh(sum_scatter_along(terms, "filter"))
+def summed(pieces):
+    return jnp.sum(pieces.astype(jnp.float32), axis=0, keepdims=True)
 
 
 def per_device(
@@ -123,18 +113,29 @@
 ):
     weight_first = master_first.astype(jnp.bfloat16)
     weight_second = master_second.astype(jnp.bfloat16)
-    whole_cotangent = gather_along(cotangent, "sample")
-    whole_input, pre_first = forward_conv(activations, weight_first)
+    width = activations.shape[3]
+    whole_input = exchange(tiled(transpose_mesh(activations), "filter"), "filter")
+    partial_first = conv_forward(whole_input, weight_first).astype(jnp.bfloat16)
+    joined = exchange(jnp.concatenate([tiled(cotangent, "sample"), partial_first], axis=3), "sample")
+    whole_cotangent = joined[..., :width]
+    pre_first = summed(joined[..., width:])
     hidden = group_silu(pre_first).astype(jnp.bfloat16)
-    whole_hidden, pre_second = forward_conv(hidden, weight_second)
-    level_out = (activations.astype(jnp.float32) + pre_second).astype(jnp.bfloat16)
-    hidden_grad = adjoint_conv(whole_cotangent, weight_second)
+    terms_second = adjoint_block(whole_cotangent, weight_second).astype(jnp.bfloat16)
+    joined = exchange(
+        jnp.concatenate([tiled(transpose_mesh(hidden), "filter"), terms_second], axis=3), "filter"
+    )
+    whole_hidden = joined[..., :width]
+    hidden_grad = transpose_mesh(summed(joined[..., width:]))
     _, pullback = jax.vjp(group_silu, pre_first)
     pre_grad = pullback(hidden_grad)[0].astype(jnp.bfloat16)
-    whole_pre_grad = gather_along(pre_grad, "sample")
-    input_grad = (cotangent.astype(jnp.float32) + adjoint_conv(whole_pre_grad, weight_first)).astype(
-        jnp.bfloat16
-    )
+    partial_second = conv_forward(whole_hidden, weight_second).astype(jnp.bfloat16)
+    joined = exchange(jnp.concatenate([partial_second, tiled(pre_grad, "sample")], axis=3), "sample")
+    pre_second = summed(joined[..., :width])
+    whole_pre_grad = joined[..., width:]
+    level_out = (activations.astype(jnp.float32) + pre_second).astype(jnp.bfloat16)
+    terms_first = adjoint_block(whole_pre_grad, weight_first).astype(jnp.bfloat16)
+    data_grad = transpose_mesh(summed(exchange(terms_first, "filter")))
+    input_grad = (cotangent.astype(jnp.float32) + data_grad).astype(jnp.bfloat16)
     grad_second = tap_grad_sum(whole_hidden, whole_cotangent)
     grad_first = tap_grad_sum(whole_input, whole_pre_grad)
     new_master_first, new_moment_first, new_second_first = adam_update(

time: 337 us -> 297 us (0.88)
  waiting for transfers between devices: 154 us -> 120 us
  blocking collectives: 33.2 us -> 53.6 us
  starting transfers between devices: 72.5 us -> 52.1 us
  local copies, waits for them, and re-layouts: 29.6 us -> 19 us
  other arithmetic: 11.7 us -> 15.2 us
    all_to_all x7 -> x4, starting transfers between devices: 49.8 us -> 28.3 us  [exchange(): return lax.all_to_all(payload, axis, 0, 0, tiled=True)]
    all_to_all x1, blocking collectives: 33.2 us -> 53.6 us  [exchange(): return lax.all_to_all(payload, axis, 0, 0, tiled=True)]
    ppermute x4, waiting for transfers between devices: 42.1 us -> 22.2 us  [transpose_mesh(): return lax.ppermute(block, ('sample', 'filter'), pairs)]
    all_to_all x7 -> x4, waiting for transfers between devices: 112 us -> 98.2 us  [exchange(): return lax.all_to_all(payload, axis, 0, 0, tiled=True)]
    unnamed x120 -> x94, local copies, waits for them, and re-layouts: 12.6 us -> 3.38 us
    dot_general x18, matrix products: 11.3 us -> 16.4 us  [tap_grad_sum(): lax.dot_general(shifted, flat_up, (((1,), (1,)), ((0,), (0,))), preferred...]
    concatenate x0 -> x3, other arithmetic: none -> 4.62 us  [the longest x1 2.78 us: per_device(): jnp.concatenate([partial_second, tiled(pre_grad, 'sample')], axis=3)]
    dot_general x18, matrix products: 11.9 us -> 8.46 us  [conv_forward(): jnp.dot(shifted.reshape(samples * height * breadth, depth_in), weight[ker...]
  transfers between devices with their start and end apart: 11 -> 8, of which waited for: 11 -> 7; matrix products, arithmetic and copies ran while one was open for 8% -> 11% of each run, Pallas kernels for 0% -> 0%
where the time goes in v2:
time: 297 us; the launch traced here: 296 us
  waiting for transfers between devices  120 us (40%)
  blocking collectives  53.6 us (18%)
  starting transfers between devices  52.1 us (18%)
  matrix products  33.6 us (11%)
  local copies, waits for them, and re-layouts  19 us (6%)
  other arithmetic  15.2 us (5%)
    all_to_all x4, waiting for transfers between devices, exchange(): return lax.all_to_all(payload, axis, 0, 0, tiled=True)  98.2 us
    all_to_all x1, blocking collectives, exchange(): return lax.all_to_all(payload, axis, 0, 0, tiled=True)  53.6 us
    all_to_all x4, starting transfers between devices, exchange(): return lax.all_to_all(payload, axis, 0, 0, tiled=True)  28.3 us
    ppermute x4, starting transfers between devices, transpose_mesh(): return lax.ppermute(block, ('sample', 'filter'), pairs)  23.9 us
    ppermute x4, waiting for transfers between devices, transpose_mesh(): return lax.ppermute(block, ('sample', 'filter'), pairs)  22.2 us
    dot_general x18, matrix products, tap_grad_sum(): lax.dot_general(shifted, flat_up, (((1,), (1,)), ((0,), (0,))), preferred...  16.4 us
    slice x4, local copies, waits for them, and re-layouts, window(): padded[:, row_start:row_start + height, column_start:column_start + bread...  9.84 us
    dot_general x18, matrix products, adjoint_block(): lax.dot_general(shifted.reshape(samples * height * breadth, depth_out), w...  8.76 us
  transfers between devices with their start and end apart: 8, of which 7 were waited for; matrix products, arithmetic and copies ran while one was open for 11% of the time, Pallas kernels for 0%

profile of v2, /device:TPU:6, one launch (start us, length us, event | category | flops | bytes accessed | tf_op | source)
XLA Modules:
  0.0 295.5 jit_solution(3987177076790964471)
XLA Ops:
  0.6 7.9 %collective-permute-start = (bf16[1,2,128,128]{3,2,1,0:T(8,128)(2,1)}, bf16[1,2,128,128]{3,2,1,0:T(8,128)(2,1)S(1)}, u32[]{:S(2)}, u32[]{:S(2)}) collective-permute-start(bf16[1,2,128,128]{3,2,1,0:T(8,128)(2,1)} %param.8), channel_id=1, source_target_pairs={{0,0},{1,16},{2,32},{3,48},{4,64},{5,80},{6,96},{7,112},{8,128},{9... | collective-permute-start | bytes 196616 | tf_op jit(solution)/shard_map/ppermute | solution.py:89
  8.5 8.0 %collective-permute-done = bf16[1,2,128,128]{3,2,1,0:T(8,128)(2,1)S(1)} collective-permute-done((bf16[1,2,128,128]{3,2,1,0:T(8,128)(2,1)}, bf16[1,2,128,128]{3,2,1,0:T(8,128)(2,1)S(1)}, u32[]{:S(2)}, u32[]{:S(2)}) %collective-permute-start) | collective-permute-done | bytes 65568 | tf_op jit(solution)/shard_map/ppermute | solution.py:89
  16.5 1.2 tile.19
  17.7 9.0 %all-to-all-start = ((bf16[16,2,128,128]{3,2,1,0:T(8,128)(2,1)}), bf16[16,2,128,128]{3,2,1,0:T(8,128)(2,1)S(1)}, u32[]{:S(2)}, u32[]{:S(2)}) async-start(bf16[16,2,128,128]{3,2,1,0:T(8,128)(2,1)} %tile.19), calls=%async_computation | async-start | bytes 2097152 | tf_op jit(solution)/shard_map/all_to_all | solution.py:93
  26.8 27.3 %all-to-all-done = bf16[16,2,128,128]{3,2,1,0:T(8,128)(2,1)S(1)} async-done(((bf16[16,2,128,128]{3,2,1,0:T(8,128)(2,1)}), bf16[16,2,128,128]{3,2,1,0:T(8,128)(2,1)S(1)}, u32[]{:S(2)}, u32[]{:S(2)}) %all-to-all-start) | async-done | bytes 1048608 | tf_op jit(solution)/shard_map/all_to_all | solution.py:93
  54.1 2.4 pad_slice_fusion.24
  61.4 1.6 pad_maximum_fusion
  63.0 6.7 %all-to-all-start.1 = ((bf16[16,2,128,256]{3,2,1,0:T(8,128)(2,1)}), bf16[16,2,128,256]{3,2,1,0:T(8,128)(2,1)}, u32[]{:S(2)}, u32[]{:S(2)}) async-start(bf16[16,2,128,256]{3,2,1,0:T(8,128)(2,1)} %pad_maximum_fusion), calls=%async_computation.1 | async-start | bytes 4194304 | tf_op jit(solution)/shard_map/all_to_all | solution.py:93
  69.8 0.8 convert_element_type.193
  70.5 25.9 %all-to-all-done.1 = bf16[16,2,128,256]{3,2,1,0:T(8,128)(2,1)} async-done(((bf16[16,2,128,256]{3,2,1,0:T(8,128)(2,1)}), bf16[16,2,128,256]{3,2,1,0:T(8,128)(2,1)}, u32[]{:S(2)}, u32[]{:S(2)}) %all-to-all-start.1) | async-done | bytes 2097184 | tf_op jit(solution)/shard_map/all_to_all | solution.py:93
  96.5 1.9 convert_reduce_fusion
  99.3 5.0 %collective-permute-start.1 = (bf16[1,2,128,128]{3,2,1,0:T(8,128)(2,1)S(1)}, bf16[1,2,128,128]{3,2,1,0:T(8,128)(2,1)S(1)}, u32[]{:S(2)}, u32[]{:S(2)}) collective-permute-start(bf16[1,2,128,128]{3,2,1,0:T(8,128)(2,1)S(1)} %multiply_convert_fusion), channel_id=1, source_target_pairs={{0,0},{1,16},{2,32},{3,48},{4,64},{5,80},{6,96},{7,112},{8,128},{9... | collective-permute-start | bytes 196616 | tf_op jit(solution)/shard_map/ppermute | solution.py:89
  104.3 1.3 slice.274
  105.6 2.5 pad_slice_fusion.16
  108.1 0.4 fusion.54
  108.6 0.4 convolution_add_fusion.23
  109.0 0.4 convolution_add_fusion.22
  109.9 0.4 convolution_add_fusion.20
  110.7 0.4 convolution_add_fusion.18
  111.6 0.4 fusion.1
  112.1 2.2 collective-permute-done.1
  114.7 53.6 %all_to_all.25 = bf16[16,2,128,256]{3,2,1,0:T(8,128)(2,1)S(1)} all-to-all(bf16[16,2,128,256]{3,2,1,0:T(8,128)(2,1)S(1)} %pad_maximum_fusion.1), channel_id=1, replica_groups=mesh['sample'=16,'filter'=16] {'filter'}, dimensions={0} | all-to-all | bytes 4194304 | tf_op jit(solution)/shard_map/all_to_all | solution.py:93
  168.5 5.9 %collective-permute-start.2 = (f32[1,2,128,128]{3,2,1,0:T(8,128)S(1)}, f32[1,2,128,128]{3,2,1,0:T(8,128)S(1)}, u32[]{:S(2)}, u32[]{:S(2)}) collective-permute-start(f32[1,2,128,128]{3,2,1,0:T(8,128)S(1)} %bitcast.343), channel_id=1, source_target_pairs={{0,0},{1,16},{2,32},{3,48},{4,64},{5,80},{6,96},{7,112},{8,128},{9... | collective-permute-start | bytes 393224 | tf_op jit(solution)/shard_map/ppermute | solution.py:89
  174.6 2.5 pad_slice_fusion.8
  177.1 1.1 fusion.35
  178.2 0.5 fusion.31
  178.7 1.1 fusion.38
  179.8 1.1 fusion.37
  180.9 1.1 fusion.36
  182.0 1.1 fusion.34
  183.2 0.5 fusion.32
  183.6 0.6 bitcast_dynamic-update-slice_fusion.9
  184.7 0.6 bitcast_dynamic-update-slice_fusion.8
  188.3 1.4 fusion.2
  189.7 1.1 fusion.33
  192.0 2.8 pad_maximum_fusion.2
  194.8 6.8 %all-to-all-start.3 = ((bf16[16,2,128,256]{3,2,1,0:T(8,128)(2,1)}), bf16[16,2,128,256]{3,2,1,0:T(8,128)(2,1)}, u32[]{:S(2)}, u32[]{:S(2)}) async-start(bf16[16,2,128,256]{3,2,1,0:T(8,128)(2,1)} %pad_maximum_fusion.2), calls=%async_computation.3 | async-start | bytes 4194304 | tf_op jit(solution)/shard_map/all_to_all | solution.py:93
  201.7 1.9 fusion.39
  203.7 1.5 multiply_subtract_fusion
  205.2 23.1 %all-to-all-done.3 = bf16[16,2,128,256]{3,2,1,0:T(8,128)(2,1)} async-done(((bf16[16,2,128,256]{3,2,1,0:T(8,128)(2,1)}), bf16[16,2,128,256]{3,2,1,0:T(8,128)(2,1)}, u32[]{:S(2)}, u32[]{:S(2)}) %all-to-all-start.3) | async-done | bytes 2097184 | tf_op jit(solution)/shard_map/all_to_all | solution.py:93
  228.3 1.3 slice.287
  229.6 2.5 pad_slice_fusion
  232.1 0.5 fusion.30
  232.6 0.7 copy-done.11
  233.3 0.5 fusion.29
  233.8 0.5 fusion.28
  234.6 0.5 fusion.27
  235.1 1.1 fusion.26
  236.3 1.1 fusion.25
  237.4 1.1 fusion.24
  238.5 1.1 fusion.23
  239.6 0.5 fusion.22
  240.1 0.4 fusion.51
  241.9 0.4 convolution_add_fusion.4
  242.7 0.4 convolution_add_fusion.2
  243.6 1.4 fusion.3
  245.1 5.7 %all-to-all-start.4 = ((bf16[16,2,128,128]{3,2,1,0:T(8,128)(2,1)}), bf16[16,2,128,128]{3,2,1,0:T(8,128)(2,1)S(1)}, u32[]{:S(2)}, u32[]{:S(2)}) async-start(bf16[16,2,128,128]{3,2,1,0:T(8,128)(2,1)} %bitcast.65), calls=%async_computation.4 | async-start | bytes 2097152 | tf_op jit(solution)/shard_map/all_to_all | solution.py:93
  250.8 1.4 convert_reduce_fusion.3
  252.5 2.5 multiply_subtract_fusion.1
  255.0 21.8 %all-to-all-done.4 = bf16[16,2,128,128]{3,2,1,0:T(8,128)(2,1)S(1)} async-done(((bf16[16,2,128,128]{3,2,1,0:T(8,128)(2,1)}), bf16[16,2,128,128]{3,2,1,0:T(8,128)(2,1)S(1)}, u32[]{:S(2)}, u32[]{:S(2)}) %all-to-all-start.4) | async-done | bytes 1048608 | tf_op jit(solution)/shard_map/all_to_all | solution.py:93
  277.0 5.1 %collective-permute-start.3 = (f32[1,2,128,128]{3,2,1,0:T(8,128)S(1)}, f32[1,2,128,128]{3,2,1,0:T(8,128)S(1)}, u32[]{:S(2)}, u32[]{:S(2)}) collective-permute-start(f32[1,2,128,128]{3,2,1,0:T(8,128)S(1)} %bitcast.344), channel_id=1, source_target_pairs={{0,0},{1,16},{2,32},{3,48},{4,64},{5,80},{6,96},{7,112},{8,128},{9... | collective-permute-start | bytes 393224 | tf_op jit(solution)/shard_map/ppermute | solution.py:89
  282.1 0.6 fusion.49
  282.8 12.1 %collective-permute-done.3 = f32[1,2,128,128]{3,2,1,0:T(8,128)S(1)} collective-permute-done((f32[1,2,128,128]{3,2,1,0:T(8,128)S(1)}, f32[1,2,128,128]{3,2,1,0:T(8,128)S(1)}, u32[]{:S(2)}, u32[]{:S(2)}) %collective-permute-start.3) | collective-permute-done | bytes 131104 | tf_op jit(solution)/shard_map/ppermute | solution.py:89
  294.9 0.6 add_convert_fusion
  (153 shorter events, 15.3 us)
Async XLA Ops:
  0.6 26.1 %copy-start.20 = (f32[9,128,128]{2,1,0:T(8,128)S(1)}, f32[9,128,128]{2,1,0:T(8,128)}, u32[]{:S(2)}) copy-start(f32[9,128,128]{2,1,0:T(8,128)} %param.10) | copy-start | bytes 1769476
  0.6 15.8 %collective-permute-start = (bf16[1,2,128,128]{3,2,1,0:T(8,128)(2,1)}, bf16[1,2,128,128]{3,2,1,0:T(8,128)(2,1)S(1)}, u32[]{:S(2)}, u32[]{:S(2)}) collective-permute-start(bf16[1,2,128,128]{3,2,1,0:T(8,128)(2,1)} %param.8), channel_id=1, source_target_pairs={{0,0},{1,16},{2,32},{3,48},{4,64},{5,80},{6,96},{7,112},{8,128},{9... | collective-permute-start | bytes 196616 | tf_op jit(solution)/shard_map/ppermute | solution.py:89
  17.7 36.4 %all-to-all-start = ((bf16[16,2,128,128]{3,2,1,0:T(8,128)(2,1)}), bf16[16,2,128,128]{3,2,1,0:T(8,128)(2,1)S(1)}, u32[]{:S(2)}, u32[]{:S(2)}) async-start(bf16[16,2,128,128]{3,2,1,0:T(8,128)(2,1)} %tile.19), calls=%async_computation | async-start | bytes 2097152 | tf_op jit(solution)/shard_map/all_to_all | solution.py:93
  26.7 33.6 %copy-start.15 = (bf16[9,128,128]{2,1,0:T(8,128)(2,1)}, bf16[9,128,128]{2,1,0:T(8,128)(2,1)S(1)}, u32[]{:S(2)}) copy-start(bf16[9,128,128]{2,1,0:T(8,128)(2,1)S(1)} %convert_element_type.188) | copy-start | bytes 884740
  56.5 1.0 copy-start
  56.5 1.3 copy-start.2
  56.5 1.7 copy-start.4
  56.5 2.6 copy-start.6
  56.5 3.0 %copy-start.8 = (bf16[16,2,128,128]{3,2,1,0:T(8,128)(2,1)}, bf16[16,2,128,128]{3,2,1,0:T(8,128)(2,1)S(1)}, u32[]{:S(2)}) copy-start(bf16[16,2,128,128]{3,2,1,0:T(8,128)(2,1)S(1)} %get-tuple-element.55) | copy-start | bytes 3145732
  56.5 3.4 %copy-start.10 = (bf16[16,2,128,128]{3,2,1,0:T(8,128)(2,1)}, bf16[16,2,128,128]{3,2,1,0:T(8,128)(2,1)S(1)}, u32[]{:S(2)}) copy-start(bf16[16,2,128,128]{3,2,1,0:T(8,128)(2,1)S(1)} %get-tuple-element.56) | copy-start | bytes 3145732
  56.5 3.8 %copy-start.12 = (bf16[16,2,128,128]{3,2,1,0:T(8,128)(2,1)}, bf16[16,2,128,128]{3,2,1,0:T(8,128)(2,1)S(1)}, u32[]{:S(2)}) copy-start(bf16[16,2,128,128]{3,2,1,0:T(8,128)(2,1)S(1)} %get-tuple-element.50) | copy-start | bytes 3145732
  60.4 0.8 copy-start.36
  63.0 6.7 %copy-start.18 = (f32[9,128,128]{2,1,0:T(8,128)S(1)}, f32[9,128,128]{2,1,0:T(8,128)}, u32[]{:S(2)}) copy-start(f32[9,128,128]{2,1,0:T(8,128)} %param.13) | copy-start | bytes 1769476
  63.0 33.4 %all-to-all-start.1 = ((bf16[16,2,128,256]{3,2,1,0:T(8,128)(2,1)}), bf16[16,2,128,256]{3,2,1,0:T(8,128)(2,1)}, u32[]{:S(2)}, u32[]{:S(2)}) async-start(bf16[16,2,128,256]{3,2,1,0:T(8,128)(2,1)} %pad_maximum_fusion), calls=%async_computation.1 | async-start | bytes 4194304 | tf_op jit(solution)/shard_map/all_to_all | solution.py:93
  99.3 15.0 %collective-permute-start.1 = (bf16[1,2,128,128]{3,2,1,0:T(8,128)(2,1)S(1)}, bf16[1,2,128,128]{3,2,1,0:T(8,128)(2,1)S(1)}, u32[]{:S(2)}, u32[]{:S(2)}) collective-permute-start(bf16[1,2,128,128]{3,2,1,0:T(8,128)(2,1)S(1)} %multiply_convert_fusion), channel_id=1, source_target_pairs={{0,0},{1,16},{2,32},{3,48},{4,64},{5,80},{6,96},{7,112},{8,128},{9... | collective-permute-start | bytes 196616 | tf_op jit(solution)/shard_map/ppermute | solution.py:89
  105.6 2.5 copy-start.17
  168.5 22.3 %collective-permute-start.2 = (f32[1,2,128,128]{3,2,1,0:T(8,128)S(1)}, f32[1,2,128,128]{3,2,1,0:T(8,128)S(1)}, u32[]{:S(2)}, u32[]{:S(2)}) collective-permute-start(f32[1,2,128,128]{3,2,1,0:T(8,128)S(1)} %bitcast.343), channel_id=1, source_target_pairs={{0,0},{1,16},{2,32},{3,48},{4,64},{5,80},{6,96},{7,112},{8,128},{9... | collective-permute-start | bytes 393224 | tf_op jit(solution)/shard_map/ppermute | solution.py:89
  177.1 11.2 %copy-start.14 = (bf16[16,2,128,128]{3,2,1,0:T(8,128)(2,1)}, bf16[16,2,128,128]{3,2,1,0:T(8,128)(2,1)S(1)}, u32[]{:S(2)}) copy-start(bf16[16,2,128,128]{3,2,1,0:T(8,128)(2,1)S(1)} %get-tuple-element.34) | copy-start | bytes 3145732
  194.8 8.8 %copy-start.31 = (f32[128,128]{1,0:T(8,128)S(1)}, f32[128,128]{1,0:T(8,128)}, u32[]{:S(2)}) copy-start(f32[128,128]{1,0:T(8,128)} %fusion.33) | copy-start | bytes 196612
  194.8 8.8 %copy-start.30 = (f32[128,128]{1,0:T(8,128)S(1)}, f32[128,128]{1,0:T(8,128)}, u32[]{:S(2)}) copy-start(f32[128,128]{1,0:T(8,128)} %fusion.34) | copy-start | bytes 196612
  194.8 8.8 %copy-start.28 = (f32[128,128]{1,0:T(8,128)S(1)}, f32[128,128]{1,0:T(8,128)}, u32[]{:S(2)}) copy-start(f32[128,128]{1,0:T(8,128)} %fusion.35) | copy-start | bytes 196612
  194.8 33.5 %all-to-all-start.3 = ((bf16[16,2,128,256]{3,2,1,0:T(8,128)(2,1)}), bf16[16,2,128,256]{3,2,1,0:T(8,128)(2,1)}, u32[]{:S(2)}, u32[]{:S(2)}) async-start(bf16[16,2,128,256]{3,2,1,0:T(8,128)(2,1)} %pad_maximum_fusion.2), calls=%async_computation.3 | async-start | bytes 4194304 | tf_op jit(solution)/shard_map/all_to_all | solution.py:93
  201.6 2.0 copy-start.22
  201.6 2.0 copy-start.29
  201.6 2.0 copy-start.27
  201.6 2.1 copy-start.26
  201.6 2.1 copy-start.19
  201.6 2.1 copy-start.23
  201.7 2.1 copy-start.24
  229.6 2.5 copy-start.13
  232.1 1.2 copy-start.11
  232.1 1.7 copy-start.9
  233.3 1.3 copy-start.7
  234.6 1.6 copy-start.5
  235.1 2.2 copy-start.3
  236.3 2.2 copy-start.1
  238.5 1.6 copy-start.16
  245.0 5.8 %copy-start.35 = (f32[128,128]{1,0:T(8,128)S(1)}, f32[128,128]{1,0:T(8,128)}, u32[]{:S(2)}) copy-start(f32[128,128]{1,0:T(8,128)} %fusion.23) | copy-start | bytes 196612
  245.0 7.2 %copy-start.33 = (f32[128,128]{1,0:T(8,128)S(1)}, f32[128,128]{1,0:T(8,128)}, u32[]{:S(2)}) copy-start(f32[128,128]{1,0:T(8,128)} %fusion.26) | copy-start | bytes 196612
  245.1 7.3 %copy-start.34 = (f32[128,128]{1,0:T(8,128)S(1)}, f32[128,128]{1,0:T(8,128)}, u32[]{:S(2)}) copy-start(f32[128,128]{1,0:T(8,128)} %fusion.24) | copy-start | bytes 196612
  245.1 7.3 %copy-start.32 = (f32[128,128]{1,0:T(8,128)S(1)}, f32[128,128]{1,0:T(8,128)}, u32[]{:S(2)}) copy-start(f32[128,128]{1,0:T(8,128)} %fusion.25) | copy-start | bytes 196612
  245.1 7.4 %copy-start.21 = (f32[9,128,128]{2,1,0:T(8,128)S(1)}, f32[9,128,128]{2,1,0:T(8,128)}, u32[]{:S(2)}) copy-start(f32[9,128,128]{2,1,0:T(8,128)} %param.10) | copy-start | bytes 1769476
  245.1 7.4 %copy-start.25 = (f32[9,128,128]{2,1,0:T(8,128)S(1)}, f32[9,128,128]{2,1,0:T(8,128)}, u32[]{:S(2)}) copy-start(f32[9,128,128]{2,1,0:T(8,128)} %param.11) | copy-start | bytes 1769476
  245.1 31.8 %all-to-all-start.4 = ((bf16[16,2,128,128]{3,2,1,0:T(8,128)(2,1)}), bf16[16,2,128,128]{3,2,1,0:T(8,128)(2,1)S(1)}, u32[]{:S(2)}, u32[]{:S(2)}) async-start(bf16[16,2,128,128]{3,2,1,0:T(8,128)(2,1)} %bitcast.65), calls=%async_computation.4 | async-start | bytes 2097152 | tf_op jit(solution)/shard_map/all_to_all | solution.py:93
  252.5 29.7 %copy-start.38 = (bf16[1,2,128,128]{3,2,1,0:T(8,128)(2,1)S(1)}, bf16[1,2,128,128]{3,2,1,0:T(8,128)(2,1)}, u32[]{:S(2)}) copy-start(bf16[1,2,128,128]{3,2,1,0:T(8,128)(2,1)} %param.8) | copy-start | bytes 196612
  252.5 42.4 %copy-start.37 = (bf16[1,2,128,128]{3,2,1,0:T(8,128)(2,1)S(1)}, bf16[1,2,128,128]{3,2,1,0:T(8,128)(2,1)}, u32[]{:S(2)}) copy-start(bf16[1,2,128,128]{3,2,1,0:T(8,128)(2,1)} %param.9) | copy-start | bytes 196612
  277.0 17.9 %collective-permute-start.3 = (f32[1,2,128,128]{3,2,1,0:T(8,128)S(1)}, f32[1,2,128,128]{3,2,1,0:T(8,128)S(1)}, u32[]{:S(2)}, u32[]{:S(2)}) collective-permute-start(f32[1,2,128,128]{3,2,1,0:T(8,128)S(1)} %bitcast.344), channel_id=1, source_target_pairs={{0,0},{1,16},{2,32},{3,48},{4,64},{5,80},{6,96},{7,112},{8,128},{9... | collective-permute-start | bytes 393224 | tf_op jit(solution)/shard_map/ppermute | solution.py:89

commit v3 on v2

--- a/solution.py
+++ b/solution.py
@@ -112,31 +112,40 @@
     second_second,
 ):
     weight_first = master_first.astype(jnp.bfloat16)
-    weight_second = master_second.astype(jnp.bfloat16)
+    swapped_second = transpose_mesh(master_second.astype(jnp.bfloat16))
     width = activations.shape[3]
-    whole_input = exchange(tiled(transpose_mesh(activations), "filter"), "filter")
+    joined = exchange(
+        jnp.concatenate(
+            [tiled(transpose_mesh(activations), "filter"), tiled(transpose_mesh(cotangent), "filter")],
+            axis=3,
+        ),
+        "filter",
+    )
+    whole_input = joined[..., :width]
+    whole_cotangent = joined[..., width:]
     partial_first = conv_forward(whole_input, weight_first).astype(jnp.bfloat16)
-    joined = exchange(jnp.concatenate([tiled(cotangent, "sample"), partial_first], axis=3), "sample")
-    whole_cotangent = joined[..., :width]
-    pre_first = summed(joined[..., width:])
+    terms_second = adjoint_block(whole_cotangent, swapped_second).astype(jnp.bfloat16)
+    joined = exchange(jnp.concatenate([partial_first, terms_second], axis=3), "sample")
+    pre_first = summed(joined[..., :width])
+    hidden_grad = summed(joined[..., width:])
     hidden = group_silu(pre_first).astype(jnp.bfloat16)
-    terms_second = adjoint_block(whole_cotangent, weight_second).astype(jnp.bfloat16)
+    _, pullback = jax.vjp(group_silu, pre_first)
+    pre_grad = pullback(hidden_grad)[0].astype(jnp.bfloat16)
     joined = exchange(
-        jnp.concatenate([tiled(transpose_mesh(hidden), "filter"), terms_second], axis=3), "filter"
+        jnp.concatenate([tiled(hidden, "sample"), tiled(pre_grad, "sample")], axis=3), "sample"
     )
     whole_hidden = joined[..., :width]
-    hidden_grad = transpose_mesh(summed(joined[..., width:]))
-    _, pullback = jax.vjp(group_silu, pre_first)
-    pre_grad = pullback(hidden_grad)[0].astype(jnp.bfloat16)
-    partial_second = conv_forward(whole_hidden, weight_second).astype(jnp.bfloat16)
-    joined = exchange(jnp.concatenate([partial_second, tiled(pre_grad, "sample")], axis=3), "sample")
-    pre_second = summed(joined[..., :width])
     whole_pre_grad = joined[..., width:]
+    partial_second = conv_forward(whole_hidden, swapped_second).astype(jnp.bfloat16)
+    terms_first = adjoint_block(whole_pre_grad, weight_first).astype(jnp.bfloat16)
+    joined = transpose_mesh(
+        summed(exchange(jnp.concatenate([partial_second, terms_first], axis=3), "filter"))
+    )
+    pre_second = joined[..., :width]
+    data_grad = joined[..., width:]
     level_out = (activations.astype(jnp.float32) + pre_second).astype(jnp.bfloat16)
-    terms_first = adjoint_block(whole_pre_grad, weight_first).astype(jnp.bfloat16)
-    data_grad = transpose_mesh(summed(exchange(terms_first, "filter")))
     input_grad = (cotangent.astype(jnp.float32) + data_grad).astype(jnp.bfloat16)
-    grad_second = tap_grad_sum(whole_hidden, whole_cotangent)
+    grad_second = transpose_mesh(tap_grad_sum(whole_hidden, whole_cotangent))
     grad_first = tap_grad_sum(whole_input, whole_pre_grad)
     new_master_first, new_moment_first, new_second_first = adam_update(
         master_first, moment_first, second_first, grad_first

time: 297 us -> 355 us (1.20)
  waiting for transfers between devices: 120 us -> 175 us
  blocking collectives: 53.6 us -> 65.9 us
  starting transfers between devices: 52.1 us -> 46.1 us
  matrix products: 33.6 us -> 29.5 us
    ppermute x4 -> x5, waiting for transfers between devices: 22.2 us -> 104 us  [transpose_mesh(): return lax.ppermute(block, ('sample', 'filter'), pairs)]
    all_to_all x4 -> x2, waiting for transfers between devices: 98.2 us -> 70.1 us  [exchange(): return lax.all_to_all(payload, axis, 0, 0, tiled=True)]
    all_to_all x4 -> x2, starting transfers between devices: 28.3 us -> 14.2 us  [exchange(): return lax.all_to_all(payload, axis, 0, 0, tiled=True)]
    all_to_all x1 -> x2, blocking collectives: 53.6 us -> 65.9 us  [exchange(): return lax.all_to_all(payload, axis, 0, 0, tiled=True)]
    ppermute x4 -> x5, starting transfers between devices: 23.9 us -> 31.9 us  [transpose_mesh(): return lax.ppermute(block, ('sample', 'filter'), pairs)]
    unnamed x94 -> x86, local copies, waits for them, and re-layouts: 3.38 us -> 8.11 us
    slice x4 -> x3, local copies, waits for them, and re-layouts: 9.84 us -> 9.4 us  [window(): padded[:, row_start:row_start + height, column_start:column_start + bread...]
  transfers between devices with their start and end apart: 8 -> 7, of which waited for: 7 -> 7; matrix products, arithmetic and copies ran while one was open for 11% -> 7% of each run, Pallas kernels for 0% -> 0%
where the time goes in v3:
time: 355 us; the launch traced here: 352 us
  waiting for transfers between devices  175 us (49%)
  blocking collectives  65.9 us (19%)
  starting transfers between devices  46.1 us (13%)
  matrix products  29.5 us (8%)
  local copies, waits for them, and re-layouts  22.2 us (6%)
  other arithmetic  12.7 us (4%)
    ppermute x5, waiting for transfers between devices, transpose_mesh(): return lax.ppermute(block, ('sample', 'filter'), pairs)  104 us
    all_to_all x2, waiting for transfers between devices, exchange(): return lax.all_to_all(payload, axis, 0, 0, tiled=True)  70.1 us
    all_to_all x2, blocking collectives, exchange(): return lax.all_to_all(payload, axis, 0, 0, tiled=True)  65.9 us
    ppermute x5, starting transfers between devices, transpose_mesh(): return lax.ppermute(block, ('sample', 'filter'), pairs)  31.9 us
    all_to_all x2, starting transfers between devices, exchange(): return lax.all_to_all(payload, axis, 0, 0, tiled=True)  14.2 us
    dot_general x18, matrix products, tap_grad_sum(): lax.dot_general(shifted, flat_up, (((1,), (1,)), ((0,), (0,))), preferred...  13.1 us
    slice x3, local copies, waits for them, and re-layouts, window(): padded[:, row_start:row_start + height, column_start:column_start + bread...  9.4 us
    dot_general x18, matrix products, adjoint_block(): lax.dot_general(shifted.reshape(samples * height * breadth, depth_out), w...  8.33 us
  transfers between devices with their start and end apart: 7, of which 7 were waited for; matrix products, arithmetic and copies ran while one was open for 7% of the time, Pallas kernels for 0%

profile of v3, /device:TPU:6, one launch (start us, length us, event | category | flops | bytes accessed | tf_op | source)
XLA Modules:
  0.0 352.3 jit_solution(6769671056199650604)
XLA Ops:
  0.6 7.7 %collective-permute-start = (bf16[1,2,128,128]{3,2,1,0:T(8,128)(2,1)}, bf16[1,2,128,128]{3,2,1,0:T(8,128)(2,1)S(1)}, u32[]{:S(2)}, u32[]{:S(2)}) collective-permute-start(bf16[1,2,128,128]{3,2,1,0:T(8,128)(2,1)} %param.8), channel_id=1, source_target_pairs={{0,0},{1,16},{2,32},{3,48},{4,64},{5,80},{6,96},{7,112},{8,128},{9... | collective-permute-start | bytes 196616 | tf_op jit(solution)/shard_map/ppermute | solution.py:89
  8.4 3.5 %collective-permute-start.1 = (bf16[1,2,128,128]{3,2,1,0:T(8,128)(2,1)}, bf16[1,2,128,128]{3,2,1,0:T(8,128)(2,1)S(1)}, u32[]{:S(2)}, u32[]{:S(2)}) collective-permute-start(bf16[1,2,128,128]{3,2,1,0:T(8,128)(2,1)} %param.9), channel_id=1, source_target_pairs={{0,0},{1,16},{2,32},{3,48},{4,64},{5,80},{6,96},{7,112},{8,128},{9... | collective-permute-start | bytes 196616 | tf_op jit(solution)/shard_map/ppermute | solution.py:89
  11.9 4.4 %collective-permute-done = bf16[1,2,128,128]{3,2,1,0:T(8,128)(2,1)S(1)} collective-permute-done((bf16[1,2,128,128]{3,2,1,0:T(8,128)(2,1)}, bf16[1,2,128,128]{3,2,1,0:T(8,128)(2,1)S(1)}, u32[]{:S(2)}, u32[]{:S(2)}) %collective-permute-start) | collective-permute-done | bytes 65568 | tf_op jit(solution)/shard_map/ppermute | solution.py:89
  16.3 5.1 %collective-permute-done.1 = bf16[1,2,128,128]{3,2,1,0:T(8,128)(2,1)S(1)} collective-permute-done((bf16[1,2,128,128]{3,2,1,0:T(8,128)(2,1)}, bf16[1,2,128,128]{3,2,1,0:T(8,128)(2,1)S(1)}, u32[]{:S(2)}, u32[]{:S(2)}) %collective-permute-start.1) | collective-permute-done | bytes 65568 | tf_op jit(solution)/shard_map/ppermute | solution.py:89
  21.9 1.6 pad_maximum_fusion
  23.5 8.3 %all-to-all-start = ((bf16[16,2,128,256]{3,2,1,0:T(8,128)(2,1)}), bf16[16,2,128,256]{3,2,1,0:T(8,128)(2,1)}, u32[]{:S(2)}, u32[]{:S(2)}) async-start(bf16[16,2,128,256]{3,2,1,0:T(8,128)(2,1)} %pad_maximum_fusion), calls=%async_computation | async-start | bytes 4194304 | tf_op jit(solution)/shard_map/all_to_all | solution.py:93
  31.8 0.8 convert_element_type.188
  32.6 6.8 %collective-permute-start.2 = (bf16[9,128,128]{2,1,0:T(8,128)(2,1)}, bf16[9,128,128]{2,1,0:T(8,128)(2,1)S(1)}, u32[]{:S(2)}, u32[]{:S(2)}) collective-permute-start(bf16[9,128,128]{2,1,0:T(8,128)(2,1)} %convert_element_type.188), channel_id=1, source_target_pairs={{0,0},{1,16},{2,32},{3,48},{4,64},{5,80},{6,96},{7,112},{8,128},{9... | collective-permute-start | bytes 884744 | tf_op jit(solution)/shard_map/ppermute | solution.py:89
  39.4 40.4 %all-to-all-done = bf16[16,2,128,256]{3,2,1,0:T(8,128)(2,1)} async-done(((bf16[16,2,128,256]{3,2,1,0:T(8,128)(2,1)}), bf16[16,2,128,256]{3,2,1,0:T(8,128)(2,1)}, u32[]{:S(2)}, u32[]{:S(2)}) %all-to-all-start) | async-done | bytes 2097184 | tf_op jit(solution)/shard_map/all_to_all | solution.py:93
  79.8 1.8 fusion.83
  81.6 4.4 %pad_slice_fusion.23 = (bf16[16,2,128,128]{3,2,1,0:T(8,128)(2,1)S(1)}, bf16[16,2,128,128]{3,2,1,0:T(8,128)(2,1)S(1)}, bf16[16,2,128,128]{3,2,1,0:T(8,128)(2,1)S(...) fusion(bf16[16,2,128,128]{3,2,1,0:T(8,128)(2,1)S(1)} %get-tuple, ...), kind=kLoop, calls=%fused_computation.59 | loop fusion | bytes 18874368 | tf_op jit(solution)/shard_map/slice | solution.py:22
  90.7 21.5 %collective-permute-done.2 = bf16[9,128,128]{2,1,0:T(8,128)(2,1)S(1)} collective-permute-done((bf16[9,128,128]{2,1,0:T(8,128)(2,1)}, bf16[9,128,128]{2,1,0:T(8,128)(2,1)S(1)}, u32[]{:S(2)}, u32[]{:S(2)}) %collective-permute-start.2) | collective-permute-done | bytes 294944 | tf_op jit(solution)/shard_map/ppermute | solution.py:89
  113.0 0.4 fusion.65
  114.3 0.4 fusion.73
  114.8 0.4 fusion.75
  115.2 0.4 fusion.77
  115.6 1.0 fusion.14
  116.9 34.1 %all_to_all.20 = bf16[16,2,128,256]{3,2,1,0:T(8,128)(2,1)S(1)} all-to-all(bf16[16,2,128,256]{3,2,1,0:T(8,128)(2,1)S(1)} %pad_maximum_fusion.1), channel_id=1, replica_groups=mesh['sample'=16,'filter'=16] {'sample'}, dimensions={0} | all-to-all | bytes 4194304 | tf_op jit(solution)/shard_map/all_to_all | solution.py:93
  151.0 0.9 convert_reduce_fusion.3
  154.4 31.8 %all_to_all.21 = bf16[16,2,128,256]{3,2,1,0:T(8,128)(2,1)S(1)} all-to-all(bf16[16,2,128,256]{3,2,1,0:T(8,128)(2,1)S(1)} %pad_maximum_fusion.2), channel_id=1, replica_groups=mesh['sample'=16,'filter'=16] {'sample'}, dimensions={0} | all-to-all | bytes 4194304 | tf_op jit(solution)/shard_map/all_to_all | solution.py:93
  186.6 2.5 pad_slice_fusion.15
  189.1 1.1 fusion.49
  190.2 0.5 fusion.53
  190.7 1.1 fusion.52
  191.8 1.1 fusion.51
  192.9 1.1 fusion.50
  194.1 1.1 fusion.48
  195.2 1.1 fusion.47
  196.3 1.1 fusion.46
  197.4 0.5 fusion.45
  197.9 0.6 bitcast_dynamic-update-slice_fusion.8
  198.5 2.6 pad_slice_fusion
  202.0 0.4 convolution_add_fusion.6
  202.8 0.4 convolution_add_fusion.4
  205.0 0.5 copy-done.21
  208.9 1.0 fusion.15
  209.9 1.5 pad_maximum_fusion.3
  211.5 5.9 %all-to-all-start.3 = ((bf16[16,2,128,256]{3,2,1,0:T(8,128)(2,1)}), bf16[16,2,128,256]{3,2,1,0:T(8,128)(2,1)}, u32[]{:S(2)}, u32[]{:S(2)}) async-start(bf16[16,2,128,256]{3,2,1,0:T(8,128)(2,1)} %pad_maximum_fusion.3), calls=%async_computation.3 | async-start | bytes 4194304 | tf_op jit(solution)/shard_map/all_to_all | solution.py:93
  217.4 0.5 fusion.44
  218.1 0.6 bitcast_dynamic-update-slice_fusion.7
  218.8 0.6 bitcast_dynamic-update-slice_fusion.6
  219.4 0.6 bitcast_dynamic-update-slice_fusion.5
  220.1 0.6 bitcast_dynamic-update-slice_fusion.4
  220.7 0.6 bitcast_dynamic-update-slice_fusion.3
  221.3 0.6 bitcast_dynamic-update-slice_fusion.2
  222.0 0.6 bitcast_dynamic-update-slice_fusion.1
  222.6 0.6 bitcast_dynamic-update-slice_fusion
  223.2 0.5 fusion.43
  223.7 6.1 %collective-permute-start.4 = (f32[9,128,128]{2,1,0:T(8,128)}, f32[9,128,128]{2,1,0:T(8,128)}, u32[]{:S(2)}, u32[]{:S(2)}) collective-permute-start(f32[9,128,128]{2,1,0:T(8,128)} %bitcast_dynamic-update-slice_fusion), channel_id=1, source_target_pairs={{0,0},{1,16},{2,32},{3,48},{4,64},{5,80},{6,96},{7,112},{8,128},{9... | collective-permute-start | bytes 1769480 | tf_op jit(solution)/shard_map/ppermute | solution.py:89
  229.8 0.5 fusion.42
  230.3 0.5 fusion.41
  230.8 0.5 fusion.40
  231.6 0.5 fusion.39
  232.1 0.5 fusion.38
  232.9 0.5 fusion.37
  233.4 0.5 fusion.36
  234.8 1.5 multiply_subtract_fusion.1
  236.3 29.7 %all-to-all-done.3 = bf16[16,2,128,256]{3,2,1,0:T(8,128)(2,1)} async-done(((bf16[16,2,128,256]{3,2,1,0:T(8,128)(2,1)}), bf16[16,2,128,256]{3,2,1,0:T(8,128)(2,1)}, u32[]{:S(2)}, u32[]{:S(2)}) %all-to-all-start.3) | async-done | bytes 2097184 | tf_op jit(solution)/shard_map/all_to_all | solution.py:93
  265.9 1.9 convert_reduce_fusion
  267.9 7.8 %collective-permute-start.3 = (f32[1,2,128,256]{3,2,1,0:T(8,128)S(1)}, f32[1,2,128,256]{3,2,1,0:T(8,128)S(1)}, u32[]{:S(2)}, u32[]{:S(2)}) collective-permute-start(f32[1,2,128,256]{3,2,1,0:T(8,128)S(1)} %bitcast.319), channel_id=1, source_target_pairs={{0,0},{1,16},{2,32},{3,48},{4,64},{5,80},{6,96},{7,112},{8,128},{9... | collective-permute-start | bytes 786440 | tf_op jit(solution)/shard_map/ppermute | solution.py:89
  275.7 68.6 %collective-permute-done.4 = f32[9,128,128]{2,1,0:T(8,128)} collective-permute-done((f32[9,128,128]{2,1,0:T(8,128)}, f32[9,128,128]{2,1,0:T(8,128)}, u32[]{:S(2)}, u32[]{:S(2)}) %collective-permute-start.4) | collective-permute-done | bytes 589856 | tf_op jit(solution)/shard_map/ppermute | solution.py:89
  344.3 2.5 multiply_subtract_fusion
  346.8 4.9 %collective-permute-done.3 = f32[1,2,128,256]{3,2,1,0:T(8,128)S(1)} collective-permute-done((f32[1,2,128,256]{3,2,1,0:T(8,128)S(1)}, f32[1,2,128,256]{3,2,1,0:T(8,128)S(1)}, u32[]{:S(2)}, u32[]{:S(2)}) %collective-permute-start.3) | collective-permute-done | bytes 262176 | tf_op jit(solution)/shard_map/ppermute | solution.py:89
  351.7 0.7 fusion.58
  (138 shorter events, 18.0 us)
Async XLA Ops:
  0.6 15.7 %collective-permute-start = (bf16[1,2,128,128]{3,2,1,0:T(8,128)(2,1)}, bf16[1,2,128,128]{3,2,1,0:T(8,128)(2,1)S(1)}, u32[]{:S(2)}, u32[]{:S(2)}) collective-permute-start(bf16[1,2,128,128]{3,2,1,0:T(8,128)(2,1)} %param.8), channel_id=1, source_target_pairs={{0,0},{1,16},{2,32},{3,48},{4,64},{5,80},{6,96},{7,112},{8,128},{9... | collective-permute-start | bytes 196616 | tf_op jit(solution)/shard_map/ppermute | solution.py:89
  8.4 13.1 %collective-permute-start.1 = (bf16[1,2,128,128]{3,2,1,0:T(8,128)(2,1)}, bf16[1,2,128,128]{3,2,1,0:T(8,128)(2,1)S(1)}, u32[]{:S(2)}, u32[]{:S(2)}) collective-permute-start(bf16[1,2,128,128]{3,2,1,0:T(8,128)(2,1)} %param.9), channel_id=1, source_target_pairs={{0,0},{1,16},{2,32},{3,48},{4,64},{5,80},{6,96},{7,112},{8,128},{9... | collective-permute-start | bytes 196616 | tf_op jit(solution)/shard_map/ppermute | solution.py:89
  23.5 8.3 %copy-start.18 = (f32[9,128,128]{2,1,0:T(8,128)S(1)}, f32[9,128,128]{2,1,0:T(8,128)}, u32[]{:S(2)}) copy-start(f32[9,128,128]{2,1,0:T(8,128)} %param.13) | copy-start | bytes 1769476
  23.5 15.9 %copy-start.16 = (f32[9,128,128]{2,1,0:T(8,128)S(1)}, f32[9,128,128]{2,1,0:T(8,128)}, u32[]{:S(2)}) copy-start(f32[9,128,128]{2,1,0:T(8,128)} %param.10) | copy-start | bytes 1769476
  23.5 56.3 %all-to-all-start = ((bf16[16,2,128,256]{3,2,1,0:T(8,128)(2,1)}), bf16[16,2,128,256]{3,2,1,0:T(8,128)(2,1)}, u32[]{:S(2)}, u32[]{:S(2)}) async-start(bf16[16,2,128,256]{3,2,1,0:T(8,128)(2,1)} %pad_maximum_fusion), calls=%async_computation | async-start | bytes 4194304 | tf_op jit(solution)/shard_map/all_to_all | solution.py:93
  32.6 79.6 %collective-permute-start.2 = (bf16[9,128,128]{2,1,0:T(8,128)(2,1)}, bf16[9,128,128]{2,1,0:T(8,128)(2,1)S(1)}, u32[]{:S(2)}, u32[]{:S(2)}) collective-permute-start(bf16[9,128,128]{2,1,0:T(8,128)(2,1)} %convert_element_type.188), channel_id=1, source_target_pairs={{0,0},{1,16},{2,32},{3,48},{4,64},{5,80},{6,96},{7,112},{8,128},{9... | collective-permute-start | bytes 884744 | tf_op jit(solution)/shard_map/ppermute | solution.py:89
  86.0 1.0 copy-start
  86.0 1.3 copy-start.2
  86.0 1.7 copy-start.4
  86.0 2.1 copy-start.6
  86.0 2.9 copy-start.8
  86.0 3.3 copy-start.10
  86.0 3.8 %copy-start.12 = (bf16[16,2,128,128]{3,2,1,0:T(8,128)(2,1)}, bf16[16,2,128,128]{3,2,1,0:T(8,128)(2,1)S(1)}, u32[]{:S(2)}) copy-start(bf16[16,2,128,128]{3,2,1,0:T(8,128)(2,1)S(1)} %get-tuple-element.60) | copy-start | bytes 3145732
  86.0 4.2 %copy-start.14 = (bf16[16,2,128,128]{3,2,1,0:T(8,128)(2,1)}, bf16[16,2,128,128]{3,2,1,0:T(8,128)(2,1)S(1)}, u32[]{:S(2)}) copy-start(bf16[16,2,128,128]{3,2,1,0:T(8,128)(2,1)S(1)} %get-tuple-element.66) | copy-start | bytes 3145732
  112.2 3.5 copy-start.20
  204.6 1.0 copy-start.21
  211.5 5.9 %copy-start.15 = (bf16[16,2,128,128]{3,2,1,0:T(8,128)(2,1)S(1)}, bf16[16,2,128,128]{3,2,1,0:T(8,128)(2,1)}, u32[]{:S(2)}) copy-start(bf16[16,2,128,128]{3,2,1,0:T(8,128)(2,1)} %copy-done.14) | copy-start | bytes 3145732
  211.5 54.5 %all-to-all-start.3 = ((bf16[16,2,128,256]{3,2,1,0:T(8,128)(2,1)}), bf16[16,2,128,256]{3,2,1,0:T(8,128)(2,1)}, u32[]{:S(2)}, u32[]{:S(2)}) async-start(bf16[16,2,128,256]{3,2,1,0:T(8,128)(2,1)} %pad_maximum_fusion.3), calls=%async_computation.3 | async-start | bytes 4194304 | tf_op jit(solution)/shard_map/all_to_all | solution.py:93
  217.3 0.8 copy-start.32
  217.3 1.5 copy-start.31
  217.3 2.1 copy-start.30
  217.3 2.7 copy-start.28
  217.4 3.3 copy-start.29
  217.4 4.0 %copy-start.27 = (f32[128,128]{1,0:T(8,128)S(1)}, f32[128,128]{1,0:T(8,128)}, u32[]{:S(2)}) copy-start(f32[128,128]{1,0:T(8,128)} %fusion.51) | copy-start | bytes 196612
  217.4 4.6 %copy-start.26 = (f32[128,128]{1,0:T(8,128)S(1)}, f32[128,128]{1,0:T(8,128)}, u32[]{:S(2)}) copy-start(f32[128,128]{1,0:T(8,128)} %fusion.52) | copy-start | bytes 196612
  217.4 5.9 %copy-start.13 = (bf16[16,2,128,128]{3,2,1,0:T(8,128)(2,1)S(1)}, bf16[16,2,128,128]{3,2,1,0:T(8,128)(2,1)}, u32[]{:S(2)}) copy-start(bf16[16,2,128,128]{3,2,1,0:T(8,128)(2,1)} %copy-done.12) | copy-start | bytes 3145732
  218.1 11.7 %copy-start.11 = (bf16[16,2,128,128]{3,2,1,0:T(8,128)(2,1)S(1)}, bf16[16,2,128,128]{3,2,1,0:T(8,128)(2,1)}, u32[]{:S(2)}) copy-start(bf16[16,2,128,128]{3,2,1,0:T(8,128)(2,1)} %copy-done.10) | copy-start | bytes 3145732
  223.2 7.1 %copy-start.9 = (bf16[16,2,128,128]{3,2,1,0:T(8,128)(2,1)S(1)}, bf16[16,2,128,128]{3,2,1,0:T(8,128)(2,1)}, u32[]{:S(2)}) copy-start(bf16[16,2,128,128]{3,2,1,0:T(8,128)(2,1)} %copy-done.8) | copy-start | bytes 3145732
  223.7 120.5 %collective-permute-start.4 = (f32[9,128,128]{2,1,0:T(8,128)}, f32[9,128,128]{2,1,0:T(8,128)}, u32[]{:S(2)}, u32[]{:S(2)}) collective-permute-start(f32[9,128,128]{2,1,0:T(8,128)} %bitcast_dynamic-update-slice_fusion), channel_id=1, source_target_pairs={{0,0},{1,16},{2,32},{3,48},{4,64},{5,80},{6,96},{7,112},{8,128},{9... | collective-permute-start | bytes 1769480 | tf_op jit(solution)/shard_map/ppermute | solution.py:89
  230.3 1.2 copy-start.7
  230.8 1.3 copy-start.5
  231.6 1.3 copy-start.3
  232.1 1.3 copy-start.1
  233.3 1.1 copy-start.17
  233.4 1.3 copy-start.22
  233.4 1.4 copy-start.23
  236.3 108.0 %copy-start.19 = (f32[9,128,128]{2,1,0:T(8,128)S(1)}, f32[9,128,128]{2,1,0:T(8,128)}, u32[]{:S(2)}) copy-start(f32[9,128,128]{2,1,0:T(8,128)} %param.13) | copy-start | bytes 1769476
  236.3 108.0 %copy-start.24 = (f32[9,128,128]{2,1,0:T(8,128)S(1)}, f32[9,128,128]{2,1,0:T(8,128)}, u32[]{:S(2)}) copy-start(f32[9,128,128]{2,1,0:T(8,128)} %param.14) | copy-start | bytes 1769476
  236.3 108.0 %copy-start.25 = (f32[9,128,128]{2,1,0:T(8,128)S(1)}, f32[9,128,128]{2,1,0:T(8,128)}, u32[]{:S(2)}) copy-start(f32[9,128,128]{2,1,0:T(8,128)} %param.15) | copy-start | bytes 1769476
  267.9 83.8 %copy-start.33 = (bf16[1,2,128,128]{3,2,1,0:T(8,128)(2,1)S(1)}, bf16[1,2,128,128]{3,2,1,0:T(8,128)(2,1)}, u32[]{:S(2)}) copy-start(bf16[1,2,128,128]{3,2,1,0:T(8,128)(2,1)} %param.9) | copy-start | bytes 196612
  267.9 83.8 %copy-start.34 = (bf16[1,2,128,128]{3,2,1,0:T(8,128)(2,1)S(1)}, bf16[1,2,128,128]{3,2,1,0:T(8,128)(2,1)}, u32[]{:S(2)}) copy-start(bf16[1,2,128,128]{3,2,1,0:T(8,128)(2,1)} %param.8) | copy-start | bytes 196612
  267.9 83.8 %collective-permute-start.3 = (f32[1,2,128,256]{3,2,1,0:T(8,128)S(1)}, f32[1,2,128,256]{3,2,1,0:T(8,128)S(1)}, u32[]{:S(2)}, u32[]{:S(2)}) collective-permute-start(f32[1,2,128,256]{3,2,1,0:T(8,128)S(1)} %bitcast.319), channel_id=1, source_target_pairs={{0,0},{1,16},{2,32},{3,48},{4,64},{5,80},{6,96},{7,112},{8,128},{9... | collective-permute-start | bytes 786440 | tf_op jit(solution)/shard_map/ppermute | solution.py:89

commit v4 on v2

--- a/solution.py
+++ b/solution.py
@@ -23,32 +23,27 @@
 
 
 def conv_forward(source, weight):
-    samples, height, breadth, depth_in = source.shape
-    padded = pad_slab(source)
-    summed = jnp.zeros((samples * height * breadth, weight.shape[2]), jnp.float32)
-    for kernel_tap in range(9):
-        shifted = window(padded, kernel_tap // 3, kernel_tap % 3, height, breadth)
-        summed = summed + jnp.dot(
-            shifted.reshape(samples * height * breadth, depth_in),
-            weight[kernel_tap],
-            preferred_element_type=jnp.float32,
-        )
-    return summed.reshape(samples, height, breadth, weight.shape[2])
+    taps = weight.reshape((3, 3) + weight.shape[1:])
+    return lax.conv_general_dilated(
+        source,
+        taps,
+        (1, 1),
+        ((1, 1), (1, 1)),
+        dimension_numbers=("NHWC", "HWIO", "NHWC"),
+        preferred_element_type=jnp.float32,
+    )
 
 
 def adjoint_block(upstream, weight):
-    samples, height, breadth, depth_out = upstream.shape
-    padded = pad_slab(upstream)
-    summed = jnp.zeros((samples * height * breadth, weight.shape[1]), jnp.float32)
-    for kernel_tap in range(9):
-        shifted = window(padded, 2 - kernel_tap // 3, 2 - kernel_tap % 3, height, breadth)
-        summed = summed + lax.dot_general(
-            shifted.reshape(samples * height * breadth, depth_out),
-            weight[kernel_tap],
-            (((1,), (1,)), ((), ())),
-            preferred_element_type=jnp.float32,
-        )
-    return summed.reshape(samples, height, breadth, weight.shape[1])
+    taps = jnp.swapaxes(weight.reshape((3, 3) + weight.shape[1:])[::-1, ::-1], 2, 3)
+    return lax.conv_general_dilated(
+        upstream,
+        taps,
+        (1, 1),
+        ((1, 1), (1, 1)),
+        dimension_numbers=("NHWC", "HWIO", "NHWC"),
+        preferred_element_type=jnp.float32,
+    )
 
 
 def group_silu(pre_act):

time: 297 us -> 290 us (0.976)
  blocking collectives: 53.6 us -> 0 us
  waiting for transfers between devices: 120 us -> 161 us
  local copies, waits for them, and re-layouts: 19 us -> 28.9 us
  matrix products: 33.6 us -> 26 us
  starting transfers between devices: 52.1 us -> 56.5 us
    all_to_all x1 -> x0, blocking collectives: 53.6 us -> none  [exchange(): return lax.all_to_all(payload, axis, 0, 0, tiled=True)]
    all_to_all x4 -> x5, waiting for transfers between devices: 98.2 us -> 131 us  [exchange(): return lax.all_to_all(payload, axis, 0, 0, tiled=True)]
    dot_general x36 -> x0, matrix products: 17.2 us -> none  [the longest x18 8.76 us: adjoint_block(): lax.dot_general(shifted.reshape(samples * height * breadth, depth_out), w...]
    conv_general_dilated x0 -> x4, matrix products: none -> 11.5 us  [the longest x2 6.25 us: conv_forward(): lax.conv_general_dilated(source, taps, (1, 1), ((1, 1), (1, 1)), dimensio...]
    ppermute x4, waiting for transfers between devices: 22.2 us -> 30.6 us  [transpose_mesh(): return lax.ppermute(block, ('sample', 'filter'), pairs)]
    all_to_all x4 -> x5, starting transfers between devices: 28.3 us -> 34.4 us  [exchange(): return lax.all_to_all(payload, axis, 0, 0, tiled=True)]
    concatenate x0 -> x3, local copies, waits for them, and re-layouts: none -> 6.01 us  [the longest x1 2 us: per_device(): jnp.concatenate([partial_second, tiled(pre_grad, 'sample')], axis=3)]
    unnamed x94 -> x75, local copies, waits for them, and re-layouts: 3.38 us -> 8.42 us
  transfers between devices with their start and end apart: 8 -> 9, of which waited for: 7 -> 9; matrix products, arithmetic and copies ran while one was open for 11% -> 13% of each run, Pallas kernels for 0% -> 0%
where the time goes in v4:
time: 290 us; the launch traced here: 288 us
  waiting for transfers between devices  161 us (56%)
  starting transfers between devices  56.5 us (19%)
  local copies, waits for them, and re-layouts  28.9 us (10%)
  matrix products  26 us (9%)
  other arithmetic  14.4 us (5%)
    all_to_all x5, waiting for transfers between devices, exchange(): return lax.all_to_all(payload, axis, 0, 0, tiled=True)  131 us
    all_to_all x5, starting transfers between devices, exchange(): return lax.all_to_all(payload, axis, 0, 0, tiled=True)  34.4 us
    ppermute x4, waiting for transfers between devices, transpose_mesh(): return lax.ppermute(block, ('sample', 'filter'), pairs)  30.6 us
    ppermute x4, starting transfers between devices, transpose_mesh(): return lax.ppermute(block, ('sample', 'filter'), pairs)  22.1 us
    dot_general x18, matrix products, tap_grad_sum(): lax.dot_general(shifted, flat_up, (((1,), (1,)), ((0,), (0,))), preferred...  14.5 us
    unnamed x75, local copies, waits for them, and re-layouts  8.42 us
    conv_general_dilated x2, matrix products, conv_forward(): lax.conv_general_dilated(source, taps, (1, 1), ((1, 1), (1, 1)), dimensio...  6.25 us
  transfers between devices with their start and end apart: 9, of which 9 were waited for; matrix products, arithmetic and copies ran while one was open for 13% of the time, Pallas kernels for 0%

profile of v4, /device:TPU:6, one launch (start us, length us, event | category | flops | bytes accessed | tf_op | source)
XLA Modules:
  0.0 288.3 jit_solution(15166294069794103693)
XLA Ops:
  0.6 7.9 %collective-permute-start = (bf16[1,2,128,128]{3,2,1,0:T(8,128)(2,1)}, bf16[1,2,128,128]{3,2,1,0:T(8,128)(2,1)S(1)}, u32[]{:S(2)}, u32[]{:S(2)}) collective-permute-start(bf16[1,2,128,128]{3,2,1,0:T(8,128)(2,1)} %param.8), channel_id=1, source_target_pairs={{0,0},{1,16},{2,32},{3,48},{4,64},{5,80},{6,96},{7,112},{8,128},{9... | collective-permute-start | bytes 196616 | tf_op jit(solution)/shard_map/ppermute | solution.py:84
  8.5 8.0 %collective-permute-done = bf16[1,2,128,128]{3,2,1,0:T(8,128)(2,1)S(1)} collective-permute-done((bf16[1,2,128,128]{3,2,1,0:T(8,128)(2,1)}, bf16[1,2,128,128]{3,2,1,0:T(8,128)(2,1)S(1)}, u32[]{:S(2)}, u32[]{:S(2)}) %collective-permute-start) | collective-permute-done | bytes 65568 | tf_op jit(solution)/shard_map/ppermute | solution.py:84
  16.5 1.2 tile.19
  17.7 9.0 %all-to-all-start = ((bf16[16,2,128,128]{3,2,1,0:T(8,128)(2,1)}), bf16[16,2,128,128]{3,2,1,0:T(8,128)(2,1)S(1)}, u32[]{:S(2)}, u32[]{:S(2)}) async-start(bf16[16,2,128,128]{3,2,1,0:T(8,128)(2,1)} %tile.19), calls=%async_computation | async-start | bytes 2097152 | tf_op jit(solution)/shard_map/all_to_all | solution.py:88
  26.8 27.3 %all-to-all-done = bf16[16,2,128,128]{3,2,1,0:T(8,128)(2,1)S(1)} async-done(((bf16[16,2,128,128]{3,2,1,0:T(8,128)(2,1)}), bf16[16,2,128,128]{3,2,1,0:T(8,128)(2,1)S(1)}, u32[]{:S(2)}, u32[]{:S(2)}) %all-to-all-start) | async-done | bytes 1048608 | tf_op jit(solution)/shard_map/all_to_all | solution.py:88
  54.1 2.6 convolution_convert_fusion.3
  57.1 2.0 copy.108
  59.1 6.7 %all-to-all-start.1 = ((bf16[16,2,128,256]{3,2,1,0:T(8,128)(2,1)}), bf16[16,2,128,256]{3,2,1,0:T(8,128)(2,1)}, u32[]{:S(2)}, u32[]{:S(2)}) async-start(bf16[16,2,128,256]{3,2,1,0:T(8,128)(2,1)} %copy.108), calls=%async_computation.1 | async-start | bytes 4194304 | tf_op jit(solution)/shard_map/all_to_all | solution.py:88
  65.9 26.6 %all-to-all-done.1 = bf16[16,2,128,256]{3,2,1,0:T(8,128)(2,1)} async-done(((bf16[16,2,128,256]{3,2,1,0:T(8,128)(2,1)}), bf16[16,2,128,256]{3,2,1,0:T(8,128)(2,1)}, u32[]{:S(2)}, u32[]{:S(2)}) %all-to-all-start.1) | async-done | bytes 2097184 | tf_op jit(solution)/shard_map/all_to_all | solution.py:88
  92.6 1.9 convert_reduce_fusion
  95.4 5.0 %collective-permute-start.1 = (bf16[1,2,128,128]{3,2,1,0:T(8,128)(2,1)S(1)}, bf16[1,2,128,128]{3,2,1,0:T(8,128)(2,1)S(1)}, u32[]{:S(2)}, u32[]{:S(2)}) collective-permute-start(bf16[1,2,128,128]{3,2,1,0:T(8,128)(2,1)S(1)} %multiply_convert_fusion), channel_id=1, source_target_pairs={{0,0},{1,16},{2,32},{3,48},{4,64},{5,80},{6,96},{7,112},{8,128},{9... | collective-permute-start | bytes 196616 | tf_op jit(solution)/shard_map/ppermute | solution.py:84
  100.4 1.3 slice.91
  101.7 2.6 convolution_convert_fusion.1
  104.3 6.0 %collective-permute-done.1 = bf16[1,2,128,128]{3,2,1,0:T(8,128)(2,1)S(1)} collective-permute-done((bf16[1,2,128,128]{3,2,1,0:T(8,128)(2,1)S(1)}, bf16[1,2,128,128]{3,2,1,0:T(8,128)(2,1)S(1)}, u32[]{:S(2)}, u32[]{:S(2)}) %collective-permute-start.1) | collective-permute-done | bytes 65568 | tf_op jit(solution)/shard_map/ppermute | solution.py:84
  110.7 2.0 copy.110
  112.7 5.6 %all-to-all-start.2 = ((bf16[16,2,128,256]{3,2,1,0:T(8,128)(2,1)}), bf16[16,2,128,256]{3,2,1,0:T(8,128)(2,1)}, u32[]{:S(2)}, u32[]{:S(2)}) async-start(bf16[16,2,128,256]{3,2,1,0:T(8,128)(2,1)} %copy.110), calls=%async_computation.2 | async-start | bytes 4194304 | tf_op jit(solution)/shard_map/all_to_all | solution.py:88
  118.3 3.7 %pad_slice_fusion = (bf16[16,2,128,128]{3,2,1,0:T(8,128)(2,1)}, bf16[16,2,128,128]{3,2,1,0:T(8,128)(2,1)}, bf16[16,2,128,128]{3,2,1,0:T(8,128)(2,1)}, bf16[16,2,...) fusion(bf16[16,2,128,128]{3,2,1,0:T(8,128)(2,1)S(1)} %all-to-al, ...), kind=kLoop, calls=%fused_computation | loop fusion | bytes 9437184 | tf_op jit(solution)/shard_map/slice | solution.py:22
  122.0 44.3 %all-to-all-done.2 = bf16[16,2,128,256]{3,2,1,0:T(8,128)(2,1)} async-done(((bf16[16,2,128,256]{3,2,1,0:T(8,128)(2,1)}), bf16[16,2,128,256]{3,2,1,0:T(8,128)(2,1)}, u32[]{:S(2)}, u32[]{:S(2)}) %all-to-all-start.2) | async-done | bytes 2097184 | tf_op jit(solution)/shard_map/all_to_all | solution.py:88
  166.3 1.3 slice.92
  167.7 3.6 %convolution_convert_fusion.2 = bf16[16,2,128,128]{3,0,2,1:T(8,128)(2,1)} fusion(bf16[3,3,128,128]{3,2,1,0:T(8,128)(2,1)S(1)} %bitcast.152, bf16[16,2,128,128]{3,2,1,0:T(8,128)(2,1)S(1)} %slice.92), kind=kOutput, calls=%fused_computation.26 | convolution fusion | flops 801636352 | bytes 2392064 | tf_op jit(solution)/shard_map/conv_general_dilated | solution.py:27
  171.3 0.7 copy.160
  172.0 1.4 convert_reduce_fusion.4
  173.4 4.1 %collective-permute-start.2 = (f32[1,2,128,128]{3,2,1,0:T(8,128)S(1)}, f32[1,2,128,128]{3,2,1,0:T(8,128)S(1)}, u32[]{:S(2)}, u32[]{:S(2)}) collective-permute-start(f32[1,2,128,128]{3,2,1,0:T(8,128)S(1)} %bitcast.162), channel_id=1, source_target_pairs={{0,0},{1,16},{2,32},{3,48},{4,64},{5,80},{6,96},{7,112},{8,128},{9... | collective-permute-start | bytes 393224 | tf_op jit(solution)/shard_map/ppermute | solution.py:84
  177.5 1.4 pad_slice_fusion.8
  178.9 1.1 fusion.35
  180.1 1.1 fusion.29
  181.2 1.1 fusion.30
  182.3 1.1 fusion.32
  183.4 1.1 fusion.33
  185.1 0.5 fusion.28
  185.6 0.6 bitcast_dynamic-update-slice_fusion.9
  186.2 0.6 bitcast_dynamic-update-slice_fusion.8
  186.9 1.1 fusion.34
  188.0 4.6 %collective-permute-done.2 = f32[1,2,128,128]{3,2,1,0:T(8,128)S(1)} collective-permute-done((f32[1,2,128,128]{3,2,1,0:T(8,128)S(1)}, f32[1,2,128,128]{3,2,1,0:T(8,128)S(1)}, u32[]{:S(2)}, u32[]{:S(2)}) %collective-permute-start.2) | collective-permute-done | bytes 131104 | tf_op jit(solution)/shard_map/ppermute | solution.py:84
  193.7 1.5 pad_maximum_fusion.2
  195.2 2.0 copy.112
  197.2 4.8 %all-to-all-start.3 = ((bf16[16,2,128,256]{3,2,1,0:T(8,128)(2,1)}), bf16[16,2,128,256]{3,2,1,0:T(8,128)(2,1)}, u32[]{:S(2)}, u32[]{:S(2)}) async-start(bf16[16,2,128,256]{3,2,1,0:T(8,128)(2,1)} %copy.112), calls=%async_computation.3 | async-start | bytes 4194304 | tf_op jit(solution)/shard_map/all_to_all | solution.py:88
  202.9 0.6 bitcast_dynamic-update-slice_fusion.7
  203.5 0.6 bitcast_dynamic-update-slice_fusion.6
  204.1 0.6 bitcast_dynamic-update-slice_fusion.5
  204.8 0.6 bitcast_dynamic-update-slice_fusion.4
  205.4 0.6 bitcast_dynamic-update-slice_fusion.3
  206.0 0.6 bitcast_dynamic-update-slice_fusion.2
  206.7 0.6 bitcast_dynamic-update-slice_fusion.1
  207.3 2.6 multiply_subtract_fusion
  209.9 18.8 %all-to-all-done.3 = bf16[16,2,128,256]{3,2,1,0:T(8,128)(2,1)} async-done(((bf16[16,2,128,256]{3,2,1,0:T(8,128)(2,1)}), bf16[16,2,128,256]{3,2,1,0:T(8,128)(2,1)}, u32[]{:S(2)}, u32[]{:S(2)}) %all-to-all-start.3) | async-done | bytes 2097184 | tf_op jit(solution)/shard_map/all_to_all | solution.py:88
  228.7 1.3 slice.95
  230.0 2.6 convolution_convert_fusion
  232.7 1.3 copy.114
  233.9 8.3 %all-to-all-start.4 = ((bf16[16,2,128,128]{3,2,1,0:T(8,128)(2,1)}), bf16[16,2,128,128]{3,2,1,0:T(8,128)(2,1)}, u32[]{:S(2)}, u32[]{:S(2)}) async-start(bf16[16,2,128,128]{3,2,1,0:T(8,128)(2,1)} %copy.114), calls=%async_computation.4 | async-start | bytes 2097152 | tf_op jit(solution)/shard_map/all_to_all | solution.py:88
  242.2 1.1 fusion.22
  244.6 1.1 fusion.20
  245.7 1.1 fusion.21
  249.2 1.4 convert_reduce_fusion.3
  250.6 0.9 copy.124
  251.6 0.8 bitcast_dynamic-update-slice_fusion.15
  252.4 0.8 bitcast_dynamic-update-slice_fusion.14
  253.4 1.4 multiply_subtract_fusion.1
  254.8 13.6 %all-to-all-done.4 = bf16[16,2,128,128]{3,2,1,0:T(8,128)(2,1)} async-done(((bf16[16,2,128,128]{3,2,1,0:T(8,128)(2,1)}), bf16[16,2,128,128]{3,2,1,0:T(8,128)(2,1)}, u32[]{:S(2)}, u32[]{:S(2)}) %all-to-all-start.4) | async-done | bytes 1048608 | tf_op jit(solution)/shard_map/all_to_all | solution.py:88
  268.4 1.4 convert_reduce_fusion.2
  269.8 5.1 %collective-permute-start.3 = (f32[1,2,128,128]{3,2,1,0:T(8,128)S(1)}, f32[1,2,128,128]{3,2,1,0:T(8,128)S(1)}, u32[]{:S(2)}, u32[]{:S(2)}) collective-permute-start(f32[1,2,128,128]{3,2,1,0:T(8,128)S(1)} %bitcast.163), channel_id=1, source_target_pairs={{0,0},{1,16},{2,32},{3,48},{4,64},{5,80},{6,96},{7,112},{8,128},{9... | collective-permute-start | bytes 393224 | tf_op jit(solution)/shard_map/ppermute | solution.py:84
  274.9 0.6 fusion.56
  275.6 12.1 %collective-permute-done.3 = f32[1,2,128,128]{3,2,1,0:T(8,128)S(1)} collective-permute-done((f32[1,2,128,128]{3,2,1,0:T(8,128)S(1)}, f32[1,2,128,128]{3,2,1,0:T(8,128)S(1)}, u32[]{:S(2)}, u32[]{:S(2)}) %collective-permute-start.3) | collective-permute-done | bytes 131104 | tf_op jit(solution)/shard_map/ppermute | solution.py:84
  287.7 0.6 add_convert_fusion
  (105 shorter events, 7.6 us)
Async XLA Ops:
  0.6 26.1 %copy-start.14 = (f32[9,128,128]{2,1,0:T(8,128)S(1)}, f32[9,128,128]{2,1,0:T(8,128)}, u32[]{:S(2)}) copy-start(f32[9,128,128]{2,1,0:T(8,128)} %param.10) | copy-start | bytes 1769476
  0.6 15.8 %collective-permute-start = (bf16[1,2,128,128]{3,2,1,0:T(8,128)(2,1)}, bf16[1,2,128,128]{3,2,1,0:T(8,128)(2,1)S(1)}, u32[]{:S(2)}, u32[]{:S(2)}) collective-permute-start(bf16[1,2,128,128]{3,2,1,0:T(8,128)(2,1)} %param.8), channel_id=1, source_target_pairs={{0,0},{1,16},{2,32},{3,48},{4,64},{5,80},{6,96},{7,112},{8,128},{9... | collective-permute-start | bytes 196616 | tf_op jit(solution)/shard_map/ppermute | solution.py:84
  17.7 36.4 %all-to-all-start = ((bf16[16,2,128,128]{3,2,1,0:T(8,128)(2,1)}), bf16[16,2,128,128]{3,2,1,0:T(8,128)(2,1)S(1)}, u32[]{:S(2)}, u32[]{:S(2)}) async-start(bf16[16,2,128,128]{3,2,1,0:T(8,128)(2,1)} %tile.19), calls=%async_computation | async-start | bytes 2097152 | tf_op jit(solution)/shard_map/all_to_all | solution.py:88
  26.7 30.0 %copy-start.20 = (bf16[1,2,128,128]{3,2,1,0:T(8,128)(2,1)S(1)}, bf16[1,2,128,128]{3,2,1,0:T(8,128)(2,1)}, u32[]{:S(2)}) copy-start(bf16[1,2,128,128]{3,2,1,0:T(8,128)(2,1)} %param.9) | copy-start | bytes 196612
  26.8 30.1 %copy-start.8 = (bf16[9,128,128]{2,1,0:T(8,128)(2,1)}, bf16[9,128,128]{2,1,0:T(8,128)(2,1)S(1)}, u32[]{:S(2)}) copy-start(bf16[9,128,128]{2,1,0:T(8,128)(2,1)S(1)} %convert_element_type.172) | copy-start | bytes 884740
  59.1 6.7 %copy-start.12 = (f32[9,128,128]{2,1,0:T(8,128)S(1)}, f32[9,128,128]{2,1,0:T(8,128)}, u32[]{:S(2)}) copy-start(f32[9,128,128]{2,1,0:T(8,128)} %param.13) | copy-start | bytes 1769476
  59.1 33.4 %all-to-all-start.1 = ((bf16[16,2,128,256]{3,2,1,0:T(8,128)(2,1)}), bf16[16,2,128,256]{3,2,1,0:T(8,128)(2,1)}, u32[]{:S(2)}, u32[]{:S(2)}) async-start(bf16[16,2,128,256]{3,2,1,0:T(8,128)(2,1)} %copy.108), calls=%async_computation.1 | async-start | bytes 4194304 | tf_op jit(solution)/shard_map/all_to_all | solution.py:88
  65.9 38.4 %copy-start.10 = (bf16[9,128,128]{2,1,0:T(8,128)(2,1)}, bf16[9,128,128]{2,1,0:T(8,128)(2,1)S(1)}, u32[]{:S(2)}) copy-start(bf16[9,128,128]{2,1,0:T(8,128)(2,1)S(1)} %convert_element_type.176) | copy-start | bytes 884740
  95.4 15.0 %collective-permute-start.1 = (bf16[1,2,128,128]{3,2,1,0:T(8,128)(2,1)S(1)}, bf16[1,2,128,128]{3,2,1,0:T(8,128)(2,1)S(1)}, u32[]{:S(2)}, u32[]{:S(2)}) collective-permute-start(bf16[1,2,128,128]{3,2,1,0:T(8,128)(2,1)S(1)} %multiply_convert_fusion), channel_id=1, source_target_pairs={{0,0},{1,16},{2,32},{3,48},{4,64},{5,80},{6,96},{7,112},{8,128},{9... | collective-permute-start | bytes 196616 | tf_op jit(solution)/shard_map/ppermute | solution.py:84
  112.7 53.6 %all-to-all-start.2 = ((bf16[16,2,128,256]{3,2,1,0:T(8,128)(2,1)}), bf16[16,2,128,256]{3,2,1,0:T(8,128)(2,1)}, u32[]{:S(2)}, u32[]{:S(2)}) async-start(bf16[16,2,128,256]{3,2,1,0:T(8,128)(2,1)} %copy.110), calls=%async_computation.2 | async-start | bytes 4194304 | tf_op jit(solution)/shard_map/all_to_all | solution.py:88
  166.3 1.3 copy-start.11
  173.4 19.2 %collective-permute-start.2 = (f32[1,2,128,128]{3,2,1,0:T(8,128)S(1)}, f32[1,2,128,128]{3,2,1,0:T(8,128)S(1)}, u32[]{:S(2)}, u32[]{:S(2)}) collective-permute-start(f32[1,2,128,128]{3,2,1,0:T(8,128)S(1)} %bitcast.162), channel_id=1, source_target_pairs={{0,0},{1,16},{2,32},{3,48},{4,64},{5,80},{6,96},{7,112},{8,128},{9... | collective-permute-start | bytes 393224 | tf_op jit(solution)/shard_map/ppermute | solution.py:84
  197.2 31.5 %all-to-all-start.3 = ((bf16[16,2,128,256]{3,2,1,0:T(8,128)(2,1)}), bf16[16,2,128,256]{3,2,1,0:T(8,128)(2,1)}, u32[]{:S(2)}, u32[]{:S(2)}) async-start(bf16[16,2,128,256]{3,2,1,0:T(8,128)(2,1)} %copy.112), calls=%async_computation.3 | async-start | bytes 4194304 | tf_op jit(solution)/shard_map/all_to_all | solution.py:88
  202.0 0.8 copy-start.26
  202.0 1.5 copy-start.25
  202.0 2.7 copy-start.24
  202.1 3.4 %copy-start.23 = (f32[128,128]{1,0:T(8,128)S(1)}, f32[128,128]{1,0:T(8,128)}, u32[]{:S(2)}) copy-start(f32[128,128]{1,0:T(8,128)} %fusion.33) | copy-start | bytes 196612
  202.1 4.0 %copy-start.27 = (f32[128,128]{1,0:T(8,128)S(1)}, f32[128,128]{1,0:T(8,128)}, u32[]{:S(2)}) copy-start(f32[128,128]{1,0:T(8,128)} %fusion.34) | copy-start | bytes 196612
  202.1 4.6 %copy-start.22 = (f32[128,128]{1,0:T(8,128)S(1)}, f32[128,128]{1,0:T(8,128)}, u32[]{:S(2)}) copy-start(f32[128,128]{1,0:T(8,128)} %fusion.35) | copy-start | bytes 196612
  202.1 5.2 %copy-start.13 = (f32[9,128,128]{2,1,0:T(8,128)S(1)}, f32[9,128,128]{2,1,0:T(8,128)}, u32[]{:S(2)}) copy-start(f32[9,128,128]{2,1,0:T(8,128)} %param.13) | copy-start | bytes 1769476
  202.1 5.2 %copy-start.16 = (f32[9,128,128]{2,1,0:T(8,128)S(1)}, f32[9,128,128]{2,1,0:T(8,128)}, u32[]{:S(2)}) copy-start(f32[9,128,128]{2,1,0:T(8,128)} %param.14) | copy-start | bytes 1769476
  202.1 5.2 %copy-start.17 = (f32[9,128,128]{2,1,0:T(8,128)S(1)}, f32[9,128,128]{2,1,0:T(8,128)}, u32[]{:S(2)}) copy-start(f32[9,128,128]{2,1,0:T(8,128)} %param.15) | copy-start | bytes 1769476
  207.3 22.7 %copy-start.9 = (bf16[9,128,128]{2,1,0:T(8,128)(2,1)S(1)}, bf16[9,128,128]{2,1,0:T(8,128)(2,1)}, u32[]{:S(2)}) copy-start(bf16[9,128,128]{2,1,0:T(8,128)(2,1)} %copy-done.8) | copy-start | bytes 884740
  233.9 9.4 %copy-start.7 = (bf16[16,2,128,128]{3,2,1,0:T(8,128)(2,1)S(1)}, bf16[16,2,128,128]{3,2,1,0:T(8,128)(2,1)}, u32[]{:S(2)}) copy-start(bf16[16,2,128,128]{3,2,1,0:T(8,128)(2,1)} %get-tuple-element.34) | copy-start | bytes 3145732
  233.9 34.5 %all-to-all-start.4 = ((bf16[16,2,128,128]{3,2,1,0:T(8,128)(2,1)}), bf16[16,2,128,128]{3,2,1,0:T(8,128)(2,1)}, u32[]{:S(2)}, u32[]{:S(2)}) async-start(bf16[16,2,128,128]{3,2,1,0:T(8,128)(2,1)} %copy.114), calls=%async_computation.4 | async-start | bytes 2097152 | tf_op jit(solution)/shard_map/all_to_all | solution.py:88
  242.2 1.6 copy-start.6
  243.3 1.3 copy-start.5
  243.8 1.9 copy-start.4
  244.6 2.2 copy-start.3
  245.7 1.6 copy-start.2
  246.9 1.3 copy-start.1
  247.3 1.3 copy-start
  248.7 4.7 %copy-start.15 = (f32[9,128,128]{2,1,0:T(8,128)S(1)}, f32[9,128,128]{2,1,0:T(8,128)}, u32[]{:S(2)}) copy-start(f32[9,128,128]{2,1,0:T(8,128)} %param.10) | copy-start | bytes 1769476
  248.7 4.7 %copy-start.18 = (f32[9,128,128]{2,1,0:T(8,128)S(1)}, f32[9,128,128]{2,1,0:T(8,128)}, u32[]{:S(2)}) copy-start(f32[9,128,128]{2,1,0:T(8,128)} %param.11) | copy-start | bytes 1769476
  249.1 4.2 %copy-start.19 = (f32[9,128,128]{2,1,0:T(8,128)S(1)}, f32[9,128,128]{2,1,0:T(8,128)}, u32[]{:S(2)}) copy-start(f32[9,128,128]{2,1,0:T(8,128)} %param.12) | copy-start | bytes 1769476
  253.3 21.6 %copy-start.28 = (bf16[1,2,128,128]{3,2,1,0:T(8,128)(2,1)S(1)}, bf16[1,2,128,128]{3,2,1,0:T(8,128)(2,1)}, u32[]{:S(2)}) copy-start(bf16[1,2,128,128]{3,2,1,0:T(8,128)(2,1)} %param.8) | copy-start | bytes 196612
  253.4 34.3 %copy-start.21 = (bf16[1,2,128,128]{3,2,1,0:T(8,128)(2,1)S(1)}, bf16[1,2,128,128]{3,2,1,0:T(8,128)(2,1)}, u32[]{:S(2)}) copy-start(bf16[1,2,128,128]{3,2,1,0:T(8,128)(2,1)} %param.9) | copy-start | bytes 196612
  269.8 17.9 %collective-permute-start.3 = (f32[1,2,128,128]{3,2,1,0:T(8,128)S(1)}, f32[1,2,128,128]{3,2,1,0:T(8,128)S(1)}, u32[]{:S(2)}, u32[]{:S(2)}) collective-permute-start(f32[1,2,128,128]{3,2,1,0:T(8,128)S(1)} %bitcast.163), channel_id=1, source_target_pairs={{0,0},{1,16},{2,32},{3,48},{4,64},{5,80},{6,96},{7,112},{8,128},{9... | collective-permute-start | bytes 393224 | tf_op jit(solution)/shard_map/ppermute | solution.py:84

commit v5 on v4

--- a/solution.py
+++ b/solution.py
@@ -131,7 +131,8 @@
     terms_first = adjoint_block(whole_pre_grad, weight_first).astype(jnp.bfloat16)
     data_grad = transpose_mesh(summed(exchange(terms_first, "filter")))
     input_grad = (cotangent.astype(jnp.float32) + data_grad).astype(jnp.bfloat16)
-    grad_second = tap_grad_sum(whole_hidden, whole_cotangent)
+    deferred_hidden, deferred_cotangent, _ = lax.optimization_barrier((whole_hidden, whole_cotangent, joined))
+    grad_second = tap_grad_sum(deferred_hidden, deferred_cotangent)
     grad_first = tap_grad_sum(whole_input, whole_pre_grad)
     new_master_first, new_moment_first, new_second_first = adam_update(
         master_first, moment_first, second_first, grad_first

time: 290 us -> 280 us (0.966)
  blocking collectives: 0 us -> 53.6 us
  waiting for transfers between devices: 161 us -> 111 us
  local copies, waits for them, and re-layouts: 28.9 us -> 22.4 us
  starting transfers between devices: 56.5 us -> 50.4 us
    all_to_all x5 -> x4, waiting for transfers between devices: 131 us -> 75.7 us  [exchange(): return lax.all_to_all(payload, axis, 0, 0, tiled=True)]
    all_to_all x0 -> x1, blocking collectives: none -> 53.6 us  [exchange(): return lax.all_to_all(payload, axis, 0, 0, tiled=True)]
    all_to_all x5 -> x4, starting transfers between devices: 34.4 us -> 27.3 us  [exchange(): return lax.all_to_all(payload, axis, 0, 0, tiled=True)]
    unnamed x75 -> x82, local copies, waits for them, and re-layouts: 8.42 us -> 2.21 us
    ppermute x4, waiting for transfers between devices: 30.6 us -> 35.4 us  [transpose_mesh(): return lax.ppermute(block, ('sample', 'filter'), pairs)]
    optimization_barrier x0 -> x2, local copies, waits for them, and re-layouts: none -> 3.38 us  [per_device(): lax.optimization_barrier((whole_hidden, whole_cotangent, joined))]
  transfers between devices with their start and end apart: 9 -> 8, of which waited for: 9 -> 8; matrix products, arithmetic and copies ran while one was open for 13% -> 14% of each run, Pallas kernels for 0% -> 0%
where the time goes in v5:
time: 280 us; the launch traced here: 278 us
  waiting for transfers between devices  111 us (40%)
  blocking collectives  53.6 us (19%)
  starting transfers between devices  50.4 us (18%)
  matrix products  27.1 us (10%)
  local copies, waits for them, and re-layouts  22.4 us (8%)
  other arithmetic  11.7 us (4%)
    all_to_all x4, waiting for transfers between devices, exchange(): return lax.all_to_all(payload, axis, 0, 0, tiled=True)  75.7 us
    all_to_all x1, blocking collectives, exchange(): return lax.all_to_all(payload, axis, 0, 0, tiled=True)  53.6 us
    ppermute x4, waiting for transfers between devices, transpose_mesh(): return lax.ppermute(block, ('sample', 'filter'), pairs)  35.4 us
    all_to_all x4, starting transfers between devices, exchange(): return lax.all_to_all(payload, axis, 0, 0, tiled=True)  27.3 us
    ppermute x4, starting transfers between devices, transpose_mesh(): return lax.ppermute(block, ('sample', 'filter'), pairs)  23.1 us
    dot_general x18, matrix products, tap_grad_sum(): lax.dot_general(shifted, flat_up, (((1,), (1,)), ((0,), (0,))), preferred...  15.6 us
    conv_general_dilated x2, matrix products, conv_forward(): lax.conv_general_dilated(source, taps, (1, 1), ((1, 1), (1, 1)), dimensio...  6.25 us
  transfers between devices with their start and end apart: 8, of which 8 were waited for; matrix products, arithmetic and copies ran while one was open for 14% of the time, Pallas kernels for 0%

profile of v5, /device:TPU:6, one launch (start us, length us, event | category | flops | bytes accessed | tf_op | source)
XLA Modules:
  0.0 277.7 jit_solution(5088964447495402644)
XLA Ops:
  0.6 7.9 %collective-permute-start = (bf16[1,2,128,128]{3,2,1,0:T(8,128)(2,1)}, bf16[1,2,128,128]{3,2,1,0:T(8,128)(2,1)S(1)}, u32[]{:S(2)}, u32[]{:S(2)}) collective-permute-start(bf16[1,2,128,128]{3,2,1,0:T(8,128)(2,1)} %param.8), channel_id=1, source_target_pairs={{0,0},{1,16},{2,32},{3,48},{4,64},{5,80},{6,96},{7,112},{8,128},{9... | collective-permute-start | bytes 196616 | tf_op jit(solution)/shard_map/ppermute | solution.py:84
  8.5 8.0 %collective-permute-done = bf16[1,2,128,128]{3,2,1,0:T(8,128)(2,1)S(1)} collective-permute-done((bf16[1,2,128,128]{3,2,1,0:T(8,128)(2,1)}, bf16[1,2,128,128]{3,2,1,0:T(8,128)(2,1)S(1)}, u32[]{:S(2)}, u32[]{:S(2)}) %collective-permute-start) | collective-permute-done | bytes 65568 | tf_op jit(solution)/shard_map/ppermute | solution.py:84
  16.5 1.2 tile.19
  17.7 9.0 %all-to-all-start = ((bf16[16,2,128,128]{3,2,1,0:T(8,128)(2,1)}), bf16[16,2,128,128]{3,2,1,0:T(8,128)(2,1)S(1)}, u32[]{:S(2)}, u32[]{:S(2)}) async-start(bf16[16,2,128,128]{3,2,1,0:T(8,128)(2,1)} %tile.19), calls=%async_computation | async-start | bytes 2097152 | tf_op jit(solution)/shard_map/all_to_all | solution.py:88
  26.8 27.3 %all-to-all-done = bf16[16,2,128,128]{3,2,1,0:T(8,128)(2,1)S(1)} async-done(((bf16[16,2,128,128]{3,2,1,0:T(8,128)(2,1)}), bf16[16,2,128,128]{3,2,1,0:T(8,128)(2,1)S(1)}, u32[]{:S(2)}, u32[]{:S(2)}) %all-to-all-start) | async-done | bytes 1048608 | tf_op jit(solution)/shard_map/all_to_all | solution.py:88
  54.1 2.6 convolution_convert_fusion.3
  56.9 0.2 pad_maximum_fusion
  57.1 2.0 copy.108
  59.1 6.7 %all-to-all-start.1 = ((bf16[16,2,128,256]{3,2,1,0:T(8,128)(2,1)}), bf16[16,2,128,256]{3,2,1,0:T(8,128)(2,1)}, u32[]{:S(2)}, u32[]{:S(2)}) async-start(bf16[16,2,128,256]{3,2,1,0:T(8,128)(2,1)} %copy.108), calls=%async_computation.1 | async-start | bytes 4194304 | tf_op jit(solution)/shard_map/all_to_all | solution.py:88
  65.9 26.6 %all-to-all-done.1 = bf16[16,2,128,256]{3,2,1,0:T(8,128)(2,1)} async-done(((bf16[16,2,128,256]{3,2,1,0:T(8,128)(2,1)}), bf16[16,2,128,256]{3,2,1,0:T(8,128)(2,1)}, u32[]{:S(2)}, u32[]{:S(2)}) %all-to-all-start.1) | async-done | bytes 2097184 | tf_op jit(solution)/shard_map/all_to_all | solution.py:88
  92.6 1.9 convert_reduce_fusion
  95.4 5.0 %collective-permute-start.1 = (bf16[1,2,128,128]{3,2,1,0:T(8,128)(2,1)S(1)}, bf16[1,2,128,128]{3,2,1,0:T(8,128)(2,1)S(1)}, u32[]{:S(2)}, u32[]{:S(2)}) collective-permute-start(bf16[1,2,128,128]{3,2,1,0:T(8,128)(2,1)S(1)} %multiply_convert_fusion), channel_id=1, source_target_pairs={{0,0},{1,16},{2,32},{3,48},{4,64},{5,80},{6,96},{7,112},{8,128},{9... | collective-permute-start | bytes 196616 | tf_op jit(solution)/shard_map/ppermute | solution.py:84
  100.4 1.3 slice.91
  101.7 2.6 convolution_convert_fusion.1
  104.3 6.0 %collective-permute-done.1 = bf16[1,2,128,128]{3,2,1,0:T(8,128)(2,1)S(1)} collective-permute-done((bf16[1,2,128,128]{3,2,1,0:T(8,128)(2,1)S(1)}, bf16[1,2,128,128]{3,2,1,0:T(8,128)(2,1)S(1)}, u32[]{:S(2)}, u32[]{:S(2)}) %collective-permute-start.1) | collective-permute-done | bytes 65568 | tf_op jit(solution)/shard_map/ppermute | solution.py:84
  110.5 0.2 pad_maximum_fusion.1
  110.7 0.7 copy.110
  111.4 53.6 %all_to_all.25 = bf16[16,2,128,256]{3,2,1,0:T(8,128)(2,1)S(1)} all-to-all(bf16[16,2,128,256]{3,2,1,0:T(8,128)(2,1)S(1)} %copy.110), channel_id=1, replica_groups=mesh['sample'=16,'filter'=16] {'filter'}, dimensions={0} | all-to-all | bytes 4194304 | tf_op jit(solution)/shard_map/all_to_all | solution.py:88
  165.2 5.2 %collective-permute-start.2 = (f32[1,2,128,128]{3,2,1,0:T(8,128)S(1)}, f32[1,2,128,128]{3,2,1,0:T(8,128)S(1)}, u32[]{:S(2)}, u32[]{:S(2)}) collective-permute-start(f32[1,2,128,128]{3,2,1,0:T(8,128)S(1)} %bitcast.150), channel_id=1, source_target_pairs={{0,0},{1,16},{2,32},{3,48},{4,64},{5,80},{6,96},{7,112},{8,128},{9... | collective-permute-start | bytes 393224 | tf_op jit(solution)/shard_map/ppermute | solution.py:84
  170.4 0.2 slice.92
  170.6 3.6 %convolution_convert_fusion.2 = bf16[16,2,128,128]{3,0,2,1:T(8,128)(2,1)} fusion(bf16[3,3,128,128]{3,2,1,0:T(8,128)(2,1)S(1)} %bitcast.131, bf16[16,2,128,128]{3,2,1,0:T(8,128)(2,1)S(1)} %slice.92), kind=kOutput, calls=%fused_computation.26 | convolution fusion | flops 801636352 | bytes 2392064 | tf_op jit(solution)/shard_map/conv_general_dilated | solution.py:27
  174.2 9.2 %collective-permute-done.2 = f32[1,2,128,128]{3,2,1,0:T(8,128)S(1)} collective-permute-done((f32[1,2,128,128]{3,2,1,0:T(8,128)S(1)}, f32[1,2,128,128]{3,2,1,0:T(8,128)S(1)}, u32[]{:S(2)}, u32[]{:S(2)}) %collective-permute-start.2) | collective-permute-done | bytes 131104 | tf_op jit(solution)/shard_map/ppermute | solution.py:84
  184.5 1.5 pad_maximum_fusion.2
  186.1 2.0 copy.112
  188.1 5.6 %all-to-all-start.3 = ((bf16[16,2,128,256]{3,2,1,0:T(8,128)(2,1)}), bf16[16,2,128,256]{3,2,1,0:T(8,128)(2,1)}, u32[]{:S(2)}, u32[]{:S(2)}) async-start(bf16[16,2,128,256]{3,2,1,0:T(8,128)(2,1)} %copy.112), calls=%async_computation.3 | async-start | bytes 4194304 | tf_op jit(solution)/shard_map/all_to_all | solution.py:88
  193.7 3.7 %pad_slice_fusion = (bf16[16,2,128,128]{3,2,1,0:T(8,128)(2,1)}, bf16[16,2,128,128]{3,2,1,0:T(8,128)(2,1)}, bf16[16,2,128,128]{3,2,1,0:T(8,128)(2,1)}, bf16[16,2,...) fusion(bf16[16,2,128,128]{3,2,1,0:T(8,128)(2,1)S(1)} %all-to-al, ...), kind=kLoop, calls=%fused_computation | loop fusion | bytes 9437184 | tf_op jit(solution)/shard_map/slice | solution.py:22
  197.4 1.7 copy.159
  199.1 1.7 copy.160
  200.8 19.6 %all-to-all-done.3 = bf16[16,2,128,256]{3,2,1,0:T(8,128)(2,1)} async-done(((bf16[16,2,128,256]{3,2,1,0:T(8,128)(2,1)}), bf16[16,2,128,256]{3,2,1,0:T(8,128)(2,1)}, u32[]{:S(2)}, u32[]{:S(2)}) %all-to-all-start.3) | async-done | bytes 2097184 | tf_op jit(solution)/shard_map/all_to_all | solution.py:88
  220.4 1.3 slice.95
  221.7 2.6 convolution_convert_fusion
  224.3 1.3 copy.114
  225.6 6.0 %all-to-all-start.4 = ((bf16[16,2,128,128]{3,2,1,0:T(8,128)(2,1)}), bf16[16,2,128,128]{3,2,1,0:T(8,128)(2,1)}, u32[]{:S(2)}, u32[]{:S(2)}) async-start(bf16[16,2,128,128]{3,2,1,0:T(8,128)(2,1)} %copy.114), calls=%async_computation.4 | async-start | bytes 2097152 | tf_op jit(solution)/shard_map/all_to_all | solution.py:88
  231.6 1.7 pad_slice_fusion.8
  233.3 0.6 fusion.27
  233.9 0.6 bitcast_dynamic-update-slice_fusion.9
  234.6 1.2 fusion.28
  235.8 1.2 fusion.29
  237.0 1.2 fusion.30
  238.3 1.2 fusion.31
  239.5 1.2 fusion.32
  240.8 1.2 fusion.33
  242.0 0.6 fusion.34
  242.6 1.2 fusion.35
  243.9 0.5 fusion.18
  244.4 0.6 bitcast_dynamic-update-slice_fusion.17
  245.0 0.5 fusion.19
  245.5 0.5 fusion.20
  246.0 0.3 copy-done.3
  246.3 0.5 fusion.21
  246.8 0.5 fusion.22
  247.4 1.8 fusion.23
  249.2 0.5 fusion.24
  249.8 0.5 fusion.25
  250.4 0.5 fusion.26
  251.2 0.3 copy-done.17
  251.5 1.7 convert_reduce_fusion.3
  253.3 2.3 multiply_subtract_fusion
  255.6 2.2 all-to-all-done.4
  257.8 1.4 convert_reduce_fusion.2
  259.2 5.0 %collective-permute-start.3 = (f32[1,2,128,128]{3,2,1,0:T(8,128)S(1)}, f32[1,2,128,128]{3,2,1,0:T(8,128)S(1)}, u32[]{:S(2)}, u32[]{:S(2)}) collective-permute-start(f32[1,2,128,128]{3,2,1,0:T(8,128)S(1)} %bitcast.151), channel_id=1, source_target_pairs={{0,0},{1,16},{2,32},{3,48},{4,64},{5,80},{6,96},{7,112},{8,128},{9... | collective-permute-start | bytes 393224 | tf_op jit(solution)/shard_map/ppermute | solution.py:84
  264.2 0.6 fusion.56
  264.9 12.2 %collective-permute-done.3 = f32[1,2,128,128]{3,2,1,0:T(8,128)S(1)} collective-permute-done((f32[1,2,128,128]{3,2,1,0:T(8,128)S(1)}, f32[1,2,128,128]{3,2,1,0:T(8,128)S(1)}, u32[]{:S(2)}, u32[]{:S(2)}) %collective-permute-start.3) | collective-permute-done | bytes 131104 | tf_op jit(solution)/shard_map/ppermute | solution.py:84
  277.1 0.6 add_convert_fusion
  (112 shorter events, 2.9 us)
Async XLA Ops:
  0.6 26.1 %copy-start.14 = (f32[9,128,128]{2,1,0:T(8,128)S(1)}, f32[9,128,128]{2,1,0:T(8,128)}, u32[]{:S(2)}) copy-start(f32[9,128,128]{2,1,0:T(8,128)} %param.10) | copy-start | bytes 1769476
  0.6 15.8 %collective-permute-start = (bf16[1,2,128,128]{3,2,1,0:T(8,128)(2,1)}, bf16[1,2,128,128]{3,2,1,0:T(8,128)(2,1)S(1)}, u32[]{:S(2)}, u32[]{:S(2)}) collective-permute-start(bf16[1,2,128,128]{3,2,1,0:T(8,128)(2,1)} %param.8), channel_id=1, source_target_pairs={{0,0},{1,16},{2,32},{3,48},{4,64},{5,80},{6,96},{7,112},{8,128},{9... | collective-permute-start | bytes 196616 | tf_op jit(solution)/shard_map/ppermute | solution.py:84
  17.7 36.4 %all-to-all-start = ((bf16[16,2,128,128]{3,2,1,0:T(8,128)(2,1)}), bf16[16,2,128,128]{3,2,1,0:T(8,128)(2,1)S(1)}, u32[]{:S(2)}, u32[]{:S(2)}) async-start(bf16[16,2,128,128]{3,2,1,0:T(8,128)(2,1)} %tile.19), calls=%async_computation | async-start | bytes 2097152 | tf_op jit(solution)/shard_map/all_to_all | solution.py:88
  26.7 30.0 %copy-start.23 = (bf16[1,2,128,128]{3,2,1,0:T(8,128)(2,1)S(1)}, bf16[1,2,128,128]{3,2,1,0:T(8,128)(2,1)}, u32[]{:S(2)}) copy-start(bf16[1,2,128,128]{3,2,1,0:T(8,128)(2,1)} %param.9) | copy-start | bytes 196612
  26.8 30.1 %copy-start.8 = (bf16[9,128,128]{2,1,0:T(8,128)(2,1)}, bf16[9,128,128]{2,1,0:T(8,128)(2,1)S(1)}, u32[]{:S(2)}) copy-start(bf16[9,128,128]{2,1,0:T(8,128)(2,1)S(1)} %convert_element_type.172) | copy-start | bytes 884740
  59.1 6.7 %copy-start.12 = (f32[9,128,128]{2,1,0:T(8,128)S(1)}, f32[9,128,128]{2,1,0:T(8,128)}, u32[]{:S(2)}) copy-start(f32[9,128,128]{2,1,0:T(8,128)} %param.13) | copy-start | bytes 1769476
  59.1 33.4 %all-to-all-start.1 = ((bf16[16,2,128,256]{3,2,1,0:T(8,128)(2,1)}), bf16[16,2,128,256]{3,2,1,0:T(8,128)(2,1)}, u32[]{:S(2)}, u32[]{:S(2)}) async-start(bf16[16,2,128,256]{3,2,1,0:T(8,128)(2,1)} %copy.108), calls=%async_computation.1 | async-start | bytes 4194304 | tf_op jit(solution)/shard_map/all_to_all | solution.py:88
  65.9 38.4 %copy-start.10 = (bf16[9,128,128]{2,1,0:T(8,128)(2,1)}, bf16[9,128,128]{2,1,0:T(8,128)(2,1)S(1)}, u32[]{:S(2)}) copy-start(bf16[9,128,128]{2,1,0:T(8,128)(2,1)S(1)} %convert_element_type.176) | copy-start | bytes 884740
  95.4 15.0 %collective-permute-start.1 = (bf16[1,2,128,128]{3,2,1,0:T(8,128)(2,1)S(1)}, bf16[1,2,128,128]{3,2,1,0:T(8,128)(2,1)S(1)}, u32[]{:S(2)}, u32[]{:S(2)}) collective-permute-start(bf16[1,2,128,128]{3,2,1,0:T(8,128)(2,1)S(1)} %multiply_convert_fusion), channel_id=1, source_target_pairs={{0,0},{1,16},{2,32},{3,48},{4,64},{5,80},{6,96},{7,112},{8,128},{9... | collective-permute-start | bytes 196616 | tf_op jit(solution)/shard_map/ppermute | solution.py:84
  165.1 5.5 %copy-start.11 = (bf16[9,128,128]{2,1,0:T(8,128)(2,1)S(1)}, bf16[9,128,128]{2,1,0:T(8,128)(2,1)}, u32[]{:S(2)}) copy-start(bf16[9,128,128]{2,1,0:T(8,128)(2,1)} %copy-done.10) | copy-start | bytes 884740
  165.2 18.2 %collective-permute-start.2 = (f32[1,2,128,128]{3,2,1,0:T(8,128)S(1)}, f32[1,2,128,128]{3,2,1,0:T(8,128)S(1)}, u32[]{:S(2)}, u32[]{:S(2)}) collective-permute-start(f32[1,2,128,128]{3,2,1,0:T(8,128)S(1)} %bitcast.150), channel_id=1, source_target_pairs={{0,0},{1,16},{2,32},{3,48},{4,64},{5,80},{6,96},{7,112},{8,128},{9... | collective-permute-start | bytes 393224 | tf_op jit(solution)/shard_map/ppermute | solution.py:84
  188.1 32.3 %all-to-all-start.3 = ((bf16[16,2,128,256]{3,2,1,0:T(8,128)(2,1)}), bf16[16,2,128,256]{3,2,1,0:T(8,128)(2,1)}, u32[]{:S(2)}, u32[]{:S(2)}) async-start(bf16[16,2,128,256]{3,2,1,0:T(8,128)(2,1)} %copy.112), calls=%async_computation.3 | async-start | bytes 4194304 | tf_op jit(solution)/shard_map/all_to_all | solution.py:88
  199.1 22.6 %copy-start.9 = (bf16[9,128,128]{2,1,0:T(8,128)(2,1)S(1)}, bf16[9,128,128]{2,1,0:T(8,128)(2,1)}, u32[]{:S(2)}) copy-start(bf16[9,128,128]{2,1,0:T(8,128)(2,1)} %copy-done.8) | copy-start | bytes 884740
  224.3 7.3 %copy-start.7 = (bf16[16,2,128,128]{3,0,2,1:T(8,128)(2,1)S(1)}, bf16[16,2,128,128]{3,0,2,1:T(8,128)(2,1)}, u32[]{:S(2)}) copy-start(bf16[16,2,128,128]{3,0,2,1:T(8,128)(2,1)} %copy.160) | copy-start | bytes 3145732
  225.6 32.2 %all-to-all-start.4 = ((bf16[16,2,128,128]{3,2,1,0:T(8,128)(2,1)}), bf16[16,2,128,128]{3,2,1,0:T(8,128)(2,1)}, u32[]{:S(2)}, u32[]{:S(2)}) async-start(bf16[16,2,128,128]{3,2,1,0:T(8,128)(2,1)} %copy.114), calls=%async_computation.4 | async-start | bytes 2097152 | tf_op jit(solution)/shard_map/all_to_all | solution.py:88
  231.6 1.7 copy-start.16
  242.6 1.3 copy-start.6
  242.6 2.4 copy-start.5
  243.9 1.6 copy-start.4
  245.0 1.3 copy-start.3
  246.8 2.4 copy-start.2
  247.4 2.3 copy-start.1
  249.2 1.2 copy-start
  249.7 1.2 copy-start.18
  249.7 1.2 copy-start.30
  249.7 1.3 copy-start.31
  249.7 1.3 copy-start.29
  249.7 1.3 copy-start.28
  249.8 1.3 copy-start.27
  249.8 1.3 copy-start.26
  249.8 1.4 copy-start.25
  250.3 1.2 copy-start.17
  250.4 2.8 %copy-start.22 = (f32[9,128,128]{2,1,0:T(8,128)S(1)}, f32[9,128,128]{2,1,0:T(8,128)}, u32[]{:S(2)}) copy-start(f32[9,128,128]{2,1,0:T(8,128)} %param.11) | copy-start | bytes 1769476
  250.9 2.3 copy-start.13
  250.9 2.3 copy-start.15
  250.9 2.3 copy-start.19
  251.0 2.3 copy-start.20
  251.0 2.3 copy-start.21
  253.3 10.9 %copy-start.32 = (bf16[1,2,128,128]{3,2,1,0:T(8,128)(2,1)S(1)}, bf16[1,2,128,128]{3,2,1,0:T(8,128)(2,1)}, u32[]{:S(2)}) copy-start(bf16[1,2,128,128]{3,2,1,0:T(8,128)(2,1)} %param.8) | copy-start | bytes 196612
  253.3 23.8 %copy-start.24 = (bf16[1,2,128,128]{3,2,1,0:T(8,128)(2,1)S(1)}, bf16[1,2,128,128]{3,2,1,0:T(8,128)(2,1)}, u32[]{:S(2)}) copy-start(bf16[1,2,128,128]{3,2,1,0:T(8,128)(2,1)} %param.9) | copy-start | bytes 196612
  259.2 17.9 %collective-permute-start.3 = (f32[1,2,128,128]{3,2,1,0:T(8,128)S(1)}, f32[1,2,128,128]{3,2,1,0:T(8,128)S(1)}, u32[]{:S(2)}, u32[]{:S(2)}) collective-permute-start(f32[1,2,128,128]{3,2,1,0:T(8,128)S(1)} %bitcast.151), channel_id=1, source_target_pairs={{0,0},{1,16},{2,32},{3,48},{4,64},{5,80},{6,96},{7,112},{8,128},{9... | collective-permute-start | bytes 393224 | tf_op jit(solution)/shard_map/ppermute | solution.py:84

commit v6 on v5

--- a/solution.py
+++ b/solution.py
@@ -124,14 +124,15 @@
     _, pullback = jax.vjp(group_silu, pre_first)
     pre_grad = pullback(hidden_grad)[0].astype(jnp.bfloat16)
     partial_second = conv_forward(whole_hidden, weight_second).astype(jnp.bfloat16)
-    joined = exchange(jnp.concatenate([partial_second, tiled(pre_grad, "sample")], axis=3), "sample")
+    payload = jnp.concatenate([partial_second, tiled(pre_grad, "sample")], axis=3)
+    joined = exchange(payload, "sample")
     pre_second = summed(joined[..., :width])
     whole_pre_grad = joined[..., width:]
     level_out = (activations.astype(jnp.float32) + pre_second).astype(jnp.bfloat16)
     terms_first = adjoint_block(whole_pre_grad, weight_first).astype(jnp.bfloat16)
     data_grad = transpose_mesh(summed(exchange(terms_first, "filter")))
     input_grad = (cotangent.astype(jnp.float32) + data_grad).astype(jnp.bfloat16)
-    deferred_hidden, deferred_cotangent, _ = lax.optimization_barrier((whole_hidden, whole_cotangent, joined))
+    deferred_hidden, deferred_cotangent, _ = lax.optimization_barrier((whole_hidden, whole_cotangent, payload))
     grad_second = tap_grad_sum(deferred_hidden, deferred_cotangent)
     grad_first = tap_grad_sum(whole_input, whole_pre_grad)
     new_master_first, new_moment_first, new_second_first = adam_update(

time: 280 us -> 283 us (1.011)
  blocking collectives: 53.6 us -> 0 us
  waiting for transfers between devices: 111 us -> 163 us
  starting transfers between devices: 50.4 us -> 56.6 us
  matrix products: 27.1 us -> 22.1 us
    all_to_all x1 -> x0, blocking collectives: 53.6 us -> none  [exchange(): return lax.all_to_all(payload, axis, 0, 0, tiled=True)]
    all_to_all x4 -> x5, waiting for transfers between devices: 75.7 us -> 128 us  [exchange(): return lax.all_to_all(payload, axis, 0, 0, tiled=True)]
    all_to_all x4 -> x5, starting transfers between devices: 27.3 us -> 34.2 us  [exchange(): return lax.all_to_all(payload, axis, 0, 0, tiled=True)]
    dot_general x18, matrix products: 15.6 us -> 10.5 us  [tap_grad_sum(): lax.dot_general(shifted, flat_up, (((1,), (1,)), ((0,), (0,))), preferred...]
  transfers between devices with their start and end apart: 8 -> 9, of which waited for: 8 -> 9; matrix products, arithmetic and copies ran while one was open for 14% -> 12% of each run, Pallas kernels for 0% -> 0%
where the time goes in v6:
time: 283 us; the launch traced here: 281 us
  waiting for transfers between devices  163 us (58%)
  starting transfers between devices  56.6 us (20%)
  local copies, waits for them, and re-layouts  24.3 us (9%)
  matrix products  22.1 us (8%)
  other arithmetic  13.9 us (5%)
    all_to_all x5, waiting for transfers between devices, exchange(): return lax.all_to_all(payload, axis, 0, 0, tiled=True)  128 us
    ppermute x4, waiting for transfers between devices, transpose_mesh(): return lax.ppermute(block, ('sample', 'filter'), pairs)  35.3 us
    all_to_all x5, starting transfers between devices, exchange(): return lax.all_to_all(payload, axis, 0, 0, tiled=True)  34.2 us
    ppermute x4, starting transfers between devices, transpose_mesh(): return lax.ppermute(block, ('sample', 'filter'), pairs)  22.4 us
    dot_general x18, matrix products, tap_grad_sum(): lax.dot_general(shifted, flat_up, (((1,), (1,)), ((0,), (0,))), preferred...  10.5 us
    conv_general_dilated x2, matrix products, conv_forward(): lax.conv_general_dilated(source, taps, (1, 1), ((1, 1), (1, 1)), dimensio...  6.28 us
  transfers between devices with their start and end apart: 9, of which 9 were waited for; matrix products, arithmetic and copies ran while one was open for 12% of the time, Pallas kernels for 0%

profile of v6, /device:TPU:6, one launch (start us, length us, event | category | flops | bytes accessed | tf_op | source)
XLA Modules:
  0.0 281.3 jit_solution(6528471507472552506)
XLA Ops:
  0.6 7.9 %collective-permute-start = (bf16[1,2,128,128]{3,2,1,0:T(8,128)(2,1)}, bf16[1,2,128,128]{3,2,1,0:T(8,128)(2,1)S(1)}, u32[]{:S(2)}, u32[]{:S(2)}) collective-permute-start(bf16[1,2,128,128]{3,2,1,0:T(8,128)(2,1)} %param.8), channel_id=1, source_target_pairs={{0,0},{1,16},{2,32},{3,48},{4,64},{5,80},{6,96},{7,112},{8,128},{9... | collective-permute-start | bytes 196616 | tf_op jit(solution)/shard_map/ppermute | solution.py:84
  8.5 8.0 %collective-permute-done = bf16[1,2,128,128]{3,2,1,0:T(8,128)(2,1)S(1)} collective-permute-done((bf16[1,2,128,128]{3,2,1,0:T(8,128)(2,1)}, bf16[1,2,128,128]{3,2,1,0:T(8,128)(2,1)S(1)}, u32[]{:S(2)}, u32[]{:S(2)}) %collective-permute-start) | collective-permute-done | bytes 65568 | tf_op jit(solution)/shard_map/ppermute | solution.py:84
  16.5 1.2 tile.19
  17.7 9.0 %all-to-all-start = ((bf16[16,2,128,128]{3,2,1,0:T(8,128)(2,1)}), bf16[16,2,128,128]{3,2,1,0:T(8,128)(2,1)S(1)}, u32[]{:S(2)}, u32[]{:S(2)}) async-start(bf16[16,2,128,128]{3,2,1,0:T(8,128)(2,1)} %tile.19), calls=%async_computation | async-start | bytes 2097152 | tf_op jit(solution)/shard_map/all_to_all | solution.py:88
  26.8 27.3 %all-to-all-done = bf16[16,2,128,128]{3,2,1,0:T(8,128)(2,1)S(1)} async-done(((bf16[16,2,128,128]{3,2,1,0:T(8,128)(2,1)}), bf16[16,2,128,128]{3,2,1,0:T(8,128)(2,1)S(1)}, u32[]{:S(2)}, u32[]{:S(2)}) %all-to-all-start) | async-done | bytes 1048608 | tf_op jit(solution)/shard_map/all_to_all | solution.py:88
  54.1 2.6 convolution_convert_fusion.3
  57.1 2.1 copy.108
  59.2 6.6 %all-to-all-start.1 = ((bf16[16,2,128,256]{3,2,1,0:T(8,128)(2,1)}), bf16[16,2,128,256]{3,2,1,0:T(8,128)(2,1)S(1)}, u32[]{:S(2)}, u32[]{:S(2)}) async-start(bf16[16,2,128,256]{3,2,1,0:T(8,128)(2,1)} %copy.108), calls=%async_computation.1 | async-start | bytes 4194304 | tf_op jit(solution)/shard_map/all_to_all | solution.py:88
  65.8 1.8 convert_element_type.176
  67.6 24.8 %all-to-all-done.1 = bf16[16,2,128,256]{3,2,1,0:T(8,128)(2,1)S(1)} async-done(((bf16[16,2,128,256]{3,2,1,0:T(8,128)(2,1)}), bf16[16,2,128,256]{3,2,1,0:T(8,128)(2,1)S(1)}, u32[]{:S(2)}, u32[]{:S(2)}) %all-to-all-start.1) | async-done | bytes 2097184 | tf_op jit(solution)/shard_map/all_to_all | solution.py:88
  92.4 0.7 convert_reduce_fusion
  94.0 5.2 %collective-permute-start.1 = (bf16[1,2,128,128]{3,2,1,0:T(8,128)(2,1)S(1)}, bf16[1,2,128,128]{3,2,1,0:T(8,128)(2,1)S(1)}, u32[]{:S(2)}, u32[]{:S(2)}) collective-permute-start(bf16[1,2,128,128]{3,2,1,0:T(8,128)(2,1)S(1)} %multiply_convert_fusion), channel_id=1, source_target_pairs={{0,0},{1,16},{2,32},{3,48},{4,64},{5,80},{6,96},{7,112},{8,128},{9... | collective-permute-start | bytes 196616 | tf_op jit(solution)/shard_map/ppermute | solution.py:84
  99.2 1.3 slice.91
  100.5 2.6 convolution_convert_fusion.1
  103.1 6.0 %collective-permute-done.1 = bf16[1,2,128,128]{3,2,1,0:T(8,128)(2,1)S(1)} collective-permute-done((bf16[1,2,128,128]{3,2,1,0:T(8,128)(2,1)S(1)}, bf16[1,2,128,128]{3,2,1,0:T(8,128)(2,1)S(1)}, u32[]{:S(2)}, u32[]{:S(2)}) %collective-permute-start.1) | collective-permute-done | bytes 65568 | tf_op jit(solution)/shard_map/ppermute | solution.py:84
  109.5 2.0 copy.110
  111.5 5.6 %all-to-all-start.2 = ((bf16[16,2,128,256]{3,2,1,0:T(8,128)(2,1)}), bf16[16,2,128,256]{3,2,1,0:T(8,128)(2,1)}, u32[]{:S(2)}, u32[]{:S(2)}) async-start(bf16[16,2,128,256]{3,2,1,0:T(8,128)(2,1)} %copy.110), calls=%async_computation.2 | async-start | bytes 4194304 | tf_op jit(solution)/shard_map/all_to_all | solution.py:88
  117.1 3.5 %pad_slice_fusion = (bf16[16,2,128,128]{3,2,1,0:T(8,128)(2,1)}, bf16[16,2,128,128]{3,2,1,0:T(8,128)(2,1)}, bf16[16,2,128,128]{3,2,1,0:T(8,128)(2,1)}, bf16[16,2,...) fusion(bf16[16,2,128,128]{3,2,1,0:T(8,128)(2,1)S(1)} %all-to-al, ...), kind=kLoop, calls=%fused_computation | loop fusion | bytes 9437184 | tf_op jit(solution)/shard_map/slice | solution.py:22
  120.6 1.6 copy.159
  122.2 42.9 %all-to-all-done.2 = bf16[16,2,128,256]{3,2,1,0:T(8,128)(2,1)} async-done(((bf16[16,2,128,256]{3,2,1,0:T(8,128)(2,1)}), bf16[16,2,128,256]{3,2,1,0:T(8,128)(2,1)}, u32[]{:S(2)}, u32[]{:S(2)}) %all-to-all-start.2) | async-done | bytes 2097184 | tf_op jit(solution)/shard_map/all_to_all | solution.py:88
  165.1 1.4 convert_reduce_fusion.4
  166.5 4.3 %collective-permute-start.2 = (f32[1,2,128,128]{3,2,1,0:T(8,128)S(1)}, f32[1,2,128,128]{3,2,1,0:T(8,128)S(1)}, u32[]{:S(2)}, u32[]{:S(2)}) collective-permute-start(f32[1,2,128,128]{3,2,1,0:T(8,128)S(1)} %bitcast.150), channel_id=1, source_target_pairs={{0,0},{1,16},{2,32},{3,48},{4,64},{5,80},{6,96},{7,112},{8,128},{9... | collective-permute-start | bytes 393224 | tf_op jit(solution)/shard_map/ppermute | solution.py:84
  170.8 1.3 slice.92
  172.1 3.6 %convolution_convert_fusion.2 = bf16[16,2,128,128]{3,0,2,1:T(8,128)(2,1)} fusion(bf16[3,3,128,128]{3,2,1,0:T(8,128)(2,1)S(1)} %bitcast.131, bf16[16,2,128,128]{3,2,1,0:T(8,128)(2,1)S(1)} %slice.92), kind=kOutput, calls=%fused_computation.26 | convolution fusion | flops 801636352 | bytes 2392064 | tf_op jit(solution)/shard_map/conv_general_dilated | solution.py:27
  175.8 0.7 copy.160
  176.5 9.2 %collective-permute-done.2 = f32[1,2,128,128]{3,2,1,0:T(8,128)S(1)} collective-permute-done((f32[1,2,128,128]{3,2,1,0:T(8,128)S(1)}, f32[1,2,128,128]{3,2,1,0:T(8,128)S(1)}, u32[]{:S(2)}, u32[]{:S(2)}) %collective-permute-start.2) | collective-permute-done | bytes 131104 | tf_op jit(solution)/shard_map/ppermute | solution.py:84
  186.8 1.5 pad_maximum_fusion.2
  188.3 2.0 copy.112
  190.3 4.8 %all-to-all-start.3 = ((bf16[16,2,128,256]{3,2,1,0:T(8,128)(2,1)}), bf16[16,2,128,256]{3,2,1,0:T(8,128)(2,1)}, u32[]{:S(2)}, u32[]{:S(2)}) async-start(bf16[16,2,128,256]{3,2,1,0:T(8,128)(2,1)} %copy.112), calls=%async_computation.3 | async-start | bytes 4194304 | tf_op jit(solution)/shard_map/all_to_all | solution.py:88
  195.2 1.4 pad_slice_fusion.8
  196.6 0.6 fusion.31
  197.2 0.6 fusion.28
  197.8 0.6 fusion.29
  198.5 0.6 fusion.30
  199.1 0.6 fusion.32
  199.7 0.6 fusion.27
  200.4 0.6 fusion.33
  201.0 0.6 fusion.34
  201.7 0.6 fusion.35
  203.1 1.4 multiply_subtract_fusion
  204.5 17.3 %all-to-all-done.3 = bf16[16,2,128,256]{3,2,1,0:T(8,128)(2,1)} async-done(((bf16[16,2,128,256]{3,2,1,0:T(8,128)(2,1)}), bf16[16,2,128,256]{3,2,1,0:T(8,128)(2,1)}, u32[]{:S(2)}, u32[]{:S(2)}) %all-to-all-start.3) | async-done | bytes 2097184 | tf_op jit(solution)/shard_map/all_to_all | solution.py:88
  221.9 1.3 slice.95
  223.2 2.6 convolution_convert_fusion
  225.8 1.3 copy.114
  227.1 8.1 %all-to-all-start.4 = ((bf16[16,2,128,128]{3,2,1,0:T(8,128)(2,1)}), bf16[16,2,128,128]{3,2,1,0:T(8,128)(2,1)}, u32[]{:S(2)}, u32[]{:S(2)}) async-start(bf16[16,2,128,128]{3,2,1,0:T(8,128)(2,1)} %copy.114), calls=%async_computation.4 | async-start | bytes 2097152 | tf_op jit(solution)/shard_map/all_to_all | solution.py:88
  235.2 0.5 fusion.22
  235.7 0.7 copy-done.7
  236.4 0.5 fusion.26
  236.9 0.5 fusion.19
  237.7 1.1 fusion.20
  238.9 0.5 fusion.21
  239.4 0.5 fusion.23
  240.1 0.5 fusion.24
  240.7 0.5 fusion.25
  241.2 0.5 fusion.18
  241.7 1.5 convert_reduce_fusion.3
  243.3 0.9 bitcast_dynamic-update-slice_fusion.15
  244.3 1.4 multiply_subtract_fusion.1
  245.7 15.7 %all-to-all-done.4 = bf16[16,2,128,128]{3,2,1,0:T(8,128)(2,1)} async-done(((bf16[16,2,128,128]{3,2,1,0:T(8,128)(2,1)}), bf16[16,2,128,128]{3,2,1,0:T(8,128)(2,1)}, u32[]{:S(2)}, u32[]{:S(2)}) %all-to-all-start.4) | async-done | bytes 1048608 | tf_op jit(solution)/shard_map/all_to_all | solution.py:88
  261.4 1.4 convert_reduce_fusion.2
  262.8 5.1 %collective-permute-start.3 = (f32[1,2,128,128]{3,2,1,0:T(8,128)S(1)}, f32[1,2,128,128]{3,2,1,0:T(8,128)S(1)}, u32[]{:S(2)}, u32[]{:S(2)}) collective-permute-start(f32[1,2,128,128]{3,2,1,0:T(8,128)S(1)} %bitcast.151), channel_id=1, source_target_pairs={{0,0},{1,16},{2,32},{3,48},{4,64},{5,80},{6,96},{7,112},{8,128},{9... | collective-permute-start | bytes 393224 | tf_op jit(solution)/shard_map/ppermute | solution.py:84
  267.9 0.6 fusion.56
  268.5 12.2 %collective-permute-done.3 = f32[1,2,128,128]{3,2,1,0:T(8,128)S(1)} collective-permute-done((f32[1,2,128,128]{3,2,1,0:T(8,128)S(1)}, f32[1,2,128,128]{3,2,1,0:T(8,128)S(1)}, u32[]{:S(2)}, u32[]{:S(2)}) %collective-permute-start.3) | collective-permute-done | bytes 131104 | tf_op jit(solution)/shard_map/ppermute | solution.py:84
  280.7 0.6 add_convert_fusion
  (94 shorter events, 4.4 us)
Async XLA Ops:
  0.6 26.1 %copy-start.13 = (f32[9,128,128]{2,1,0:T(8,128)S(1)}, f32[9,128,128]{2,1,0:T(8,128)}, u32[]{:S(2)}) copy-start(f32[9,128,128]{2,1,0:T(8,128)} %param.10) | copy-start | bytes 1769476
  0.6 15.8 %collective-permute-start = (bf16[1,2,128,128]{3,2,1,0:T(8,128)(2,1)}, bf16[1,2,128,128]{3,2,1,0:T(8,128)(2,1)S(1)}, u32[]{:S(2)}, u32[]{:S(2)}) collective-permute-start(bf16[1,2,128,128]{3,2,1,0:T(8,128)(2,1)} %param.8), channel_id=1, source_target_pairs={{0,0},{1,16},{2,32},{3,48},{4,64},{5,80},{6,96},{7,112},{8,128},{9... | collective-permute-start | bytes 196616 | tf_op jit(solution)/shard_map/ppermute | solution.py:84
  17.7 36.4 %all-to-all-start = ((bf16[16,2,128,128]{3,2,1,0:T(8,128)(2,1)}), bf16[16,2,128,128]{3,2,1,0:T(8,128)(2,1)S(1)}, u32[]{:S(2)}, u32[]{:S(2)}) async-start(bf16[16,2,128,128]{3,2,1,0:T(8,128)(2,1)} %tile.19), calls=%async_computation | async-start | bytes 2097152 | tf_op jit(solution)/shard_map/all_to_all | solution.py:88
  26.7 30.0 %copy-start.20 = (bf16[1,2,128,128]{3,2,1,0:T(8,128)(2,1)S(1)}, bf16[1,2,128,128]{3,2,1,0:T(8,128)(2,1)}, u32[]{:S(2)}) copy-start(bf16[1,2,128,128]{3,2,1,0:T(8,128)(2,1)} %param.9) | copy-start | bytes 196612
  26.8 30.1 %copy-start.8 = (bf16[9,128,128]{2,1,0:T(8,128)(2,1)}, bf16[9,128,128]{2,1,0:T(8,128)(2,1)S(1)}, u32[]{:S(2)}) copy-start(bf16[9,128,128]{2,1,0:T(8,128)(2,1)S(1)} %convert_element_type.172) | copy-start | bytes 884740
  59.2 33.2 %all-to-all-start.1 = ((bf16[16,2,128,256]{3,2,1,0:T(8,128)(2,1)}), bf16[16,2,128,256]{3,2,1,0:T(8,128)(2,1)S(1)}, u32[]{:S(2)}, u32[]{:S(2)}) async-start(bf16[16,2,128,256]{3,2,1,0:T(8,128)(2,1)} %copy.108), calls=%async_computation.1 | async-start | bytes 4194304 | tf_op jit(solution)/shard_map/all_to_all | solution.py:88
  92.4 1.6 copy-start
  93.9 6.6 %copy-start.10 = (bf16[9,128,128]{2,1,0:T(8,128)(2,1)S(1)}, bf16[9,128,128]{2,1,0:T(8,128)(2,1)}, u32[]{:S(2)}) copy-start(bf16[9,128,128]{2,1,0:T(8,128)(2,1)} %convert_element_type.176) | copy-start | bytes 884740
  94.0 15.1 %collective-permute-start.1 = (bf16[1,2,128,128]{3,2,1,0:T(8,128)(2,1)S(1)}, bf16[1,2,128,128]{3,2,1,0:T(8,128)(2,1)S(1)}, u32[]{:S(2)}, u32[]{:S(2)}) collective-permute-start(bf16[1,2,128,128]{3,2,1,0:T(8,128)(2,1)S(1)} %multiply_convert_fusion), channel_id=1, source_target_pairs={{0,0},{1,16},{2,32},{3,48},{4,64},{5,80},{6,96},{7,112},{8,128},{9... | collective-permute-start | bytes 196616 | tf_op jit(solution)/shard_map/ppermute | solution.py:84
  111.5 53.6 %all-to-all-start.2 = ((bf16[16,2,128,256]{3,2,1,0:T(8,128)(2,1)}), bf16[16,2,128,256]{3,2,1,0:T(8,128)(2,1)}, u32[]{:S(2)}, u32[]{:S(2)}) async-start(bf16[16,2,128,256]{3,2,1,0:T(8,128)(2,1)} %copy.110), calls=%async_computation.2 | async-start | bytes 4194304 | tf_op jit(solution)/shard_map/all_to_all | solution.py:88
  122.2 49.9 %copy-start.11 = (bf16[9,128,128]{2,1,0:T(8,128)(2,1)S(1)}, bf16[9,128,128]{2,1,0:T(8,128)(2,1)}, u32[]{:S(2)}) copy-start(bf16[9,128,128]{2,1,0:T(8,128)(2,1)} %convert_element_type.176) | copy-start | bytes 884740
  166.5 19.2 %collective-permute-start.2 = (f32[1,2,128,128]{3,2,1,0:T(8,128)S(1)}, f32[1,2,128,128]{3,2,1,0:T(8,128)S(1)}, u32[]{:S(2)}, u32[]{:S(2)}) collective-permute-start(f32[1,2,128,128]{3,2,1,0:T(8,128)S(1)} %bitcast.150), channel_id=1, source_target_pairs={{0,0},{1,16},{2,32},{3,48},{4,64},{5,80},{6,96},{7,112},{8,128},{9... | collective-permute-start | bytes 393224 | tf_op jit(solution)/shard_map/ppermute | solution.py:84
  190.3 31.5 %all-to-all-start.3 = ((bf16[16,2,128,256]{3,2,1,0:T(8,128)(2,1)}), bf16[16,2,128,256]{3,2,1,0:T(8,128)(2,1)}, u32[]{:S(2)}, u32[]{:S(2)}) async-start(bf16[16,2,128,256]{3,2,1,0:T(8,128)(2,1)} %copy.112), calls=%async_computation.3 | async-start | bytes 4194304 | tf_op jit(solution)/shard_map/all_to_all | solution.py:88
  195.1 1.5 copy-start.15
  201.6 1.1 copy-start.12
  201.7 1.2 copy-start.16
  201.7 1.4 copy-start.17
  203.1 20.1 %copy-start.9 = (bf16[9,128,128]{2,1,0:T(8,128)(2,1)S(1)}, bf16[9,128,128]{2,1,0:T(8,128)(2,1)}, u32[]{:S(2)}) copy-start(bf16[9,128,128]{2,1,0:T(8,128)(2,1)} %copy-done.8) | copy-start | bytes 884740
  227.1 34.3 %all-to-all-start.4 = ((bf16[16,2,128,128]{3,2,1,0:T(8,128)(2,1)}), bf16[16,2,128,128]{3,2,1,0:T(8,128)(2,1)}, u32[]{:S(2)}, u32[]{:S(2)}) async-start(bf16[16,2,128,128]{3,2,1,0:T(8,128)(2,1)} %copy.114), calls=%async_computation.4 | async-start | bytes 2097152 | tf_op jit(solution)/shard_map/all_to_all | solution.py:88
  235.2 1.2 copy-start.7
  235.2 1.7 copy-start.6
  236.4 1.3 copy-start.5
  236.9 1.9 copy-start.4
  237.7 1.6 copy-start.3
  238.9 1.3 copy-start.2
  239.4 1.3 copy-start.1
  241.2 3.1 %copy-start.14 = (f32[9,128,128]{2,1,0:T(8,128)S(1)}, f32[9,128,128]{2,1,0:T(8,128)}, u32[]{:S(2)}) copy-start(f32[9,128,128]{2,1,0:T(8,128)} %param.10) | copy-start | bytes 1769476
  241.7 2.6 copy-start.18
  241.7 2.6 copy-start.19
  244.2 23.6 %copy-start.22 = (bf16[1,2,128,128]{3,2,1,0:T(8,128)(2,1)S(1)}, bf16[1,2,128,128]{3,2,1,0:T(8,128)(2,1)}, u32[]{:S(2)}) copy-start(bf16[1,2,128,128]{3,2,1,0:T(8,128)(2,1)} %param.8) | copy-start | bytes 196612
  244.3 36.4 %copy-start.21 = (bf16[1,2,128,128]{3,2,1,0:T(8,128)(2,1)S(1)}, bf16[1,2,128,128]{3,2,1,0:T(8,128)(2,1)}, u32[]{:S(2)}) copy-start(bf16[1,2,128,128]{3,2,1,0:T(8,128)(2,1)} %param.9) | copy-start | bytes 196612
  262.8 17.9 %collective-permute-start.3 = (f32[1,2,128,128]{3,2,1,0:T(8,128)S(1)}, f32[1,2,128,128]{3,2,1,0:T(8,128)S(1)}, u32[]{:S(2)}, u32[]{:S(2)}) collective-permute-start(f32[1,2,128,128]{3,2,1,0:T(8,128)S(1)} %bitcast.151), channel_id=1, source_target_pairs={{0,0},{1,16},{2,32},{3,48},{4,64},{5,80},{6,96},{7,112},{8,128},{9... | collective-permute-start | bytes 393224 | tf_op jit(solution)/shard_map/ppermute | solution.py:84

commit v7 on v5

--- a/solution.py
+++ b/solution.py
@@ -1,6 +1,7 @@
 import jax
 import jax.numpy as jnp
 from jax import lax
+from jax.experimental.layout import Layout, with_layout_constraint
 from jax.sharding import PartitionSpec as P
 
 GROUP = 64
@@ -88,6 +89,10 @@
     return lax.all_to_all(payload, axis, 0, 0, tiled=True)
 
 
+def sample_major(field):
+    return with_layout_constraint(field, Layout(major_to_minor=(0, 1, 2, 3)))
+
+
 def tiled(block, axis):
     return jnp.tile(block, (lax.axis_size(axis), 1, 1, 1))
 
@@ -110,12 +115,12 @@
     weight_second = master_second.astype(jnp.bfloat16)
     width = activations.shape[3]
     whole_input = exchange(tiled(transpose_mesh(activations), "filter"), "filter")
-    partial_first = conv_forward(whole_input, weight_first).astype(jnp.bfloat16)
+    partial_first = sample_major(conv_forward(whole_input, weight_first).astype(jnp.bfloat16))
     joined = exchange(jnp.concatenate([tiled(cotangent, "sample"), partial_first], axis=3), "sample")
     whole_cotangent = joined[..., :width]
     pre_first = summed(joined[..., width:])
     hidden = group_silu(pre_first).astype(jnp.bfloat16)
-    terms_second = adjoint_block(whole_cotangent, weight_second).astype(jnp.bfloat16)
+    terms_second = sample_major(adjoint_block(whole_cotangent, weight_second).astype(jnp.bfloat16))
     joined = exchange(
         jnp.concatenate([tiled(transpose_mesh(hidden), "filter"), terms_second], axis=3), "filter"
     )
@@ -123,12 +128,12 @@
     hidden_grad = transpose_mesh(summed(joined[..., width:]))
     _, pullback = jax.vjp(group_silu, pre_first)
     pre_grad = pullback(hidden_grad)[0].astype(jnp.bfloat16)
-    partial_second = conv_forward(whole_hidden, weight_second).astype(jnp.bfloat16)
+    partial_second = sample_major(conv_forward(whole_hidden, weight_second).astype(jnp.bfloat16))
     joined = exchange(jnp.concatenate([partial_second, tiled(pre_grad, "sample")], axis=3), "sample")
     pre_second = summed(joined[..., :width])
     whole_pre_grad = joined[..., width:]
     level_out = (activations.astype(jnp.float32) + pre_second).astype(jnp.bfloat16)
-    terms_first = adjoint_block(whole_pre_grad, weight_first).astype(jnp.bfloat16)
+    terms_first = sample_major(adjoint_block(whole_pre_grad, weight_first).astype(jnp.bfloat16))
     data_grad = transpose_mesh(summed(exchange(terms_first, "filter")))
     input_grad = (cotangent.astype(jnp.float32) + data_grad).astype(jnp.bfloat16)
     deferred_hidden, deferred_cotangent, _ = lax.optimization_barrier((whole_hidden, whole_cotangent, joined))

time: 280 us -> 277 us (0.989)
    concatenate x3 -> x0, local copies, waits for them, and re-layouts: 4.71 us -> none  [the longest x1 2 us: per_device(): jnp.concatenate([tiled(cotangent, 'sample'), partial_first], axis=3)]
    optimization_barrier x2 -> x0, local copies, waits for them, and re-layouts: 3.38 us -> none  [per_device(): lax.optimization_barrier((whole_hidden, whole_cotangent, joined))]
  transfers between devices with their start and end apart: 8 -> 8, of which waited for: 8 -> 7; matrix products, arithmetic and copies ran while one was open for 14% -> 14% of each run, Pallas kernels for 0% -> 0%
where the time goes in v7:
time: 277 us; the launch traced here: 276 us
  waiting for transfers between devices  112 us (40%)
  blocking collectives  53.6 us (19%)
  starting transfers between devices  51.6 us (19%)
  matrix products  24.4 us (9%)
  local copies, waits for them, and re-layouts  19.6 us (7%)
  other arithmetic  13.7 us (5%)
    all_to_all x4, waiting for transfers between devices, exchange(): return lax.all_to_all(payload, axis, 0, 0, tiled=True)  75.1 us
    all_to_all x1, blocking collectives, exchange(): return lax.all_to_all(payload, axis, 0, 0, tiled=True)  53.6 us
    ppermute x4, waiting for transfers between devices, transpose_mesh(): return lax.ppermute(block, ('sample', 'filter'), pairs)  36.5 us
    all_to_all x4, starting transfers between devices, exchange(): return lax.all_to_all(payload, axis, 0, 0, tiled=True)  27.2 us
    ppermute x4, starting transfers between devices, transpose_mesh(): return lax.ppermute(block, ('sample', 'filter'), pairs)  24.4 us
    dot_general x18, matrix products, tap_grad_sum(): lax.dot_general(shifted, flat_up, (((1,), (1,)), ((0,), (0,))), preferred...  13.8 us
    slice x2, local copies, waits for them, and re-layouts, window(): padded[:, row_start:row_start + height, column_start:column_start + bread...  8.16 us
  transfers between devices with their start and end apart: 8, of which 7 were waited for; matrix products, arithmetic and copies ran while one was open for 14% of the time, Pallas kernels for 0%

profile of v7, /device:TPU:6, one launch (start us, length us, event | category | flops | bytes accessed | tf_op | source)
XLA Modules:
  0.0 275.9 jit_solution(11021266606160794314)
XLA Ops:
  0.6 7.9 %collective-permute-start = (bf16[1,2,128,128]{3,2,1,0:T(8,128)(2,1)}, bf16[1,2,128,128]{3,2,1,0:T(8,128)(2,1)S(1)}, u32[]{:S(2)}, u32[]{:S(2)}) collective-permute-start(bf16[1,2,128,128]{3,2,1,0:T(8,128)(2,1)} %param.8), channel_id=1, source_target_pairs={{0,0},{1,16},{2,32},{3,48},{4,64},{5,80},{6,96},{7,112},{8,128},{9... | collective-permute-start | bytes 196616 | tf_op jit(solution)/shard_map/ppermute | solution.py:85
  8.5 8.0 %collective-permute-done = bf16[1,2,128,128]{3,2,1,0:T(8,128)(2,1)S(1)} collective-permute-done((bf16[1,2,128,128]{3,2,1,0:T(8,128)(2,1)}, bf16[1,2,128,128]{3,2,1,0:T(8,128)(2,1)S(1)}, u32[]{:S(2)}, u32[]{:S(2)}) %collective-permute-start) | collective-permute-done | bytes 65568 | tf_op jit(solution)/shard_map/ppermute | solution.py:85
  16.5 1.2 tile.19
  17.7 9.0 %all-to-all-start = ((bf16[16,2,128,128]{3,2,1,0:T(8,128)(2,1)}), bf16[16,2,128,128]{3,2,1,0:T(8,128)(2,1)S(1)}, u32[]{:S(2)}, u32[]{:S(2)}) async-start(bf16[16,2,128,128]{3,2,1,0:T(8,128)(2,1)} %tile.19), calls=%async_computation | async-start | bytes 2097152 | tf_op jit(solution)/shard_map/all_to_all | solution.py:89
  26.8 27.3 %all-to-all-done = bf16[16,2,128,128]{3,2,1,0:T(8,128)(2,1)S(1)} async-done(((bf16[16,2,128,128]{3,2,1,0:T(8,128)(2,1)}), bf16[16,2,128,128]{3,2,1,0:T(8,128)(2,1)S(1)}, u32[]{:S(2)}, u32[]{:S(2)}) %all-to-all-start) | async-done | bytes 1048608 | tf_op jit(solution)/shard_map/all_to_all | solution.py:89
  54.1 2.6 fusion.42
  56.7 0.3 copy.140
  57.0 0.2 tile.17
  57.2 1.6 pad_maximum_fusion
  58.9 6.6 %all-to-all-start.1 = ((bf16[16,2,128,256]{3,2,1,0:T(8,128)(2,1)}), bf16[16,2,128,256]{3,2,1,0:T(8,128)(2,1)S(1)}, u32[]{:S(2)}, u32[]{:S(2)}) async-start(bf16[16,2,128,256]{3,2,1,0:T(8,128)(2,1)} %pad_maximum_fusion), calls=%async_computation.1 | async-start | bytes 4194304 | tf_op jit(solution)/shard_map/all_to_all | solution.py:89
  65.5 1.8 convert_element_type.176
  67.3 24.8 %all-to-all-done.1 = bf16[16,2,128,256]{3,2,1,0:T(8,128)(2,1)S(1)} async-done(((bf16[16,2,128,256]{3,2,1,0:T(8,128)(2,1)}), bf16[16,2,128,256]{3,2,1,0:T(8,128)(2,1)S(1)}, u32[]{:S(2)}, u32[]{:S(2)}) %all-to-all-start.1) | async-done | bytes 2097184 | tf_op jit(solution)/shard_map/all_to_all | solution.py:89
  92.1 0.7 convert_reduce_fusion
  93.7 5.2 %collective-permute-start.1 = (bf16[1,2,128,128]{3,2,1,0:T(8,128)(2,1)S(1)}, bf16[1,2,128,128]{3,2,1,0:T(8,128)(2,1)S(1)}, u32[]{:S(2)}, u32[]{:S(2)}) collective-permute-start(bf16[1,2,128,128]{3,2,1,0:T(8,128)(2,1)S(1)} %multiply_convert_fusion), channel_id=1, source_target_pairs={{0,0},{1,16},{2,32},{3,48},{4,64},{5,80},{6,96},{7,112},{8,128},{9... | collective-permute-start | bytes 196616 | tf_op jit(solution)/shard_map/ppermute | solution.py:85
  98.9 1.3 slice.91
  100.2 2.6 fusion.40
  102.8 0.3 copy.139
  103.1 5.7 %collective-permute-done.1 = bf16[1,2,128,128]{3,2,1,0:T(8,128)(2,1)S(1)} collective-permute-done((bf16[1,2,128,128]{3,2,1,0:T(8,128)(2,1)S(1)}, bf16[1,2,128,128]{3,2,1,0:T(8,128)(2,1)S(1)}, u32[]{:S(2)}, u32[]{:S(2)}) %collective-permute-start.1) | collective-permute-done | bytes 65568 | tf_op jit(solution)/shard_map/ppermute | solution.py:85
  109.0 0.3 pad_maximum_fusion.1
  109.3 53.6 %all_to_all.25 = bf16[16,2,128,256]{3,2,1,0:T(8,128)(2,1)S(1)} all-to-all(bf16[16,2,128,256]{3,2,1,0:T(8,128)(2,1)S(1)} %pad_maximum_fusion.1), channel_id=1, replica_groups=mesh['sample'=16,'filter'=16] {'filter'}, dimensions={0} | all-to-all | bytes 4194304 | tf_op jit(solution)/shard_map/all_to_all | solution.py:89
  163.1 5.2 %collective-permute-start.2 = (f32[1,2,128,128]{3,2,1,0:T(8,128)S(1)}, f32[1,2,128,128]{3,2,1,0:T(8,128)S(1)}, u32[]{:S(2)}, u32[]{:S(2)}) collective-permute-start(f32[1,2,128,128]{3,2,1,0:T(8,128)S(1)} %bitcast.166), channel_id=1, source_target_pairs={{0,0},{1,16},{2,32},{3,48},{4,64},{5,80},{6,96},{7,112},{8,128},{9... | collective-permute-start | bytes 393224 | tf_op jit(solution)/shard_map/ppermute | solution.py:85
  168.5 2.7 fusion.38
  171.1 0.3 copy.138
  171.4 9.9 %collective-permute-done.2 = f32[1,2,128,128]{3,2,1,0:T(8,128)S(1)} collective-permute-done((f32[1,2,128,128]{3,2,1,0:T(8,128)S(1)}, f32[1,2,128,128]{3,2,1,0:T(8,128)S(1)}, u32[]{:S(2)}, u32[]{:S(2)}) %collective-permute-start.2) | collective-permute-done | bytes 131104 | tf_op jit(solution)/shard_map/ppermute | solution.py:85
  182.3 0.2 tile.43
  182.5 1.5 pad_maximum_fusion.2
  184.0 5.6 %all-to-all-start.3 = ((bf16[16,2,128,256]{3,2,1,0:T(8,128)(2,1)}), bf16[16,2,128,256]{3,2,1,0:T(8,128)(2,1)}, u32[]{:S(2)}, u32[]{:S(2)}) async-start(bf16[16,2,128,256]{3,2,1,0:T(8,128)(2,1)} %pad_maximum_fusion.2), calls=%async_computation.3 | async-start | bytes 4194304 | tf_op jit(solution)/shard_map/all_to_all | solution.py:89
  189.6 3.7 %pad_slice_fusion.8 = (bf16[16,2,128,128]{3,2,1,0:T(8,128)(2,1)}, bf16[16,2,128,128]{3,2,1,0:T(8,128)(2,1)}, bf16[16,2,128,128]{3,2,1,0:T(8,128)(2,1)}, bf16[16,...) fusion(bf16[16,2,128,128]{3,2,1,0:T(8,128)(2,1)S(1)} %all-to-al, ...), kind=kLoop, calls=%fused_computation.8 | loop fusion | bytes 9437184 | tf_op jit(solution)/shard_map/slice | solution.py:23
  193.3 23.0 %all-to-all-done.3 = bf16[16,2,128,256]{3,2,1,0:T(8,128)(2,1)} async-done(((bf16[16,2,128,256]{3,2,1,0:T(8,128)(2,1)}), bf16[16,2,128,256]{3,2,1,0:T(8,128)(2,1)}, u32[]{:S(2)}, u32[]{:S(2)}) %all-to-all-start.3) | async-done | bytes 2097184 | tf_op jit(solution)/shard_map/all_to_all | solution.py:89
  216.3 1.3 slice.95
  217.7 2.6 fusion.36
  220.3 1.3 copy.137
  221.5 6.0 %all-to-all-start.4 = ((bf16[16,2,128,128]{3,2,1,0:T(8,128)(2,1)}), bf16[16,2,128,128]{3,2,1,0:T(8,128)(2,1)}, u32[]{:S(2)}, u32[]{:S(2)}) async-start(bf16[16,2,128,128]{3,2,1,0:T(8,128)(2,1)} %copy.137), calls=%async_computation.4 | async-start | bytes 2097152 | tf_op jit(solution)/shard_map/all_to_all | solution.py:89
  227.6 4.5 %pad_slice_fusion = (bf16[16,2,128,128]{3,2,1,0:T(8,128)(2,1)S(1)}, bf16[16,2,128,128]{3,2,1,0:T(8,128)(2,1)S(1)}, bf16[16,2,128,128]{3,2,1,0:T(8,128)(2,1)S(1)}...) fusion(bf16[16,2,128,128]{3,2,1,0:T(8,128)(2,1)} %copy-done), kind=kLoop, calls=%fused_computation | loop fusion | bytes 9437184 | tf_op jit(solution)/shard_map/slice | solution.py:23
  232.1 0.5 fusion.27
  232.6 0.6 bitcast_dynamic-update-slice_fusion.9
  233.2 1.1 fusion.28
  234.3 1.1 fusion.29
  235.4 1.1 fusion.30
  236.5 0.5 fusion.31
  237.0 0.5 fusion.32
  237.5 0.5 fusion.33
  238.0 0.5 fusion.34
  238.5 0.5 fusion.35
  239.0 0.2 copy-done.9
  239.2 0.5 fusion.18
  239.7 0.6 bitcast_dynamic-update-slice_fusion.17
  240.4 1.1 fusion.19
  241.5 1.1 fusion.20
  242.6 0.5 fusion.21
  243.1 1.1 fusion.22
  244.2 1.6 copy.93
  245.8 1.8 fusion.23
  247.6 0.5 fusion.24
  248.2 0.5 fusion.25
  248.9 0.5 fusion.26
  249.6 0.3 copy-done.16
  249.9 1.6 convert_reduce_fusion.3
  251.7 2.3 multiply_subtract_fusion
  254.0 1.4 convert_reduce_fusion.2
  255.4 6.2 %collective-permute-start.3 = (f32[1,2,128,128]{3,2,1,0:T(8,128)S(1)}, f32[1,2,128,128]{3,2,1,0:T(8,128)S(1)}, u32[]{:S(2)}, u32[]{:S(2)}) collective-permute-start(f32[1,2,128,128]{3,2,1,0:T(8,128)S(1)} %bitcast.167), channel_id=1, source_target_pairs={{0,0},{1,16},{2,32},{3,48},{4,64},{5,80},{6,96},{7,112},{8,128},{9... | collective-permute-start | bytes 393224 | tf_op jit(solution)/shard_map/ppermute | solution.py:85
  261.6 0.6 fusion.53
  262.3 13.0 %collective-permute-done.3 = f32[1,2,128,128]{3,2,1,0:T(8,128)S(1)} collective-permute-done((f32[1,2,128,128]{3,2,1,0:T(8,128)S(1)}, f32[1,2,128,128]{3,2,1,0:T(8,128)S(1)}, u32[]{:S(2)}, u32[]{:S(2)}) %collective-permute-start.3) | collective-permute-done | bytes 131104 | tf_op jit(solution)/shard_map/ppermute | solution.py:85
  275.2 0.6 add_convert_fusion
  (106 shorter events, 2.8 us)
Async XLA Ops:
  0.6 26.1 %copy-start.14 = (f32[9,128,128]{2,1,0:T(8,128)S(1)}, f32[9,128,128]{2,1,0:T(8,128)}, u32[]{:S(2)}) copy-start(f32[9,128,128]{2,1,0:T(8,128)} %param.10) | copy-start | bytes 1769476
  0.6 15.8 %collective-permute-start = (bf16[1,2,128,128]{3,2,1,0:T(8,128)(2,1)}, bf16[1,2,128,128]{3,2,1,0:T(8,128)(2,1)S(1)}, u32[]{:S(2)}, u32[]{:S(2)}) collective-permute-start(bf16[1,2,128,128]{3,2,1,0:T(8,128)(2,1)} %param.8), channel_id=1, source_target_pairs={{0,0},{1,16},{2,32},{3,48},{4,64},{5,80},{6,96},{7,112},{8,128},{9... | collective-permute-start | bytes 196616 | tf_op jit(solution)/shard_map/ppermute | solution.py:85
  17.7 36.4 %all-to-all-start = ((bf16[16,2,128,128]{3,2,1,0:T(8,128)(2,1)}), bf16[16,2,128,128]{3,2,1,0:T(8,128)(2,1)S(1)}, u32[]{:S(2)}, u32[]{:S(2)}) async-start(bf16[16,2,128,128]{3,2,1,0:T(8,128)(2,1)} %tile.19), calls=%async_computation | async-start | bytes 2097152 | tf_op jit(solution)/shard_map/all_to_all | solution.py:89
  26.7 30.2 %copy-start.10 = (bf16[9,128,128]{2,1,0:T(8,128)(2,1)}, bf16[9,128,128]{2,1,0:T(8,128)(2,1)S(1)}, u32[]{:S(2)}) copy-start(bf16[9,128,128]{2,1,0:T(8,128)(2,1)S(1)} %convert_element_type.172) | copy-start | bytes 884740
  54.1 2.9 %copy-start.27 = (bf16[1,2,128,128]{3,2,1,0:T(8,128)(2,1)S(1)}, bf16[1,2,128,128]{3,2,1,0:T(8,128)(2,1)}, u32[]{:S(2)}) copy-start(bf16[1,2,128,128]{3,2,1,0:T(8,128)(2,1)} %param.9) | copy-start | bytes 196612
  58.9 33.2 %all-to-all-start.1 = ((bf16[16,2,128,256]{3,2,1,0:T(8,128)(2,1)}), bf16[16,2,128,256]{3,2,1,0:T(8,128)(2,1)S(1)}, u32[]{:S(2)}, u32[]{:S(2)}) async-start(bf16[16,2,128,256]{3,2,1,0:T(8,128)(2,1)} %pad_maximum_fusion), calls=%async_computation.1 | async-start | bytes 4194304 | tf_op jit(solution)/shard_map/all_to_all | solution.py:89
  92.1 1.6 copy-start.2
  93.6 6.5 %copy-start.12 = (bf16[9,128,128]{2,1,0:T(8,128)(2,1)S(1)}, bf16[9,128,128]{2,1,0:T(8,128)(2,1)}, u32[]{:S(2)}) copy-start(bf16[9,128,128]{2,1,0:T(8,128)(2,1)} %convert_element_type.176) | copy-start | bytes 884740
  93.7 15.1 %collective-permute-start.1 = (bf16[1,2,128,128]{3,2,1,0:T(8,128)(2,1)S(1)}, bf16[1,2,128,128]{3,2,1,0:T(8,128)(2,1)S(1)}, u32[]{:S(2)}, u32[]{:S(2)}) collective-permute-start(bf16[1,2,128,128]{3,2,1,0:T(8,128)(2,1)S(1)} %multiply_convert_fusion), channel_id=1, source_target_pairs={{0,0},{1,16},{2,32},{3,48},{4,64},{5,80},{6,96},{7,112},{8,128},{9... | collective-permute-start | bytes 196616 | tf_op jit(solution)/shard_map/ppermute | solution.py:85
  163.1 18.2 %collective-permute-start.2 = (f32[1,2,128,128]{3,2,1,0:T(8,128)S(1)}, f32[1,2,128,128]{3,2,1,0:T(8,128)S(1)}, u32[]{:S(2)}, u32[]{:S(2)}) collective-permute-start(f32[1,2,128,128]{3,2,1,0:T(8,128)S(1)} %bitcast.166), channel_id=1, source_target_pairs={{0,0},{1,16},{2,32},{3,48},{4,64},{5,80},{6,96},{7,112},{8,128},{9... | collective-permute-start | bytes 393224 | tf_op jit(solution)/shard_map/ppermute | solution.py:85
  168.5 3.0 %copy-start = (bf16[16,2,128,128]{3,2,1,0:T(8,128)(2,1)}, bf16[16,2,128,128]{3,2,1,0:T(8,128)(2,1)S(1)}, u32[]{:S(2)}) copy-start(bf16[16,2,128,128]{3,2,1,0:T(8,128)(2,1)S(1)} %slice.92) | copy-start | bytes 3145732
  184.0 32.3 %all-to-all-start.3 = ((bf16[16,2,128,256]{3,2,1,0:T(8,128)(2,1)}), bf16[16,2,128,256]{3,2,1,0:T(8,128)(2,1)}, u32[]{:S(2)}, u32[]{:S(2)}) async-start(bf16[16,2,128,256]{3,2,1,0:T(8,128)(2,1)} %pad_maximum_fusion.2), calls=%async_computation.3 | async-start | bytes 4194304 | tf_op jit(solution)/shard_map/all_to_all | solution.py:89
  193.3 24.3 %copy-start.11 = (bf16[9,128,128]{2,1,0:T(8,128)(2,1)S(1)}, bf16[9,128,128]{2,1,0:T(8,128)(2,1)}, u32[]{:S(2)}) copy-start(bf16[9,128,128]{2,1,0:T(8,128)(2,1)} %copy-done.10) | copy-start | bytes 884740
  221.5 32.5 %all-to-all-start.4 = ((bf16[16,2,128,128]{3,2,1,0:T(8,128)(2,1)}), bf16[16,2,128,128]{3,2,1,0:T(8,128)(2,1)}, u32[]{:S(2)}, u32[]{:S(2)}) async-start(bf16[16,2,128,128]{3,2,1,0:T(8,128)(2,1)} %copy.137), calls=%async_computation.4 | async-start | bytes 2097152 | tf_op jit(solution)/shard_map/all_to_all | solution.py:89
  234.3 2.2 copy-start.1
  238.0 1.2 copy-start.9
  238.5 1.9 copy-start.8
  239.2 2.3 copy-start.7
  240.4 2.2 copy-start.6
  243.1 4.5 %copy-start.5 = (bf16[16,2,128,128]{3,2,1,0:T(8,128)(2,1)S(1)}, bf16[16,2,128,128]{3,2,1,0:T(8,128)(2,1)}, u32[]{:S(2)}) copy-start(bf16[16,2,128,128]{3,2,1,0:T(8,128)(2,1)} %get-tuple-element.43) | copy-start | bytes 3145732
  245.8 2.3 copy-start.4
  247.6 1.2 copy-start.3
  248.1 1.2 copy-start.17
  248.1 1.2 copy-start.25
  248.2 1.3 copy-start.26
  248.2 1.3 copy-start.24
  248.7 1.2 copy-start.16
  248.7 1.2 copy-start.22
  248.7 1.2 copy-start.23
  248.9 2.7 copy-start.29
  248.9 2.8 %copy-start.21 = (f32[9,128,128]{2,1,0:T(8,128)S(1)}, f32[9,128,128]{2,1,0:T(8,128)}, u32[]{:S(2)}) copy-start(f32[9,128,128]{2,1,0:T(8,128)} %param.11) | copy-start | bytes 1769476
  249.4 2.3 copy-start.13
  249.4 2.3 copy-start.15
  249.4 2.3 copy-start.18
  249.4 2.3 copy-start.19
  249.4 2.3 copy-start.20
  251.7 9.9 %copy-start.30 = (bf16[1,2,128,128]{3,2,1,0:T(8,128)(2,1)S(1)}, bf16[1,2,128,128]{3,2,1,0:T(8,128)(2,1)}, u32[]{:S(2)}) copy-start(bf16[1,2,128,128]{3,2,1,0:T(8,128)(2,1)} %param.8) | copy-start | bytes 196612
  251.7 23.5 %copy-start.28 = (bf16[1,2,128,128]{3,2,1,0:T(8,128)(2,1)S(1)}, bf16[1,2,128,128]{3,2,1,0:T(8,128)(2,1)}, u32[]{:S(2)}) copy-start(bf16[1,2,128,128]{3,2,1,0:T(8,128)(2,1)} %param.9) | copy-start | bytes 196612
  255.4 19.8 %collective-permute-start.3 = (f32[1,2,128,128]{3,2,1,0:T(8,128)S(1)}, f32[1,2,128,128]{3,2,1,0:T(8,128)S(1)}, u32[]{:S(2)}, u32[]{:S(2)}) collective-permute-start(f32[1,2,128,128]{3,2,1,0:T(8,128)S(1)} %bitcast.167), channel_id=1, source_target_pairs={{0,0},{1,16},{2,32},{3,48},{4,64},{5,80},{6,96},{7,112},{8,128},{9... | collective-permute-start | bytes 393224 | tf_op jit(solution)/shard_map/ppermute | solution.py:85

commit v8 on v7

--- a/solution.py
+++ b/solution.py
@@ -129,14 +129,15 @@
     _, pullback = jax.vjp(group_silu, pre_first)
     pre_grad = pullback(hidden_grad)[0].astype(jnp.bfloat16)
     partial_second = sample_major(conv_forward(whole_hidden, weight_second).astype(jnp.bfloat16))
-    joined = exchange(jnp.concatenate([partial_second, tiled(pre_grad, "sample")], axis=3), "sample")
+    payload = jnp.concatenate([partial_second, tiled(pre_grad, "sample")], axis=3)
+    joined = exchange(payload, "sample")
     pre_second = summed(joined[..., :width])
     whole_pre_grad = joined[..., width:]
     level_out = (activations.astype(jnp.float32) + pre_second).astype(jnp.bfloat16)
     terms_first = sample_major(adjoint_block(whole_pre_grad, weight_first).astype(jnp.bfloat16))
     data_grad = transpose_mesh(summed(exchange(terms_first, "filter")))
     input_grad = (cotangent.astype(jnp.float32) + data_grad).astype(jnp.bfloat16)
-    deferred_hidden, deferred_cotangent, _ = lax.optimization_barrier((whole_hidden, whole_cotangent, joined))
+    deferred_hidden, deferred_cotangent, _ = lax.optimization_barrier((whole_hidden, whole_cotangent, payload))
     grad_second = tap_grad_sum(deferred_hidden, deferred_cotangent)
     grad_first = tap_grad_sum(whole_input, whole_pre_grad)
     new_master_first, new_moment_first, new_second_first = adam_update(

time: 277 us -> 282 us (1.018)
  blocking collectives: 53.6 us -> 0 us
  waiting for transfers between devices: 112 us -> 163 us
  starting transfers between devices: 51.6 us -> 56.7 us
  other arithmetic: 13.7 us -> 17.9 us
  matrix products: 24.4 us -> 21.1 us
    all_to_all x1 -> x0, blocking collectives: 53.6 us -> none  [exchange(): return lax.all_to_all(payload, axis, 0, 0, tiled=True)]
    all_to_all x4 -> x5, waiting for transfers between devices: 75.1 us -> 127 us  [exchange(): return lax.all_to_all(payload, axis, 0, 0, tiled=True)]
    all_to_all x4 -> x5, starting transfers between devices: 27.2 us -> 34.3 us  [exchange(): return lax.all_to_all(payload, axis, 0, 0, tiled=True)]
    dot_general x18, matrix products: 13.8 us -> 10.6 us  [tap_grad_sum(): lax.dot_general(shifted, flat_up, (((1,), (1,)), ((0,), (0,))), preferred...]
  transfers between devices with their start and end apart: 8 -> 9, of which waited for: 7 -> 9; matrix products, arithmetic and copies ran while one was open for 14% -> 13% of each run, Pallas kernels for 0% -> 0%
where the time goes in v8:
time: 282 us; the launch traced here: 280 us
  waiting for transfers between devices  163 us (58%)
  starting transfers between devices  56.7 us (20%)
  matrix products  21.1 us (7%)
  local copies, waits for them, and re-layouts  20.1 us (7%)
  other arithmetic  17.9 us (6%)
    all_to_all x5, waiting for transfers between devices, exchange(): return lax.all_to_all(payload, axis, 0, 0, tiled=True)  127 us
    ppermute x4, waiting for transfers between devices, transpose_mesh(): return lax.ppermute(block, ('sample', 'filter'), pairs)  35.4 us
    all_to_all x5, starting transfers between devices, exchange(): return lax.all_to_all(payload, axis, 0, 0, tiled=True)  34.3 us
    ppermute x4, starting transfers between devices, transpose_mesh(): return lax.ppermute(block, ('sample', 'filter'), pairs)  22.4 us
    dot_general x18, matrix products, tap_grad_sum(): lax.dot_general(shifted, flat_up, (((1,), (1,)), ((0,), (0,))), preferred...  10.6 us
    slice x2, local copies, waits for them, and re-layouts, window(): padded[:, row_start:row_start + height, column_start:column_start + bread...  6.15 us
  transfers between devices with their start and end apart: 9, of which 9 were waited for; matrix products, arithmetic and copies ran while one was open for 13% of the time, Pallas kernels for 0%

profile of v8, /device:TPU:6, one launch (start us, length us, event | category | flops | bytes accessed | tf_op | source)
XLA Modules:
  0.0 279.8 jit_solution(17923581932438090764)
XLA Ops:
  0.6 7.9 %collective-permute-start = (bf16[1,2,128,128]{3,2,1,0:T(8,128)(2,1)}, bf16[1,2,128,128]{3,2,1,0:T(8,128)(2,1)S(1)}, u32[]{:S(2)}, u32[]{:S(2)}) collective-permute-start(bf16[1,2,128,128]{3,2,1,0:T(8,128)(2,1)} %param.8), channel_id=1, source_target_pairs={{0,0},{1,16},{2,32},{3,48},{4,64},{5,80},{6,96},{7,112},{8,128},{9... | collective-permute-start | bytes 196616 | tf_op jit(solution)/shard_map/ppermute | solution.py:85
  8.5 8.0 %collective-permute-done = bf16[1,2,128,128]{3,2,1,0:T(8,128)(2,1)S(1)} collective-permute-done((bf16[1,2,128,128]{3,2,1,0:T(8,128)(2,1)}, bf16[1,2,128,128]{3,2,1,0:T(8,128)(2,1)S(1)}, u32[]{:S(2)}, u32[]{:S(2)}) %collective-permute-start) | collective-permute-done | bytes 65568 | tf_op jit(solution)/shard_map/ppermute | solution.py:85
  16.5 1.2 tile.19
  17.7 9.0 %all-to-all-start = ((bf16[16,2,128,128]{3,2,1,0:T(8,128)(2,1)}), bf16[16,2,128,128]{3,2,1,0:T(8,128)(2,1)S(1)}, u32[]{:S(2)}, u32[]{:S(2)}) async-start(bf16[16,2,128,128]{3,2,1,0:T(8,128)(2,1)} %tile.19), calls=%async_computation | async-start | bytes 2097152 | tf_op jit(solution)/shard_map/all_to_all | solution.py:89
  26.8 27.3 %all-to-all-done = bf16[16,2,128,128]{3,2,1,0:T(8,128)(2,1)S(1)} async-done(((bf16[16,2,128,128]{3,2,1,0:T(8,128)(2,1)}), bf16[16,2,128,128]{3,2,1,0:T(8,128)(2,1)S(1)}, u32[]{:S(2)}, u32[]{:S(2)}) %all-to-all-start) | async-done | bytes 1048608 | tf_op jit(solution)/shard_map/all_to_all | solution.py:89
  54.1 2.6 fusion.42
  57.2 1.6 pad_maximum_fusion
  58.9 6.6 %all-to-all-start.1 = ((bf16[16,2,128,256]{3,2,1,0:T(8,128)(2,1)}), bf16[16,2,128,256]{3,2,1,0:T(8,128)(2,1)S(1)}, u32[]{:S(2)}, u32[]{:S(2)}) async-start(bf16[16,2,128,256]{3,2,1,0:T(8,128)(2,1)} %pad_maximum_fusion), calls=%async_computation.1 | async-start | bytes 4194304 | tf_op jit(solution)/shard_map/all_to_all | solution.py:89
  65.5 1.8 convert_element_type.176
  67.3 24.8 %all-to-all-done.1 = bf16[16,2,128,256]{3,2,1,0:T(8,128)(2,1)S(1)} async-done(((bf16[16,2,128,256]{3,2,1,0:T(8,128)(2,1)}), bf16[16,2,128,256]{3,2,1,0:T(8,128)(2,1)S(1)}, u32[]{:S(2)}, u32[]{:S(2)}) %all-to-all-start.1) | async-done | bytes 2097184 | tf_op jit(solution)/shard_map/all_to_all | solution.py:89
  92.1 0.7 convert_reduce_fusion
  93.7 5.2 %collective-permute-start.1 = (bf16[1,2,128,128]{3,2,1,0:T(8,128)(2,1)S(1)}, bf16[1,2,128,128]{3,2,1,0:T(8,128)(2,1)S(1)}, u32[]{:S(2)}, u32[]{:S(2)}) collective-permute-start(bf16[1,2,128,128]{3,2,1,0:T(8,128)(2,1)S(1)} %multiply_convert_fusion), channel_id=1, source_target_pairs={{0,0},{1,16},{2,32},{3,48},{4,64},{5,80},{6,96},{7,112},{8,128},{9... | collective-permute-start | bytes 196616 | tf_op jit(solution)/shard_map/ppermute | solution.py:85
  98.9 1.3 slice.91
  100.2 2.6 fusion.40
  103.1 5.7 %collective-permute-done.1 = bf16[1,2,128,128]{3,2,1,0:T(8,128)(2,1)S(1)} collective-permute-done((bf16[1,2,128,128]{3,2,1,0:T(8,128)(2,1)S(1)}, bf16[1,2,128,128]{3,2,1,0:T(8,128)(2,1)S(1)}, u32[]{:S(2)}, u32[]{:S(2)}) %collective-permute-start.1) | collective-permute-done | bytes 65568 | tf_op jit(solution)/shard_map/ppermute | solution.py:85
  109.0 1.6 pad_maximum_fusion.1
  110.6 5.6 %all-to-all-start.2 = ((bf16[16,2,128,256]{3,2,1,0:T(8,128)(2,1)}), bf16[16,2,128,256]{3,2,1,0:T(8,128)(2,1)}, u32[]{:S(2)}, u32[]{:S(2)}) async-start(bf16[16,2,128,256]{3,2,1,0:T(8,128)(2,1)} %pad_maximum_fusion.1), calls=%async_computation.2 | async-start | bytes 4194304 | tf_op jit(solution)/shard_map/all_to_all | solution.py:89
  116.2 3.7 %pad_slice_fusion.8 = (bf16[16,2,128,128]{3,2,1,0:T(8,128)(2,1)}, bf16[16,2,128,128]{3,2,1,0:T(8,128)(2,1)}, bf16[16,2,128,128]{3,2,1,0:T(8,128)(2,1)}, bf16[16,...) fusion(bf16[16,2,128,128]{3,2,1,0:T(8,128)(2,1)S(1)} %all-to-al, ...), kind=kLoop, calls=%fused_computation.8 | loop fusion | bytes 9437184 | tf_op jit(solution)/shard_map/slice | solution.py:23
  119.9 44.3 %all-to-all-done.2 = bf16[16,2,128,256]{3,2,1,0:T(8,128)(2,1)} async-done(((bf16[16,2,128,256]{3,2,1,0:T(8,128)(2,1)}), bf16[16,2,128,256]{3,2,1,0:T(8,128)(2,1)}, u32[]{:S(2)}, u32[]{:S(2)}) %all-to-all-start.2) | async-done | bytes 2097184 | tf_op jit(solution)/shard_map/all_to_all | solution.py:89
  164.2 1.4 convert_reduce_fusion.4
  165.7 4.3 %collective-permute-start.2 = (f32[1,2,128,128]{3,2,1,0:T(8,128)S(1)}, f32[1,2,128,128]{3,2,1,0:T(8,128)S(1)}, u32[]{:S(2)}, u32[]{:S(2)}) collective-permute-start(f32[1,2,128,128]{3,2,1,0:T(8,128)S(1)} %bitcast.166), channel_id=1, source_target_pairs={{0,0},{1,16},{2,32},{3,48},{4,64},{5,80},{6,96},{7,112},{8,128},{9... | collective-permute-start | bytes 393224 | tf_op jit(solution)/shard_map/ppermute | solution.py:85
  170.0 1.3 slice.92
  171.3 2.6 fusion.38
  173.9 1.3 copy.138
  175.2 9.6 %collective-permute-done.2 = f32[1,2,128,128]{3,2,1,0:T(8,128)S(1)} collective-permute-done((f32[1,2,128,128]{3,2,1,0:T(8,128)S(1)}, f32[1,2,128,128]{3,2,1,0:T(8,128)S(1)}, u32[]{:S(2)}, u32[]{:S(2)}) %collective-permute-start.2) | collective-permute-done | bytes 131104 | tf_op jit(solution)/shard_map/ppermute | solution.py:85
  186.0 2.8 pad_maximum_fusion.2
  188.8 4.8 %all-to-all-start.3 = ((bf16[16,2,128,256]{3,2,1,0:T(8,128)(2,1)}), bf16[16,2,128,256]{3,2,1,0:T(8,128)(2,1)}, u32[]{:S(2)}, u32[]{:S(2)}) async-start(bf16[16,2,128,256]{3,2,1,0:T(8,128)(2,1)} %pad_maximum_fusion.2), calls=%async_computation.3 | async-start | bytes 4194304 | tf_op jit(solution)/shard_map/all_to_all | solution.py:89
  193.6 2.4 pad_slice_fusion
  196.0 0.5 fusion.31
  196.5 0.5 fusion.35
  197.0 0.5 fusion.28
  197.5 0.5 fusion.29
  198.0 0.5 fusion.30
  198.5 0.5 fusion.32
  199.0 0.5 fusion.33
  199.5 0.5 fusion.27
  200.0 0.5 fusion.34
  200.6 0.4 copy-done.13
  201.4 1.5 multiply_subtract_fusion
  202.8 17.5 %all-to-all-done.3 = bf16[16,2,128,256]{3,2,1,0:T(8,128)(2,1)} async-done(((bf16[16,2,128,256]{3,2,1,0:T(8,128)(2,1)}), bf16[16,2,128,256]{3,2,1,0:T(8,128)(2,1)}, u32[]{:S(2)}, u32[]{:S(2)}) %all-to-all-start.3) | async-done | bytes 2097184 | tf_op jit(solution)/shard_map/all_to_all | solution.py:89
  220.3 1.3 slice.95
  221.6 2.6 fusion.36
  224.2 1.3 copy.137
  225.5 8.3 %all-to-all-start.4 = ((bf16[16,2,128,128]{3,2,1,0:T(8,128)(2,1)}), bf16[16,2,128,128]{3,2,1,0:T(8,128)(2,1)}, u32[]{:S(2)}, u32[]{:S(2)}) async-start(bf16[16,2,128,128]{3,2,1,0:T(8,128)(2,1)} %copy.137), calls=%async_computation.4 | async-start | bytes 2097152 | tf_op jit(solution)/shard_map/all_to_all | solution.py:89
  233.8 1.1 fusion.22
  234.9 0.5 fusion.26
  235.4 0.5 fusion.19
  236.1 1.1 fusion.20
  237.2 1.1 fusion.21
  238.4 0.5 fusion.23
  238.9 0.5 fusion.24
  239.6 0.5 fusion.25
  240.2 0.5 fusion.18
  240.7 1.4 convert_reduce_fusion.3
  242.1 0.9 copy.93
  243.1 0.8 bitcast_dynamic-update-slice_fusion.15
  243.9 0.8 bitcast_dynamic-update-slice_fusion.14
  244.9 1.4 multiply_subtract_fusion.1
  246.3 13.6 %all-to-all-done.4 = bf16[16,2,128,128]{3,2,1,0:T(8,128)(2,1)} async-done(((bf16[16,2,128,128]{3,2,1,0:T(8,128)(2,1)}), bf16[16,2,128,128]{3,2,1,0:T(8,128)(2,1)}, u32[]{:S(2)}, u32[]{:S(2)}) %all-to-all-start.4) | async-done | bytes 1048608 | tf_op jit(solution)/shard_map/all_to_all | solution.py:89
  259.9 1.4 convert_reduce_fusion.2
  261.3 5.1 %collective-permute-start.3 = (f32[1,2,128,128]{3,2,1,0:T(8,128)S(1)}, f32[1,2,128,128]{3,2,1,0:T(8,128)S(1)}, u32[]{:S(2)}, u32[]{:S(2)}) collective-permute-start(f32[1,2,128,128]{3,2,1,0:T(8,128)S(1)} %bitcast.167), channel_id=1, source_target_pairs={{0,0},{1,16},{2,32},{3,48},{4,64},{5,80},{6,96},{7,112},{8,128},{9... | collective-permute-start | bytes 393224 | tf_op jit(solution)/shard_map/ppermute | solution.py:85
  266.4 0.6 fusion.53
  267.1 12.1 %collective-permute-done.3 = f32[1,2,128,128]{3,2,1,0:T(8,128)S(1)} collective-permute-done((f32[1,2,128,128]{3,2,1,0:T(8,128)S(1)}, f32[1,2,128,128]{3,2,1,0:T(8,128)S(1)}, u32[]{:S(2)}, u32[]{:S(2)}) %collective-permute-start.3) | collective-permute-done | bytes 131104 | tf_op jit(solution)/shard_map/ppermute | solution.py:85
  279.2 0.6 add_convert_fusion
  (92 shorter events, 4.2 us)
Async XLA Ops:
  0.6 26.1 %copy-start.14 = (f32[9,128,128]{2,1,0:T(8,128)S(1)}, f32[9,128,128]{2,1,0:T(8,128)}, u32[]{:S(2)}) copy-start(f32[9,128,128]{2,1,0:T(8,128)} %param.10) | copy-start | bytes 1769476
  0.6 15.8 %collective-permute-start = (bf16[1,2,128,128]{3,2,1,0:T(8,128)(2,1)}, bf16[1,2,128,128]{3,2,1,0:T(8,128)(2,1)S(1)}, u32[]{:S(2)}, u32[]{:S(2)}) collective-permute-start(bf16[1,2,128,128]{3,2,1,0:T(8,128)(2,1)} %param.8), channel_id=1, source_target_pairs={{0,0},{1,16},{2,32},{3,48},{4,64},{5,80},{6,96},{7,112},{8,128},{9... | collective-permute-start | bytes 196616 | tf_op jit(solution)/shard_map/ppermute | solution.py:85
  17.7 36.4 %all-to-all-start = ((bf16[16,2,128,128]{3,2,1,0:T(8,128)(2,1)}), bf16[16,2,128,128]{3,2,1,0:T(8,128)(2,1)S(1)}, u32[]{:S(2)}, u32[]{:S(2)}) async-start(bf16[16,2,128,128]{3,2,1,0:T(8,128)(2,1)} %tile.19), calls=%async_computation | async-start | bytes 2097152 | tf_op jit(solution)/shard_map/all_to_all | solution.py:89
  26.7 30.2 %copy-start.9 = (bf16[9,128,128]{2,1,0:T(8,128)(2,1)}, bf16[9,128,128]{2,1,0:T(8,128)(2,1)S(1)}, u32[]{:S(2)}) copy-start(bf16[9,128,128]{2,1,0:T(8,128)(2,1)S(1)} %convert_element_type.172) | copy-start | bytes 884740
  54.1 2.9 %copy-start.20 = (bf16[1,2,128,128]{3,2,1,0:T(8,128)(2,1)S(1)}, bf16[1,2,128,128]{3,2,1,0:T(8,128)(2,1)}, u32[]{:S(2)}) copy-start(bf16[1,2,128,128]{3,2,1,0:T(8,128)(2,1)} %param.9) | copy-start | bytes 196612
  58.9 33.2 %all-to-all-start.1 = ((bf16[16,2,128,256]{3,2,1,0:T(8,128)(2,1)}), bf16[16,2,128,256]{3,2,1,0:T(8,128)(2,1)S(1)}, u32[]{:S(2)}, u32[]{:S(2)}) async-start(bf16[16,2,128,256]{3,2,1,0:T(8,128)(2,1)} %pad_maximum_fusion), calls=%async_computation.1 | async-start | bytes 4194304 | tf_op jit(solution)/shard_map/all_to_all | solution.py:89
  92.1 1.6 copy-start
  93.6 6.5 %copy-start.11 = (bf16[9,128,128]{2,1,0:T(8,128)(2,1)S(1)}, bf16[9,128,128]{2,1,0:T(8,128)(2,1)}, u32[]{:S(2)}) copy-start(bf16[9,128,128]{2,1,0:T(8,128)(2,1)} %convert_element_type.176) | copy-start | bytes 884740
  93.7 15.1 %collective-permute-start.1 = (bf16[1,2,128,128]{3,2,1,0:T(8,128)(2,1)S(1)}, bf16[1,2,128,128]{3,2,1,0:T(8,128)(2,1)S(1)}, u32[]{:S(2)}, u32[]{:S(2)}) collective-permute-start(bf16[1,2,128,128]{3,2,1,0:T(8,128)(2,1)S(1)} %multiply_convert_fusion), channel_id=1, source_target_pairs={{0,0},{1,16},{2,32},{3,48},{4,64},{5,80},{6,96},{7,112},{8,128},{9... | collective-permute-start | bytes 196616 | tf_op jit(solution)/shard_map/ppermute | solution.py:85
  110.6 53.6 %all-to-all-start.2 = ((bf16[16,2,128,256]{3,2,1,0:T(8,128)(2,1)}), bf16[16,2,128,256]{3,2,1,0:T(8,128)(2,1)}, u32[]{:S(2)}, u32[]{:S(2)}) async-start(bf16[16,2,128,256]{3,2,1,0:T(8,128)(2,1)} %pad_maximum_fusion.1), calls=%async_computation.2 | async-start | bytes 4194304 | tf_op jit(solution)/shard_map/all_to_all | solution.py:89
  164.2 7.0 %copy-start.12 = (bf16[9,128,128]{2,1,0:T(8,128)(2,1)S(1)}, bf16[9,128,128]{2,1,0:T(8,128)(2,1)}, u32[]{:S(2)}) copy-start(bf16[9,128,128]{2,1,0:T(8,128)(2,1)} %convert_element_type.176) | copy-start | bytes 884740
  165.7 19.1 %collective-permute-start.2 = (f32[1,2,128,128]{3,2,1,0:T(8,128)S(1)}, f32[1,2,128,128]{3,2,1,0:T(8,128)S(1)}, u32[]{:S(2)}, u32[]{:S(2)}) collective-permute-start(f32[1,2,128,128]{3,2,1,0:T(8,128)S(1)} %bitcast.166), channel_id=1, source_target_pairs={{0,0},{1,16},{2,32},{3,48},{4,64},{5,80},{6,96},{7,112},{8,128},{9... | collective-permute-start | bytes 393224 | tf_op jit(solution)/shard_map/ppermute | solution.py:85
  188.8 31.5 %all-to-all-start.3 = ((bf16[16,2,128,256]{3,2,1,0:T(8,128)(2,1)}), bf16[16,2,128,256]{3,2,1,0:T(8,128)(2,1)}, u32[]{:S(2)}, u32[]{:S(2)}) async-start(bf16[16,2,128,256]{3,2,1,0:T(8,128)(2,1)} %pad_maximum_fusion.2), calls=%async_computation.3 | async-start | bytes 4194304 | tf_op jit(solution)/shard_map/all_to_all | solution.py:89
  200.0 1.1 copy-start.13
  200.0 1.2 copy-start.16
  200.0 1.4 copy-start.17
  201.4 20.2 %copy-start.10 = (bf16[9,128,128]{2,1,0:T(8,128)(2,1)S(1)}, bf16[9,128,128]{2,1,0:T(8,128)(2,1)}, u32[]{:S(2)}) copy-start(bf16[9,128,128]{2,1,0:T(8,128)(2,1)} %copy-done.9) | copy-start | bytes 884740
  225.5 9.4 %copy-start.8 = (bf16[16,2,128,128]{3,2,1,0:T(8,128)(2,1)S(1)}, bf16[16,2,128,128]{3,2,1,0:T(8,128)(2,1)}, u32[]{:S(2)}) copy-start(bf16[16,2,128,128]{3,2,1,0:T(8,128)(2,1)} %get-tuple-element.38) | copy-start | bytes 3145732
  225.5 34.4 %all-to-all-start.4 = ((bf16[16,2,128,128]{3,2,1,0:T(8,128)(2,1)}), bf16[16,2,128,128]{3,2,1,0:T(8,128)(2,1)}, u32[]{:S(2)}, u32[]{:S(2)}) async-start(bf16[16,2,128,128]{3,2,1,0:T(8,128)(2,1)} %copy.137), calls=%async_computation.4 | async-start | bytes 2097152 | tf_op jit(solution)/shard_map/all_to_all | solution.py:89
  233.7 1.6 copy-start.7
  234.9 1.3 copy-start.6
  235.4 1.9 copy-start.5
  236.1 2.2 copy-start.4
  237.2 1.6 copy-start.3
  238.4 1.3 copy-start.2
  238.9 1.3 copy-start.1
  240.2 4.7 %copy-start.15 = (f32[9,128,128]{2,1,0:T(8,128)S(1)}, f32[9,128,128]{2,1,0:T(8,128)}, u32[]{:S(2)}) copy-start(f32[9,128,128]{2,1,0:T(8,128)} %param.10) | copy-start | bytes 1769476
  240.2 4.7 %copy-start.18 = (f32[9,128,128]{2,1,0:T(8,128)S(1)}, f32[9,128,128]{2,1,0:T(8,128)}, u32[]{:S(2)}) copy-start(f32[9,128,128]{2,1,0:T(8,128)} %param.11) | copy-start | bytes 1769476
  240.7 4.2 %copy-start.19 = (f32[9,128,128]{2,1,0:T(8,128)S(1)}, f32[9,128,128]{2,1,0:T(8,128)}, u32[]{:S(2)}) copy-start(f32[9,128,128]{2,1,0:T(8,128)} %param.12) | copy-start | bytes 1769476
  244.9 21.5 %copy-start.22 = (bf16[1,2,128,128]{3,2,1,0:T(8,128)(2,1)S(1)}, bf16[1,2,128,128]{3,2,1,0:T(8,128)(2,1)}, u32[]{:S(2)}) copy-start(bf16[1,2,128,128]{3,2,1,0:T(8,128)(2,1)} %param.8) | copy-start | bytes 196612
  244.9 34.3 %copy-start.21 = (bf16[1,2,128,128]{3,2,1,0:T(8,128)(2,1)S(1)}, bf16[1,2,128,128]{3,2,1,0:T(8,128)(2,1)}, u32[]{:S(2)}) copy-start(bf16[1,2,128,128]{3,2,1,0:T(8,128)(2,1)} %param.9) | copy-start | bytes 196612
  261.3 17.9 %collective-permute-start.3 = (f32[1,2,128,128]{3,2,1,0:T(8,128)S(1)}, f32[1,2,128,128]{3,2,1,0:T(8,128)S(1)}, u32[]{:S(2)}, u32[]{:S(2)}) collective-permute-start(f32[1,2,128,128]{3,2,1,0:T(8,128)S(1)} %bitcast.167), channel_id=1, source_target_pairs={{0,0},{1,16},{2,32},{3,48},{4,64},{5,80},{6,96},{7,112},{8,128},{9... | collective-permute-start | bytes 393224 | tf_op jit(solution)/shard_map/ppermute | solution.py:85
